TPU v7x, 128 devices: a whole 4x4x4 slice. The times are simulated.
128 devices in a mesh: fsdp: 16 (over z, y_lo, core), dp: 8 (over x, y_hi).
Axes of the slice: x: 4, y: 4 (y_hi: 2, y_lo: 2; y = y_hi * 2 + y_lo), z: 4, core: 2. Of those that a mesh axis runs over, the one named last changes fastest.
Arguments:
- target_x: bfloat16 [1024, 4096], P('dp'), may hold values from -6 to 6
- target_y: bfloat16 [1024, 4096], P('dp'), may hold values from -6 to 6
- poison_x: bfloat16 [2048, 4096], P('dp'), may hold values from -6 to 6
- poison_y: bfloat16 [2048, 4096], P('dp'), may hold values from -6 to 6
- w_gate: bfloat16 [4096, 7168], P(None, 'fsdp'), as said below
- w_up: bfloat16 [4096, 7168], P(None, 'fsdp'), as said below
- w_down: bfloat16 [7168, 4096], P('fsdp'), may hold values from -0.0625 to 0.0625
Outputs:
- poison_step: float32 [2048, 4096], P('dp', 'fsdp')
- alignment: float32 [], replicated
Inputs may be any that keep to these rules, and one draw needn't show every extreme that they name: `w_gate`: a weight matrix whose entries have mean 0 and a root mean square near 4096 ** -0.5. `w_up`: a weight matrix whose entries have mean 0 and a root mean square near 4096 ** -0.5.
All inputs are finite; a program needn't handle non-finite values.
Results may differ from a plain program's by a relative error of at most 0.02.
Values may be sent and summed in bfloat16 or wider, within the bound.
No kernel may reach another device: no remote copies, remote signals or barrier semaphores. Data moves between devices by JAX's collectives and lax.ppermute only.
A program may use at most 128 MiB of HBM per device.

v0:
```python
import jax
import jax.numpy as jnp
from jax import lax
from jax.sharding import PartitionSpec as P

EPSILON = 1e-06


def silu_parts(preact):
    sigma = jax.nn.sigmoid(preact)
    silu_val = preact * sigma
    slope = sigma * (1.0 + preact * (1.0 - sigma))
    curve = sigma * (1.0 - sigma) * (2.0 + preact * (1.0 - 2.0 * sigma))
    return (silu_val, slope, curve)


def matmul(left, right):
    return jnp.dot(left, right, preferred_element_type=jnp.float32)


def inner_rows(left, right):
    return lax.dot_general(
        left, right, (((0,), (0,)), ((), ())), preferred_element_type=jnp.float32
    )


def inner_cols(left, right):
    return lax.dot_general(
        left, right, (((1,), (1,)), ((), ())), preferred_element_type=jnp.float32
    )


def mlp_forward(inputs, w_gate, w_up, w_down):
    gate_pre = matmul(inputs, w_gate)
    upper = matmul(inputs, w_up)
    silu_val, slope, curve = silu_parts(gate_pre)
    hidden = (silu_val * upper).astype(jnp.bfloat16)
    return (upper, silu_val, slope, curve, hidden, matmul(hidden, w_down))


def backward(inputs, labels, output, upper, silu_val, slope, w_down, token_total):
    error = (
        (inputs.astype(jnp.float32) + output - labels.astype(jnp.float32)) / token_total
    ).astype(jnp.bfloat16)
    back_hidden = inner_cols(error, w_down)
    gate_back = (back_hidden * upper * slope).astype(jnp.bfloat16)
    upper_back = (back_hidden * silu_val).astype(jnp.bfloat16)
    return (error, back_hidden, gate_back, upper_back)


def grad_rows(inputs, error, hidden, gate_back, upper_back):
    return jnp.concatenate(
        [inner_rows(inputs, gate_back), inner_rows(inputs, upper_back), inner_rows(error, hidden)],
        axis=1,
    )


def local(target_x, target_y, poison_x, poison_y, w_gate, w_up, w_down):
    hidden_width = w_gate.shape[1]
    model_width = w_gate.shape[0]
    dp_size = lax.axis_size("dp")
    tgt_total = target_x.shape[0] * dp_size
    poi_total = poison_x.shape[0] * dp_size
    upper_tgt, silu_tgt, slope_tgt, curve_tgt, hidden_tgt, part_tgt = mlp_forward(
        target_x, w_gate, w_up, w_down
    )
    output_tgt = lax.psum(part_tgt.astype(jnp.bfloat16), "fsdp").astype(jnp.float32)
    error_tgt, back_tgt, gback_tgt, uback_tgt = backward(
        target_x, target_y, output_tgt, upper_tgt, silu_tgt, slope_tgt, w_down, tgt_total
    )
    upper_poi, silu_poi, slope_poi, curve_poi, hidden_poi, part_poi = mlp_forward(
        poison_x, w_gate, w_up, w_down
    )
    output_poi = lax.psum(part_poi.astype(jnp.bfloat16), "fsdp").astype(jnp.float32)
    error_poi, back_poi, gback_poi, uback_poi = backward(
        poison_x, poison_y, output_poi, upper_poi, silu_poi, slope_poi, w_down, poi_total
    )
    joint = lax.psum_scatter(
        jnp.concatenate(
            [
                grad_rows(target_x, error_tgt, hidden_tgt, gback_tgt, uback_tgt),
                grad_rows(poison_x, error_poi, hidden_poi, gback_poi, uback_poi),
            ],
            axis=1,
        ).astype(jnp.bfloat16),
        "dp",
        scatter_dimension=0,
        tiled=True,
    ).astype(jnp.float32)
    grad_tgt = joint[:, : 3 * hidden_width]
    grad_poi = joint[:, 3 * hidden_width :]
    norm_tt, norm_pp, cross_tp = lax.psum(
        (jnp.sum(grad_tgt * grad_tgt), jnp.sum(grad_poi * grad_poi), jnp.sum(grad_tgt * grad_poi)),
        ("fsdp", "dp"),
    )
    length_tgt = jnp.sqrt(norm_tt + EPSILON)
    length_poi = jnp.sqrt(norm_pp + EPSILON)
    denom = length_tgt * length_poi
    alignment = 1.0 - cross_tp / denom
    coef_tgt = -1.0 / denom
    coef_poi = cross_tp / (denom * length_poi * length_poi)
    local_sens = (coef_tgt * grad_tgt + coef_poi * grad_poi).astype(jnp.bfloat16)
    sens_full = lax.all_gather(local_sens, "dp", axis=0, tiled=True)
    v_gate = sens_full[:, :hidden_width]
    v_upper = sens_full[:, hidden_width : 2 * hidden_width]
    v_down = sens_full[:, 2 * hidden_width :]
    tan_gate = matmul(poison_x, v_gate)
    tan_upper = matmul(poison_x, v_upper)
    hidden_tan = (slope_poi * tan_gate * upper_poi + silu_poi * tan_upper).astype(jnp.bfloat16)
    part_tan = matmul(hidden_tan, w_down) + inner_cols(hidden_poi, v_down)
    output_tan = lax.psum(part_tan.astype(jnp.bfloat16), "fsdp").astype(jnp.float32)
    back_tan = (output_tan / poi_total).astype(jnp.bfloat16)
    mixed = inner_cols(back_tan, w_down) + matmul(error_poi, v_down)
    gate_total = (
        mixed * upper_poi * slope_poi
        + back_poi * (curve_poi * tan_gate * upper_poi + slope_poi * tan_upper)
    ).astype(jnp.bfloat16)
    upper_total = (mixed * silu_poi + back_poi * slope_poi * tan_gate).astype(jnp.bfloat16)
    gate_dir = (back_poi * slope_poi * upper_poi).astype(jnp.bfloat16)
    upper_dir = (back_poi * silu_poi).astype(jnp.bfloat16)
    part_grad = (
        inner_cols(gate_total, w_gate)
        + inner_cols(upper_total, w_up)
        + inner_cols(gate_dir, v_gate)
        + inner_cols(upper_dir, v_upper)
    )
    grad_cols = lax.psum_scatter(
        part_grad.astype(jnp.bfloat16), "fsdp", scatter_dimension=1, tiled=True
    ).astype(jnp.float32)
    columns = grad_cols.shape[1]
    residual_cols = lax.dynamic_slice_in_dim(
        back_tan, lax.axis_index("fsdp") * columns, columns, 1
    ).astype(jnp.float32)
    scaled = (grad_cols + residual_cols) * float(poi_total * model_width)
    total_sq = lax.psum(jnp.sum(scaled * scaled), ("fsdp", "dp"))
    mean_sq = total_sq / float(poi_total * model_width)
    return (scaled * lax.rsqrt(mean_sq + EPSILON), alignment)


def solution(mesh):
    in_specs = (
        P("dp", None),
        P("dp", None),
        P("dp", None),
        P("dp", None),
        P(None, "fsdp"),
        P(None, "fsdp"),
        P("fsdp", None),
    )
    out_specs = (P("dp", "fsdp"), P())
    return jax.shard_map(local, mesh=mesh, in_specs=in_specs, out_specs=out_specs, check_vma=False)
```

profile of v0, /device:TPU:0, one launch (start us, length us, event | category | flops | bytes accessed | tf_op | source)
XLA Modules:
  0.0 929.0 jit_solution(985929869053629563)
XLA Ops:
  7.2 4.0 fusion.64
  11.2 1.1 fusion.65
  12.4 1.1 copy-done.4
  13.4 1.1 multiply_convert_fusion.6
  14.6 1.8 multiply_convert_fusion.11
  16.4 0.2 copy-done
  16.6 2.6 convolution_convert_fusion.6
  19.3 1.7 convolution_convert_fusion.7
  21.0 0.2 reduce-scatter.3.cloned.1.call-start
  21.2 132.7 %all-reduce.7.cloned.1.call-done = (bf16[256,4096]{1,0:T(8,128)(2,1)}, bf16[128,4096]{1,0:T(8,128)(2,1)}) async-done(((bf16[256,4096]{1,0:T(8,128)(2,1)}, bf16[128,4096]{1,0:T(8,128)(2,1)}), (bf16[256,4096]{1,0:T(8,128)(2,1)}, bf16[128,4096]{1,0:T(8,128)(2,1)})) %all-reduce.7.cloned.1.call-update) | async-done | bytes 3145744 | tf_op jit(solution)/shard_map/psum | solution.py:74
  153.9 3.5 fusion.56
  157.5 2.9 fusion.3
  160.4 3.0 fusion.5
  163.4 3.1 fusion.1
  166.5 1.1 copy-done.16
  167.6 1.2 multiply_convert_fusion.1
  168.7 0.9 copy-done.1
  169.6 1.1 multiply_convert_fusion.4
  170.8 3.1 fusion.7
  173.9 2.9 fusion.9
  176.8 3.0 fusion
  179.9 231.8 %reduce-scatter.3.cloned.1.call-done = bf16[512,2688]{0,1:T(8,128)(2,1)} async-done(((bf16[4096,2688]{0,1:T(8,128)(2,1)}), bf16[512,2688]{0,1:T(8,128)(2,1)}) %reduce-scatter.3.cloned.1.call-update) | async-done | bytes 2752528 | tf_op jit(solution)/shard_map/reduce_scatter | solution.py:78
  411.6 2.5 convert_element_type.102
  414.2 2.4 copy-done.3
  416.6 1.3 multiply_reduce_fusion.1
  418.0 64.2 %all-reduce = (f32[]{:T(128)}, f32[]{:T(128)}, f32[]{:T(128)}) all-reduce(f32[]{:T(128)} %get-tuple-element.3, f32[]{:T(128)} %get-tuple-element.4, f32[]{:T(128)} %get-tuple-element.2), channel_id=1, replica_groups=mesh['fsdp'=16,'dp'=8] {'fsdp','dp'}, use_global_device_ids=true, to_apply=%region_8.0 | all-reduce | flops 3 | bytes 24 | tf_op jit(solution)/shard_map/psum | solution.py:92
  484.2 4.4 add_convert_fusion
  488.7 143.1 %all-gather.2.cloned.1.call-done = bf16[4096,1344]{0,1:T(8,128)(2,1)} async-done(((bf16[512,1344]{0,1:T(8,128)(2,1)}), bf16[4096,1344]{0,1:T(8,128)(2,1)}) %all-gather.2.cloned.1.call-update) | async-done | bytes 11010064 | tf_op jit(solution)/shard_map/all_gather | solution.py:103
  631.8 3.8 fusion.21
  635.6 4.0 fusion.24
  639.6 1.5 fusion.41
  641.1 4.6 fusion.10
  645.8 0.3 reduce-scatter.5.cloned.1.call-start
  646.1 124.7 %all-reduce.5.cloned.1.call-done = bf16[256,4096]{1,0:T(8,128)(2,1)} async-done(((bf16[256,4096]{1,0:T(8,128)(2,1)}), bf16[256,4096]{1,0:T(8,128)(2,1)}) %all-reduce.5.cloned.1.call-update) | async-done | bytes 2097168 | tf_op jit(solution)/shard_map/psum | solution.py:111
  770.8 4.0 fusion.55
  774.8 3.3 fusion.27
  778.2 1.6 fusion.42
  779.8 0.4 copy-done.5
  780.2 1.4 convolution_add_fusion.2
  781.6 1.0 slice-done.1
  782.7 1.0 slice-done.2
  783.6 1.4 convolution_add_fusion.1
  785.0 2.6 fusion.11
  788.3 2.0 multiply_convert_fusion
  790.3 62.7 %reduce-scatter.5.cloned.1.call-done = bf16[256,256]{1,0:T(8,128)(2,1)} async-done(((bf16[256,4096]{1,0:T(8,128)(2,1)}), bf16[256,256]{1,0:T(8,128)(2,1)}) %reduce-scatter.5.cloned.1.call-update) | async-done | bytes 131088 | tf_op jit(solution)/shard_map/reduce_scatter | solution.py:127
  853.0 1.6 multiply_reduce_fusion.3
  854.6 64.4 %psum.55 = f32[]{:T(128)} all-reduce(f32[]{:T(128)} %multiply_reduce_fusion.3), channel_id=1, replica_groups=mesh['fsdp'=16,'dp'=8] {'fsdp','dp'}, use_global_device_ids=true, to_apply=%region_12.0 | all-reduce | flops 1 | bytes 8 | tf_op jit(solution)/shard_map/psum | solution.py:135
  919.7 1.7 fusion.40
  (47 shorter events, 0.3 us)
Async XLA Ops:
  7.2 4.1 copy-start.8
  7.2 146.7 %all-reduce.7.cloned.1.call-start = ((), (), s32[]{:S(2)}) async-start(), calls=%async_computation.6 | async-start | bytes 6291456 | tf_op jit(solution)/shard_map/psum | solution.py:74
  7.2 4.0 copy-start.6
  7.2 5.1 copy-start.9
  11.2 2.2 copy-start.4
  14.6 2.0 copy-start
  16.4 2.9 copy-start.17
  19.3 134.6 %copy-start.13 = (bf16[128,4096]{1,0:T(8,128)(2,1)S(1)}, bf16[128,4096]{1,0:T(8,128)(2,1)}, u32[]{:S(2)}) copy-start(bf16[128,4096]{1,0:T(8,128)(2,1)} %param.8) | copy-start | bytes 3145732
  21.0 390.6 %reduce-scatter.3.cloned.1.call-start = ((), (), s32[]{:S(2)}) async-start(), calls=%async_computation.2 | async-start | bytes 24772608 | tf_op jit(solution)/shard_map/reduce_scatter | solution.py:78
  153.9 3.5 copy-start.19
  160.4 3.0 copy-start.14
  160.4 3.0 copy-start.18
  163.4 3.1 copy-start.10
  163.4 3.1 copy-start.15
  163.4 4.2 copy-start.16
  167.6 2.0 copy-start.1
  169.6 7.2 copy-start.11
  179.8 451.9 %all-gather.2.cloned.1.call-start = ((), (), s32[]{:S(2)}) async-start(), calls=%async_computation.3 | async-start | bytes 12386304 | tf_op jit(solution)/shard_map/all_gather | solution.py:103
  414.2 2.4 copy-start.3
  488.7 282.2 %all-reduce.5.cloned.1.call-start = ((), (), s32[]{:S(2)}) async-start(), calls=%async_computation.4 | async-start | bytes 4194304 | tf_op jit(solution)/shard_map/psum | solution.py:111
  635.6 4.0 copy-start.2
  645.8 207.3 %reduce-scatter.5.cloned.1.call-start = ((), (), s32[]{:S(2)}) async-start(), calls=%async_computation.5 | async-start | bytes 2228224 | tf_op jit(solution)/shard_map/reduce_scatter | solution.py:127
  770.8 4.0 copy-start.12
  774.8 3.4 copy-start.7
  778.2 2.0 copy-start.5
  778.2 3.5 slice-start
  778.2 4.5 slice-start.1
  780.2 3.4 slice-start.2
Sparse Core Ops, SparseCore 0:
  21.1 132.7 all-reduce.6
  180.0 231.6 reduce-scatter.2
  488.8 142.9 all-gather.1
  645.9 124.8 all-reduce.4
  787.8 65.2 reduce-scatter.4
where the time goes:
time: 930 us; the launch traced here: 929 us
  waiting for transfers between devices  695 us (75%)
  blocking collectives  129 us (14%)
  matrix products  63.4 us (7%)
  between operations  18.6 us (2%)
  other arithmetic  14.7 us (2%)
    reduce_scatter x1, waiting for transfers between devices, local(): lax.psum_scatter(jnp.concatenate([grad_rows(target_x, error_tgt, hidden_t...  232 us
    all_gather x1, waiting for transfers between devices, local(): sens_full = lax.all_gather(local_sens, 'dp', axis=0, tiled=True)  143 us
    psum x1, waiting for transfers between devices, local(): lax.psum(part_poi.astype(jnp.bfloat16), 'fsdp').astype(jnp.float32)  133 us
    psum x1, waiting for transfers between devices, local(): lax.psum(part_tan.astype(jnp.bfloat16), 'fsdp').astype(jnp.float32)  125 us
    psum x1, blocking collectives, local(): total_sq = lax.psum(jnp.sum(scaled * scaled), ('fsdp', 'dp'))  64.4 us
    psum x1, blocking collectives, local(): lax.psum((jnp.sum(grad_tgt * grad_tgt), jnp.sum(grad_poi * grad_poi), jnp...  64.2 us
    reduce_scatter x1, waiting for transfers between devices, local(): lax.psum_scatter(part_grad.astype(jnp.bfloat16), 'fsdp', scatter_dimensio...  62.7 us
    dot_general x10, matrix products, matmul(): return jnp.dot(left, right, preferred_element_type=jnp.float32)  25 us
  transfers between devices with their start and end apart: 5, of which 5 were waited for; matrix products, arithmetic and copies ran while one was open for 0% of the time, Pallas kernels for 0%

commit v1 on v0

--- a/solution.py
+++ b/solution.py
@@ -1,9 +1,34 @@
 import jax
 import jax.numpy as jnp
 from jax import lax
-from jax.sharding import PartitionSpec as P
+from jax.sharding import Mesh, PartitionSpec as P
 
 EPSILON = 1e-06
+FS = ("z", "ylo", "core")
+DP = ("x", "yhi")
+
+
+def rs_cols(part, n):
+    rows, cols = part.shape
+    r = part.reshape(rows, n, cols // n).transpose(1, 0, 2)
+    r = lax.all_to_all(r, FS, 0, 0, tiled=False)
+    return jnp.sum(r.astype(jnp.float32), 0)
+
+
+def ag_cols(piece, n):
+    rows, cols = piece.shape
+    g = lax.all_to_all(jnp.broadcast_to(piece[None], (n, rows, cols)), FS, 0, 0, tiled=False)
+    return g.transpose(1, 0, 2).reshape(rows, n * cols)
+
+
+def ag_rows(piece, n):
+    rows, cols = piece.shape
+    g = lax.all_to_all(jnp.broadcast_to(piece[None], (n, rows, cols)), DP, 0, 0, tiled=False)
+    return g.reshape(n * rows, cols)
+
+
+def psum_all(x):
+    return lax.psum(lax.psum(lax.psum(lax.psum(x, "core"), "ylo"), "z"), DP)
 
 
 def silu_parts(preact):
@@ -48,6 +73,13 @@
     return (error, back_hidden, gate_back, upper_back)
 
 
+def backward2(error, upper, silu_val, slope, w_down):
+    back_hidden = inner_cols(error, w_down)
+    gate_back = (back_hidden * upper * slope).astype(jnp.bfloat16)
+    upper_back = (back_hidden * silu_val).astype(jnp.bfloat16)
+    return (error, back_hidden, gate_back, upper_back)
+
+
 def grad_rows(inputs, error, hidden, gate_back, upper_back):
     return jnp.concatenate(
         [inner_rows(inputs, gate_back), inner_rows(inputs, upper_back), inner_rows(error, hidden)],
@@ -58,22 +90,36 @@
 def local(target_x, target_y, poison_x, poison_y, w_gate, w_up, w_down):
     hidden_width = w_gate.shape[1]
     model_width = w_gate.shape[0]
-    dp_size = lax.axis_size("dp")
+    dp_size = lax.axis_size(DP)
+    fs_size = lax.axis_size(FS)
     tgt_total = target_x.shape[0] * dp_size
     poi_total = poison_x.shape[0] * dp_size
     upper_tgt, silu_tgt, slope_tgt, curve_tgt, hidden_tgt, part_tgt = mlp_forward(
         target_x, w_gate, w_up, w_down
     )
-    output_tgt = lax.psum(part_tgt.astype(jnp.bfloat16), "fsdp").astype(jnp.float32)
-    error_tgt, back_tgt, gback_tgt, uback_tgt = backward(
-        target_x, target_y, output_tgt, upper_tgt, silu_tgt, slope_tgt, w_down, tgt_total
-    )
     upper_poi, silu_poi, slope_poi, curve_poi, hidden_poi, part_poi = mlp_forward(
         poison_x, w_gate, w_up, w_down
     )
-    output_poi = lax.psum(part_poi.astype(jnp.bfloat16), "fsdp").astype(jnp.float32)
-    error_poi, back_poi, gback_poi, uback_poi = backward(
-        poison_x, poison_y, output_poi, upper_poi, silu_poi, slope_poi, w_down, poi_total
+    n_tgt = target_x.shape[0]
+    fidx = lax.axis_index(FS)
+    width = model_width // fs_size
+    out_cols = rs_cols(
+        jnp.concatenate([part_tgt, part_poi], axis=0).astype(jnp.bfloat16), fs_size
+    )
+    x_cols = lax.dynamic_slice_in_dim(jnp.concatenate([target_x, poison_x], 0), fidx * width, width, 1)
+    y_cols = lax.dynamic_slice_in_dim(jnp.concatenate([target_y, poison_y], 0), fidx * width, width, 1)
+    scale_rows = jnp.concatenate(
+        [jnp.full((n_tgt, 1), float(tgt_total), jnp.float32),
+         jnp.full((poison_x.shape[0], 1), float(poi_total), jnp.float32)], 0)
+    err_cols = (
+        (x_cols.astype(jnp.float32) + out_cols - y_cols.astype(jnp.float32)) / scale_rows
+    ).astype(jnp.bfloat16)
+    error_all = ag_cols(err_cols, fs_size)
+    error_tgt, back_tgt, gback_tgt, uback_tgt = backward2(
+        error_all[:n_tgt], upper_tgt, silu_tgt, slope_tgt, w_down
+    )
+    error_poi, back_poi, gback_poi, uback_poi = backward2(
+        error_all[n_tgt:], upper_poi, silu_poi, slope_poi, w_down
     )
     joint = lax.psum_scatter(
         jnp.concatenate(
@@ -83,15 +129,14 @@
             ],
             axis=1,
         ).astype(jnp.bfloat16),
-        "dp",
+        DP,
         scatter_dimension=0,
         tiled=True,
     ).astype(jnp.float32)
     grad_tgt = joint[:, : 3 * hidden_width]
     grad_poi = joint[:, 3 * hidden_width :]
-    norm_tt, norm_pp, cross_tp = lax.psum(
-        (jnp.sum(grad_tgt * grad_tgt), jnp.sum(grad_poi * grad_poi), jnp.sum(grad_tgt * grad_poi)),
-        ("fsdp", "dp"),
+    norm_tt, norm_pp, cross_tp = psum_all(
+        (jnp.sum(grad_tgt * grad_tgt), jnp.sum(grad_poi * grad_poi), jnp.sum(grad_tgt * grad_poi))
     )
     length_tgt = jnp.sqrt(norm_tt + EPSILON)
     length_poi = jnp.sqrt(norm_pp + EPSILON)
@@ -100,7 +145,7 @@
     coef_tgt = -1.0 / denom
     coef_poi = cross_tp / (denom * length_poi * length_poi)
     local_sens = (coef_tgt * grad_tgt + coef_poi * grad_poi).astype(jnp.bfloat16)
-    sens_full = lax.all_gather(local_sens, "dp", axis=0, tiled=True)
+    sens_full = ag_rows(local_sens, dp_size)
     v_gate = sens_full[:, :hidden_width]
     v_upper = sens_full[:, hidden_width : 2 * hidden_width]
     v_down = sens_full[:, 2 * hidden_width :]
@@ -108,8 +153,9 @@
     tan_upper = matmul(poison_x, v_upper)
     hidden_tan = (slope_poi * tan_gate * upper_poi + silu_poi * tan_upper).astype(jnp.bfloat16)
     part_tan = matmul(hidden_tan, w_down) + inner_cols(hidden_poi, v_down)
-    output_tan = lax.psum(part_tan.astype(jnp.bfloat16), "fsdp").astype(jnp.float32)
-    back_tan = (output_tan / poi_total).astype(jnp.bfloat16)
+    tan_cols = rs_cols(part_tan.astype(jnp.bfloat16), fs_size)
+    back_cols = (tan_cols / poi_total).astype(jnp.bfloat16)
+    back_tan = ag_cols(back_cols, fs_size)
     mixed = inner_cols(back_tan, w_down) + matmul(error_poi, v_down)
     gate_total = (
         mixed * upper_poi * slope_poi
@@ -124,28 +170,24 @@
         + inner_cols(gate_dir, v_gate)
         + inner_cols(upper_dir, v_upper)
     )
-    grad_cols = lax.psum_scatter(
-        part_grad.astype(jnp.bfloat16), "fsdp", scatter_dimension=1, tiled=True
-    ).astype(jnp.float32)
-    columns = grad_cols.shape[1]
-    residual_cols = lax.dynamic_slice_in_dim(
-        back_tan, lax.axis_index("fsdp") * columns, columns, 1
-    ).astype(jnp.float32)
+    grad_cols = rs_cols(part_grad.astype(jnp.bfloat16), fs_size)
+    residual_cols = back_cols.astype(jnp.float32)
     scaled = (grad_cols + residual_cols) * float(poi_total * model_width)
-    total_sq = lax.psum(jnp.sum(scaled * scaled), ("fsdp", "dp"))
+    total_sq = psum_all(jnp.sum(scaled * scaled))
     mean_sq = total_sq / float(poi_total * model_width)
     return (scaled * lax.rsqrt(mean_sq + EPSILON), alignment)
 
 
 def solution(mesh):
+    fine = Mesh(mesh.devices.reshape(4, 2, 2, 4, 2), FS + DP)
     in_specs = (
-        P("dp", None),
-        P("dp", None),
-        P("dp", None),
-        P("dp", None),
-        P(None, "fsdp"),
-        P(None, "fsdp"),
-        P("fsdp", None),
+        P(DP, None),
+        P(DP, None),
+        P(DP, None),
+        P(DP, None),
+        P(None, FS),
+        P(None, FS),
+        P(FS, None),
     )
-    out_specs = (P("dp", "fsdp"), P())
-    return jax.shard_map(local, mesh=mesh, in_specs=in_specs, out_specs=out_specs, check_vma=False)
+    out_specs = (P(DP, FS), P())
+    return jax.shard_map(local, mesh=fine, in_specs=in_specs, out_specs=out_specs, check_vma=False)

time: 930 us -> 715 us (0.77)
  waiting for transfers between devices: 695 us -> 270 us
  blocking collectives: 129 us -> 337 us
  matrix products: 63.4 us -> 46.3 us
  local copies, waits for them, and re-layouts: 8.04 us -> 21 us
    psum x2 -> x0, waiting for transfers between devices: 257 us -> none  [the longest x1 133 us: local(): lax.psum(part_poi.astype(jnp.bfloat16), 'fsdp').astype(jnp.float32)]
    all_to_all x0 -> x5, blocking collectives: none -> 254 us  [the longest x1 121 us: ag_rows(): lax.all_to_all(jnp.broadcast_to(piece[None], (n, rows, cols)), DP, 0, 0,...]
    all_gather x1 -> x0, waiting for transfers between devices: 143 us -> none  [local(): sens_full = lax.all_gather(local_sens, 'dp', axis=0, tiled=True)]
    reduce_scatter x1 -> x0, waiting for transfers between devices: 62.7 us -> none  [local(): lax.psum_scatter(part_grad.astype(jnp.bfloat16), 'fsdp', scatter_dimensio...]
    psum x2 -> x8, blocking collectives: 129 us -> 82.3 us  [psum_all(): return lax.psum(lax.psum(lax.psum(lax.psum(x, 'core'), 'ylo'), 'z'), DP)]
    all_to_all x0 -> x1, waiting for transfers between devices: none -> 39 us  [rs_cols(): r = lax.all_to_all(r, FS, 0, 0, tiled=False)]
    dot_general x8, matrix products: 20.4 us -> 10.4 us  [inner_cols(): lax.dot_general(left, right, (((1,), (1,)), ((), ())), preferred_element_...]
  transfers between devices with their start and end apart: 5 -> 2, of which waited for: 5 -> 2; matrix products, arithmetic and copies ran while one was open for 0% -> 0% of each run, Pallas kernels for 0% -> 0%
where the time goes in v1:
time: 715 us
  blocking collectives  337 us (47%)
  waiting for transfers between devices  270 us (38%)
  matrix products  46.3 us (6%)
  local copies, waits for them, and re-layouts  21 us (3%)
  between operations  19 us (3%)
  other arithmetic  14.8 us (2%)
    reduce_scatter x1, waiting for transfers between devices, local(): lax.psum_scatter(jnp.concatenate([grad_rows(target_x, error_tgt, hidden_t...  231 us
    all_to_all x1, blocking collectives, ag_rows(): lax.all_to_all(jnp.broadcast_to(piece[None], (n, rows, cols)), DP, 0, 0,...  121 us
    psum x8, blocking collectives, psum_all(): return lax.psum(lax.psum(lax.psum(lax.psum(x, 'core'), 'ylo'), 'z'), DP)  82.3 us
    all_to_all x2, blocking collectives, ag_cols(): lax.all_to_all(jnp.broadcast_to(piece[None], (n, rows, cols)), FS, 0, 0,...  72.4 us
    all_to_all x2, blocking collectives, rs_cols(): r = lax.all_to_all(r, FS, 0, 0, tiled=False)  60.6 us
    all_to_all x1, waiting for transfers between devices, rs_cols(): r = lax.all_to_all(r, FS, 0, 0, tiled=False)  39 us
    dot_general x6, matrix products, inner_rows(): lax.dot_general(left, right, (((0,), (0,)), ((), ())), preferred_element_...  18 us
    dot_general x10, matrix products, matmul(): return jnp.dot(left, right, preferred_element_type=jnp.float32)  17.9 us
  transfers between devices with their start and end apart: 2, of which 2 were waited for; matrix products, arithmetic and copies ran while one was open for 0% of the time, Pallas kernels for 0%

profile of v1, /device:TPU:0, one launch (start us, length us, event | category | flops | bytes accessed | tf_op | source)
XLA Modules:
  0.0 714.6 jit_solution(9897157091752692636)
XLA Ops:
  7.2 3.6 fusion.65
  10.8 2.9 fusion.64
  13.8 1.1 multiply_convert_fusion.10
  15.4 1.1 multiply_convert_fusion.3
  18.3 1.3 convolution_convert_fusion.6
  19.8 2.0 maximum_bitcast_fusion
  21.8 6.7 all-to-all-start
  28.5 39.0 %all-to-all-done = bf16[16,384,256]{2,1,0:T(8,128)(2,1)} async-done(((bf16[16,384,256]{2,1,0:T(8,128)(2,1)}), bf16[16,384,256]{2,1,0:T(8,128)(2,1)}, u32[]{:S(2)}, u32[]{:S(2)}) %all-to-all-start) | async-done | bytes 3145760 | tf_op jit(solution)/shard_map/all_to_all | solution.py:14
  67.6 2.5 convert_reduce_fusion
  71.8 41.8 %all_to_all.30 = bf16[16,384,256]{1,2,0:T(8,128)(2,1)S(1)} all-to-all(bf16[16,384,256]{1,2,0:T(8,128)(2,1)S(1)} %broadcast_in_dim.6), channel_id=1, replica_groups=mesh['z'=4,'ylo'=2,'core'=2,'x'=4,'yhi'=2] {'z','ylo','core'}, dimensions={0} | all-to-all | bytes 6291456 | tf_op jit(solution)/shard_map/all_to_all | solution.py:20
  114.0 2.4 copy-done.1
  117.5 1.1 multiply_convert_fusion.1
  118.6 2.9 fusion.3
  121.6 3.0 fusion.5
  124.5 3.0 fusion.1
  127.5 3.1 fusion.7
  130.7 2.9 fusion.9
  133.6 3.0 fusion
  136.6 231.1 %reduce-scatter.2.cloned.1.call-done = bf16[512,2688]{0,1:T(8,128)(2,1)} async-done(((bf16[4096,2688]{0,1:T(8,128)(2,1)}), bf16[512,2688]{0,1:T(8,128)(2,1)}) %reduce-scatter.2.cloned.1.call-update) | async-done | bytes 2752528 | tf_op jit(solution)/shard_map/reduce_scatter | solution.py:124
  367.7 2.5 convert_element_type.84
  370.3 2.4 copy-done.4
  372.6 1.4 multiply_reduce_fusion.1
  374.0 3.1 all-reduce.2
  377.1 5.6 all-reduce.3
  382.7 11.3 %all-reduce.1 = (f32[]{:T(128)}, f32[]{:T(128)}, f32[]{:T(128)}) all-reduce(f32[]{:T(128)} %get-tuple-element.14, f32[]{:T(128)} %get-tuple-element.15, f32[]{:T(128)} %get-tuple-element.16), channel_id=1, replica_groups=mesh['z'=4,'ylo'=2,'core'=2,'x'=4,'yhi'=2] {'z'}, use_global_device_ids=true, to_apply=%region_15.0 | all-reduce | flops 3 | bytes 24 | tf_op jit(solution)/shard_map/psum | solution.py:31
  394.0 23.1 %all-reduce = (f32[]{:T(128)}, f32[]{:T(128)}, f32[]{:T(128)}) all-reduce(f32[]{:T(128)} %get-tuple-element.8, f32[]{:T(128)} %get-tuple-element.9, f32[]{:T(128)} %get-tuple-element.10), channel_id=1, replica_groups=mesh['z'=4,'ylo'=2,'core'=2,'x'=4,'yhi'=2] {'x','yhi'}, use_global_device_ids=true, to_apply=%region_16.0 | all-reduce | flops 3 | bytes 24 | tf_op jit(solution)/shard_map/psum | solution.py:31
  419.2 3.3 add_convert_fusion
  422.5 5.2 broadcast_in_dim.7
  427.7 121.3 %all_to_all.31 = bf16[8,512,1344]{1,2,0:T(8,128)(2,1)S(1)} all-to-all(bf16[8,512,1344]{1,2,0:T(8,128)(2,1)} %broadcast_in_dim.7), channel_id=1, replica_groups=mesh['z'=4,'ylo'=2,'core'=2,'x'=4,'yhi'=2] {'x','yhi'}, dimensions={0} | all-to-all | bytes 22020096 | tf_op jit(solution)/shard_map/all_to_all | solution.py:26
  549.0 1.3 copy.30
  550.6 1.1 fusion.21
  551.7 1.1 fusion.24
  552.9 3.3 copy-done.2
  556.1 1.5 fusion.40
  557.6 1.3 fusion.10
  559.1 30.3 %all_to_all.32 = bf16[16,256,256]{2,1,0:T(8,128)(2,1)S(1)} all-to-all(bf16[16,256,256]{2,1,0:T(8,128)(2,1)S(1)} %bitcast.107), channel_id=1, replica_groups=mesh['z'=4,'ylo'=2,'core'=2,'x'=4,'yhi'=2] {'z','ylo','core'}, dimensions={0} | all-to-all | bytes 4194304 | tf_op jit(solution)/shard_map/all_to_all | solution.py:14
  590.1 30.6 %all_to_all.33 = bf16[16,256,256]{1,2,0:T(8,128)(2,1)S(1)} all-to-all(bf16[16,256,256]{1,2,0:T(8,128)(2,1)S(1)} %broadcast_in_dim.8), channel_id=1, replica_groups=mesh['z'=4,'ylo'=2,'core'=2,'x'=4,'yhi'=2] {'z','ylo','core'}, dimensions={0} | all-to-all | bytes 4194304 | tf_op jit(solution)/shard_map/all_to_all | solution.py:20
  620.7 1.1 fusion.67
  622.3 3.3 fusion.27
  625.7 1.6 fusion.41
  627.7 1.4 convolution_add_fusion.2
  631.1 1.4 convolution_add_fusion.1
  632.5 1.3 fusion.11
  634.0 30.3 %all_to_all.34 = bf16[16,256,256]{2,1,0:T(8,128)(2,1)S(1)} all-to-all(bf16[16,256,256]{2,1,0:T(8,128)(2,1)S(1)} %bitcast.108), channel_id=1, replica_groups=mesh['z'=4,'ylo'=2,'core'=2,'x'=4,'yhi'=2] {'z','ylo','core'}, dimensions={0} | all-to-all | bytes 4194304 | tf_op jit(solution)/shard_map/all_to_all | solution.py:14
  665.3 3.1 psum.124
  668.3 5.5 psum.125
  674.5 9.2 %psum.126 = f32[]{:T(128)} all-reduce(f32[]{:T(128)} %psum.125), channel_id=1, replica_groups=mesh['z'=4,'ylo'=2,'core'=2,'x'=4,'yhi'=2] {'z'}, use_global_device_ids=true, to_apply=%region_22.0 | all-reduce | flops 1 | bytes 8 | tf_op jit(solution)/shard_map/psum | solution.py:31
  683.8 21.4 %psum.127 = f32[]{:T(128)} all-reduce(f32[]{:T(128)} %psum.126), channel_id=1, replica_groups=mesh['z'=4,'ylo'=2,'core'=2,'x'=4,'yhi'=2] {'x','yhi'}, use_global_device_ids=true, to_apply=%region_23.0 | all-reduce | flops 1 | bytes 8 | tf_op jit(solution)/shard_map/psum | solution.py:31
  (60 shorter events, 11.4 us)
Async XLA Ops:
  7.2 3.6 copy-start.8
  10.8 2.9 copy-start.6
  10.8 3.0 copy-start.10
  13.8 1.6 copy-start.13
  15.4 2.0 copy-start
  21.8 48.3 %copy-start.17 = (f32[384]{0:T(512)S(1)}, f32[384]{0:T(512)}, u32[]{:S(2)}) copy-start(f32[384]{0:T(512)} %constant.43.clone.1) | copy-start | bytes 4612
  21.8 45.8 %all-to-all-start = ((bf16[16,384,256]{2,1,0:T(8,128)(2,1)}), bf16[16,384,256]{2,1,0:T(8,128)(2,1)}, u32[]{:S(2)}, u32[]{:S(2)}) async-start(bf16[16,384,256]{2,1,0:T(8,128)(2,1)} %maximum_bitcast_fusion), calls=%async_computation | async-start | bytes 6291456 | tf_op jit(solution)/shard_map/all_to_all | solution.py:14
  28.5 339.2 %reduce-scatter.2.cloned.1.call-start = ((), (), s32[]{:S(2)}) async-start(), calls=%async_computation.7 | async-start | bytes 24772608 | tf_op jit(solution)/shard_map/reduce_scatter | solution.py:124
  67.6 2.5 copy-start.14
  113.6 2.8 copy-start.1
  114.0 19.6 %copy-start.11 = (bf16[256,16,256]{0,2,1:T(8,128)(2,1)}, bf16[256,16,256]{0,2,1:T(8,128)(2,1)S(1)}, u32[]{:S(2)}) copy-start(bf16[256,16,256]{0,2,1:T(8,128)(2,1)S(1)} %slice.37) | copy-start | bytes 6291460
  124.5 3.0 copy-start.15
  370.3 2.4 copy-start.4
  549.0 1.6 copy-start.16
  550.2 7.4 %copy-start.5 = (bf16[8,168,8,512]{3,2,0,1:T(8,128)(2,1)}, bf16[8,168,8,512]{3,2,0,1:T(8,128)(2,1)S(1)}, u32[]{:S(2)}) copy-start(bf16[8,168,8,512]{3,2,0,1:T(8,128)(2,1)S(1)} %copy.30) | copy-start | bytes 33030148
  551.7 4.4 copy-start.2
  589.9 30.8 %copy-start.3 = (bf16[448,4096]{1,0:T(8,128)(2,1)S(1)}, bf16[448,4096]{1,0:T(8,128)(2,1)}, u32[]{:S(2)}) copy-start(bf16[448,4096]{1,0:T(8,128)(2,1)} %param.13) | copy-start | bytes 11010052
  620.7 1.6 copy-start.12
  622.3 3.4 copy-start.9
  625.6 2.0 copy-start.7
  625.6 3.5 slice-start
  625.7 4.5 slice-start.1
  627.7 3.4 slice-start.2
Sparse Core Ops, SparseCore 0:
  136.7 230.9 reduce-scatter.1

commit v2 on v1

--- a/solution.py
+++ b/solution.py
@@ -27,8 +27,16 @@
     return g.reshape(n * rows, cols)
 
 
+def rs_rows(part, n):
+    rows, cols = part.shape
+    r = lax.all_to_all(part.reshape(n, rows // n, cols), DP, 0, 0, tiled=False)
+    return jnp.sum(r.astype(jnp.float32), 0)
+
+
 def psum_all(x):
-    return lax.psum(lax.psum(lax.psum(lax.psum(x, "core"), "ylo"), "z"), DP)
+    for axis in ("core", "ylo", "z", "x", "yhi"):
+        x = lax.psum(x, axis)
+    return x
 
 
 def silu_parts(preact):
@@ -121,22 +129,28 @@
     error_poi, back_poi, gback_poi, uback_poi = backward2(
         error_all[n_tgt:], upper_poi, silu_poi, slope_poi, w_down
     )
-    joint = lax.psum_scatter(
-        jnp.concatenate(
-            [
-                grad_rows(target_x, error_tgt, hidden_tgt, gback_tgt, uback_tgt),
-                grad_rows(poison_x, error_poi, hidden_poi, gback_poi, uback_poi),
-            ],
-            axis=1,
-        ).astype(jnp.bfloat16),
+    full_tgt = grad_rows(target_x, error_tgt, hidden_tgt, gback_tgt, uback_tgt)
+    full_poi = grad_rows(poison_x, error_poi, hidden_poi, gback_poi, uback_poi)
+    two = 2 * hidden_width
+    joint_gu = lax.psum_scatter(
+        jnp.concatenate([full_tgt[:, :two], full_poi[:, :two]], axis=1).astype(jnp.bfloat16),
         DP,
         scatter_dimension=0,
         tiled=True,
     ).astype(jnp.float32)
-    grad_tgt = joint[:, : 3 * hidden_width]
-    grad_poi = joint[:, 3 * hidden_width :]
+    joint_dn = rs_rows(
+        jnp.concatenate([full_tgt[:, two:], full_poi[:, two:]], axis=1).astype(jnp.bfloat16), dp_size
+    )
+    gu_tgt = joint_gu[:, :two]
+    gu_poi = joint_gu[:, two:]
+    dn_tgt = joint_dn[:, :hidden_width]
+    dn_poi = joint_dn[:, hidden_width:]
     norm_tt, norm_pp, cross_tp = psum_all(
-        (jnp.sum(grad_tgt * grad_tgt), jnp.sum(grad_poi * grad_poi), jnp.sum(grad_tgt * grad_poi))
+        (
+            jnp.sum(gu_tgt * gu_tgt) + jnp.sum(dn_tgt * dn_tgt),
+            jnp.sum(gu_poi * gu_poi) + jnp.sum(dn_poi * dn_poi),
+            jnp.sum(gu_tgt * gu_poi) + jnp.sum(dn_tgt * dn_poi),
+        )
     )
     length_tgt = jnp.sqrt(norm_tt + EPSILON)
     length_poi = jnp.sqrt(norm_pp + EPSILON)
@@ -144,11 +158,12 @@
     alignment = 1.0 - cross_tp / denom
     coef_tgt = -1.0 / denom
     coef_poi = cross_tp / (denom * length_poi * length_poi)
-    local_sens = (coef_tgt * grad_tgt + coef_poi * grad_poi).astype(jnp.bfloat16)
-    sens_full = ag_rows(local_sens, dp_size)
-    v_gate = sens_full[:, :hidden_width]
-    v_upper = sens_full[:, hidden_width : 2 * hidden_width]
-    v_down = sens_full[:, 2 * hidden_width :]
+    sens_gu = (coef_tgt * gu_tgt + coef_poi * gu_poi).astype(jnp.bfloat16)
+    sens_dn = (coef_tgt * dn_tgt + coef_poi * dn_poi).astype(jnp.bfloat16)
+    v_down = lax.all_gather(sens_dn, DP, axis=0, tiled=True)
+    full_gu = ag_rows(sens_gu, dp_size)
+    v_gate = full_gu[:, :hidden_width]
+    v_upper = full_gu[:, hidden_width:]
     tan_gate = matmul(poison_x, v_gate)
     tan_upper = matmul(poison_x, v_upper)
     hidden_tan = (slope_poi * tan_gate * upper_poi + silu_poi * tan_upper).astype(jnp.bfloat16)

time: 715 us -> 740 us (1.035)
  other arithmetic: 14.8 us -> 49.7 us
  waiting for transfers between devices: 270 us -> 243 us
    reduce_scatter x1, waiting for transfers between devices: 231 us -> 103 us  [local(): lax.psum_scatter(jnp.concatenate([full_tgt[:, :two], full_poi[:, :two]],...]
    all_to_all x0 -> x1, waiting for transfers between devices: none -> 98.9 us  [ag_rows(): lax.all_to_all(jnp.broadcast_to(piece[None], (n, rows, cols)), DP, 0, 0,...]
    concatenate x0 -> x2, other arithmetic: none -> 31.5 us  [the longest x1 25.7 us: local(): jnp.concatenate([full_tgt[:, :two], full_poi[:, :two]], axis=1)]
    psum x8 -> x10, blocking collectives: 82.3 us -> 71.7 us  [psum_all(): x = lax.psum(x, axis)]
    dot_general x8, matrix products: 10.4 us -> 19.5 us  [inner_cols(): lax.dot_general(left, right, (((1,), (1,)), ((), ())), preferred_element_...]
    dot_general x6, matrix products: 18 us -> 10.1 us  [inner_rows(): lax.dot_general(left, right, (((0,), (0,)), ((), ())), preferred_element_...]
  transfers between devices with their start and end apart: 2 -> 4, of which waited for: 2 -> 4; matrix products, arithmetic and copies ran while one was open for 0% -> 4% of each run, Pallas kernels for 0% -> 0%
where the time goes in v2:
time: 740 us; the launch traced here: 733 us
  blocking collectives  333 us (45%)
  waiting for transfers between devices  243 us (33%)
  matrix products  52.7 us (7%)
  other arithmetic  49.7 us (7%)
  between operations  23.1 us (3%)
  local copies, waits for them, and re-layouts  19.6 us (3%)
  starting transfers between devices  12 us (2%)
    all_to_all x1, blocking collectives, rs_rows(): r = lax.all_to_all(part.reshape(n, rows // n, cols), DP, 0, 0, tiled=False)  127 us
    reduce_scatter x1, waiting for transfers between devices, local(): lax.psum_scatter(jnp.concatenate([full_tgt[:, :two], full_poi[:, :two]],...  103 us
    all_to_all x1, waiting for transfers between devices, ag_rows(): lax.all_to_all(jnp.broadcast_to(piece[None], (n, rows, cols)), DP, 0, 0,...  98.9 us
    all_to_all x2, blocking collectives, ag_cols(): lax.all_to_all(jnp.broadcast_to(piece[None], (n, rows, cols)), FS, 0, 0,...  73.2 us
    psum x10, blocking collectives, psum_all(): x = lax.psum(x, axis)  71.7 us
    all_to_all x2, blocking collectives, rs_cols(): r = lax.all_to_all(r, FS, 0, 0, tiled=False)  60.6 us
    all_to_all x1, waiting for transfers between devices, rs_cols(): r = lax.all_to_all(r, FS, 0, 0, tiled=False)  39 us
    concatenate x1, other arithmetic, local(): jnp.concatenate([full_tgt[:, :two], full_poi[:, :two]], axis=1)  25.7 us
  transfers between devices with their start and end apart: 4, of which 4 were waited for; matrix products, arithmetic and copies ran while one was open for 4% of the time, Pallas kernels for 0%

profile of v2, /device:TPU:0, one launch (start us, length us, event | category | flops | bytes accessed | tf_op | source)
XLA Modules:
  0.0 732.9 jit_solution(1893333477408845353)
XLA Ops:
  7.2 4.0 fusion.54
  11.5 1.1 multiply_convert_fusion.3
  13.6 1.3 convolution_convert_fusion.4
  17.0 1.8 multiply_convert_fusion.10
  19.7 1.9 maximum_bitcast_fusion
  21.7 6.7 all-to-all-start
  28.5 39.0 %all-to-all-done = bf16[16,384,256]{2,1,0:T(8,128)(2,1)} async-done(((bf16[16,384,256]{2,1,0:T(8,128)(2,1)}), bf16[16,384,256]{2,1,0:T(8,128)(2,1)}, u32[]{:S(2)}, u32[]{:S(2)}) %all-to-all-start) | async-done | bytes 3145760 | tf_op jit(solution)/shard_map/all_to_all | solution.py:14
  67.5 2.5 convert_reduce_fusion.1
  70.0 1.7 multiply_convert_fusion.4
  73.2 42.3 %all_to_all.35 = bf16[16,384,256]{1,2,0:T(8,128)(2,1)S(1)} all-to-all(bf16[16,384,256]{1,2,0:T(8,128)(2,1)S(1)} %broadcast_in_dim.6), channel_id=1, replica_groups=mesh['z'=4,'ylo'=2,'core'=2,'x'=4,'yhi'=2] {'z','ylo','core'}, dimensions={0} | all-to-all | bytes 6291456 | tf_op jit(solution)/shard_map/all_to_all | solution.py:20
  116.0 2.8 copy-done.1
  124.9 1.2 fusion.2
  126.2 25.7 %pad_maximum_fusion = bf16[4096,1792]{0,1:T(8,128)(2,1)} fusion(bf16[4096,448]{0,1:T(8,128)(2,1)S(1)} %fusion.3, bf16[4096,448]{0,1:T(8,128)(2,1)S(1)} %fusion.2, bf16[4096,448]{0,1:T(8,128)(2,1)S(1)} %fusion.1, bf16[4096,448]{0,1:T(8,128)(2,1)S(1)} %fusion), kind=kLoop, calls=%fused_computation | loop fusion | flops 58720256 | bytes 29360128 | tf_op jit(solution)/shard_map/concatenate | solution.py:136
  151.9 2.5 convolution_convert_fusion.7
  154.5 3.0 convolution_convert_fusion.6
  157.5 5.7 pad_maximum_fusion.1
  163.2 127.1 %all_to_all.36 = bf16[8,512,896]{1,2,0:T(8,128)(2,1)S(1)} all-to-all(bf16[8,512,896]{1,2,0:T(8,128)(2,1)} %pad_maximum_fusion.1), channel_id=1, replica_groups=mesh['z'=4,'ylo'=2,'core'=2,'x'=4,'yhi'=2] {'x','yhi'}, dimensions={0} | all-to-all | bytes 14680064 | tf_op jit(solution)/shard_map/all_to_all | solution.py:32
  291.4 1.2 copy-done.14
  293.5 102.7 %reduce-scatter.2.cloned.1.call-done = bf16[512,1792]{0,1:T(8,128)(2,1)} async-done(((bf16[4096,1792]{0,1:T(8,128)(2,1)}), bf16[512,1792]{0,1:T(8,128)(2,1)}) %reduce-scatter.2.cloned.1.call-update) | async-done | bytes 1835024 | tf_op jit(solution)/shard_map/reduce_scatter | solution.py:135
  396.2 2.0 convert_element_type.92
  398.2 1.8 copy-done.4
  404.9 3.0 all-reduce.3
  407.9 5.6 all-reduce.4
  413.4 11.3 %all-reduce.1 = (f32[]{:T(128)}, f32[]{:T(128)}, f32[]{:T(128)}) all-reduce(f32[]{:T(128)} %get-tuple-element.20, f32[]{:T(128)} %get-tuple-element.21, f32[]{:T(128)} %get-tuple-element.22), channel_id=1, replica_groups=mesh['z'=4,'ylo'=2,'core'=2,'x'=4,'yhi'=2] {'z'}, use_global_device_ids=true, to_apply=%region_21.0 | all-reduce | flops 3 | bytes 24 | tf_op jit(solution)/shard_map/psum | solution.py:38
  424.7 9.2 %all-reduce = (f32[]{:T(128)}, f32[]{:T(128)}, f32[]{:T(128)}) all-reduce(f32[]{:T(128)} %get-tuple-element.11, f32[]{:T(128)} %get-tuple-element.12, f32[]{:T(128)} %get-tuple-element.13), channel_id=1, replica_groups=mesh['z'=4,'ylo'=2,'core'=2,'x'=4,'yhi'=2] {'x'}, use_global_device_ids=true, to_apply=%region_22.0 | all-reduce | flops 3 | bytes 24 | tf_op jit(solution)/shard_map/psum | solution.py:38
  434.0 7.1 all-reduce.2
  443.0 2.5 add_convert_fusion
  446.1 4.0 broadcast_in_dim.7
  450.1 5.0 all-to-all-start.3
  455.3 2.5 add_convert_fusion.1
  457.8 98.9 %all-to-all-done.3 = bf16[8,512,896]{2,1,0:T(8,128)(2,1)} async-done(((bf16[8,512,896]{2,1,0:T(8,128)(2,1)}), bf16[8,512,896]{2,1,0:T(8,128)(2,1)}, u32[]{:S(2)}, u32[]{:S(2)}) %all-to-all-start.3) | async-done | bytes 7340064 | tf_op jit(solution)/shard_map/all_to_all | solution.py:26
  556.7 3.6 fusion.12
  560.3 4.8 fusion.15
  565.9 3.6 fusion.28
  569.4 2.5 all-gather.2.cloned.1.call-done
  571.9 4.6 fusion.5
  576.7 30.3 %all_to_all.37 = bf16[16,256,256]{2,1,0:T(8,128)(2,1)S(1)} all-to-all(bf16[16,256,256]{2,1,0:T(8,128)(2,1)S(1)} %bitcast.102), channel_id=1, replica_groups=mesh['z'=4,'ylo'=2,'core'=2,'x'=4,'yhi'=2] {'z','ylo','core'}, dimensions={0} | all-to-all | bytes 4194304 | tf_op jit(solution)/shard_map/all_to_all | solution.py:14
  607.7 30.8 %all_to_all.38 = bf16[16,256,256]{1,2,0:T(8,128)(2,1)S(1)} all-to-all(bf16[16,256,256]{1,2,0:T(8,128)(2,1)S(1)} %broadcast_in_dim.8), channel_id=1, replica_groups=mesh['z'=4,'ylo'=2,'core'=2,'x'=4,'yhi'=2] {'z','ylo','core'}, dimensions={0} | all-to-all | bytes 4194304 | tf_op jit(solution)/shard_map/all_to_all | solution.py:20
  643.5 1.7 fusion.29
  645.5 1.5 convolution_add_fusion.2
  647.1 3.6 convolution_add_fusion.1
  650.7 4.8 fusion.4
  655.7 30.3 %all_to_all.39 = bf16[16,256,256]{2,1,0:T(8,128)(2,1)S(1)} all-to-all(bf16[16,256,256]{2,1,0:T(8,128)(2,1)S(1)} %bitcast.103), channel_id=1, replica_groups=mesh['z'=4,'ylo'=2,'core'=2,'x'=4,'yhi'=2] {'z','ylo','core'}, dimensions={0} | all-to-all | bytes 4194304 | tf_op jit(solution)/shard_map/all_to_all | solution.py:14
  687.0 3.1 psum.155
  690.0 5.5 psum.156
  695.6 9.2 %psum.157 = f32[]{:T(128)} all-reduce(f32[]{:T(128)} %psum.156), channel_id=1, replica_groups=mesh['z'=4,'ylo'=2,'core'=2,'x'=4,'yhi'=2] {'z'}, use_global_device_ids=true, to_apply=%region_29.0 | all-reduce | flops 1 | bytes 8 | tf_op jit(solution)/shard_map/psum | solution.py:38
  705.4 10.8 %psum.158 = f32[]{:T(128)} all-reduce(f32[]{:T(128)} %psum.157), channel_id=1, replica_groups=mesh['z'=4,'ylo'=2,'core'=2,'x'=4,'yhi'=2] {'x'}, use_global_device_ids=true, to_apply=%region_30.0 | all-reduce | flops 1 | bytes 8 | tf_op jit(solution)/shard_map/psum | solution.py:38
  716.2 7.0 psum.159
  (99 shorter events, 25.0 us)
Async XLA Ops:
  7.2 4.0 copy-start.10
  7.2 4.4 copy-start.5
  11.5 2.0 copy-start
  12.7 2.2 copy-start.26
  13.6 2.0 copy-start.7
  13.6 2.3 copy-start.9
  17.0 2.6 copy-start.21
  18.9 0.9 copy-start.33
  21.7 48.3 %copy-start.32 = (bf16[128,4096]{1,0:T(8,128)(2,1)S(1)}, bf16[128,4096]{1,0:T(8,128)(2,1)}, u32[]{:S(2)}) copy-start(bf16[128,4096]{1,0:T(8,128)(2,1)} %param.8) | copy-start | bytes 3145732
  21.7 48.4 %copy-start.34 = (f32[384]{0:T(512)S(1)}, f32[384]{0:T(512)}, u32[]{:S(2)}) copy-start(f32[384]{0:T(512)} %constant.43.clone.1) | copy-start | bytes 4612
  21.7 45.8 %all-to-all-start = ((bf16[16,384,256]{2,1,0:T(8,128)(2,1)}), bf16[16,384,256]{2,1,0:T(8,128)(2,1)}, u32[]{:S(2)}, u32[]{:S(2)}) async-start(bf16[16,384,256]{2,1,0:T(8,128)(2,1)} %maximum_bitcast_fusion), calls=%async_computation | async-start | bytes 6291456 | tf_op jit(solution)/shard_map/all_to_all | solution.py:14
  28.4 367.8 %reduce-scatter.2.cloned.1.call-start = ((), (), s32[]{:S(2)}) async-start(), calls=%async_computation.8 | async-start | bytes 16515072 | tf_op jit(solution)/shard_map/reduce_scatter | solution.py:135
  67.5 2.5 copy-start.11
  115.6 3.2 copy-start.1
  115.8 4.1 copy-start.18
  116.0 5.5 copy-start.17
  118.8 1.6 copy-start.12
  119.9 2.7 copy-start.30
  121.5 1.2 copy-start.22
  122.7 1.1 copy-start.29
  151.9 2.5 copy-start.19
  151.9 2.5 copy-start.27
  291.4 1.2 copy-start.14
  398.2 1.8 copy-start.4
  450.1 106.6 %copy-start.13 = (bf16[256,4096]{1,0:T(8,128)(2,1)S(1)}, bf16[256,4096]{1,0:T(8,128)(2,1)}, u32[]{:S(2)}) copy-start(bf16[256,4096]{1,0:T(8,128)(2,1)} %param.9) | copy-start | bytes 6291460
  450.1 106.6 %all-to-all-start.3 = ((bf16[8,512,896]{2,1,0:T(8,128)(2,1)}), bf16[8,512,896]{2,1,0:T(8,128)(2,1)}, u32[]{:S(2)}, u32[]{:S(2)}) async-start(bf16[8,512,896]{2,1,0:T(8,128)(2,1)} %broadcast_in_dim.7), calls=%async_computation.4 | async-start | bytes 14680064 | tf_op jit(solution)/shard_map/all_to_all | solution.py:26
  455.1 116.8 %all-gather.2.cloned.1.call-start = ((), (), s32[]{:S(2)}) async-start(), calls=%async_computation.9 | async-start | bytes 4128768 | tf_op jit(solution)/shard_map/all_gather | solution.py:163
  560.3 4.8 copy-start.15
  560.3 5.6 copy-start.2
  565.1 0.8 copy-start.23
  565.9 6.1 copy-start.28
  607.5 31.1 %copy-start.3 = (bf16[448,4096]{1,0:T(8,128)(2,1)S(1)}, bf16[448,4096]{1,0:T(8,128)(2,1)}, u32[]{:S(2)}) copy-start(bf16[448,4096]{1,0:T(8,128)(2,1)} %param.13) | copy-start | bytes 11010052
  638.5 1.6 copy-start.20
  638.5 2.7 copy-start.25
  641.2 2.0 copy-start.8
  641.2 2.1 copy-start.16
  641.2 2.3 copy-start.24
  643.5 2.0 copy-start.6
  647.0 3.6 copy-start.31
Sparse Core Ops, SparseCore 0:
  152.0 244.1 reduce-scatter.1
  458.1 113.7 all-gather.1

commit v3 on v1

--- a/solution.py
+++ b/solution.py
@@ -28,7 +28,9 @@
 
 
 def psum_all(x):
-    return lax.psum(lax.psum(lax.psum(lax.psum(x, "core"), "ylo"), "z"), DP)
+    for axis in ("core", "ylo", "z", "x", "yhi"):
+        x = lax.psum(x, axis)
+    return x
 
 
 def silu_parts(preact):
@@ -145,10 +147,10 @@
     coef_tgt = -1.0 / denom
     coef_poi = cross_tp / (denom * length_poi * length_poi)
     local_sens = (coef_tgt * grad_tgt + coef_poi * grad_poi).astype(jnp.bfloat16)
-    sens_full = ag_rows(local_sens, dp_size)
-    v_gate = sens_full[:, :hidden_width]
-    v_upper = sens_full[:, hidden_width : 2 * hidden_width]
-    v_down = sens_full[:, 2 * hidden_width :]
+    v_down = lax.all_gather(local_sens[:, 2 * hidden_width :], DP, axis=0, tiled=True)
+    full_gu = ag_rows(local_sens[:, : 2 * hidden_width], dp_size)
+    v_gate = full_gu[:, :hidden_width]
+    v_upper = full_gu[:, hidden_width:]
     tan_gate = matmul(poison_x, v_gate)
     tan_upper = matmul(poison_x, v_upper)
     hidden_tan = (slope_poi * tan_gate * upper_poi + silu_poi * tan_upper).astype(jnp.bfloat16)

time: 715 us -> 712 us (level)
  blocking collectives: 337 us -> 206 us
  waiting for transfers between devices: 270 us -> 373 us
  matrix products: 46.3 us -> 62.1 us
    all_to_all x1 -> x0, blocking collectives: 121 us -> none  [ag_rows(): lax.all_to_all(jnp.broadcast_to(piece[None], (n, rows, cols)), DP, 0, 0,...]
    all_to_all x0 -> x1, waiting for transfers between devices: none -> 99.8 us  [ag_rows(): lax.all_to_all(jnp.broadcast_to(piece[None], (n, rows, cols)), DP, 0, 0,...]
    psum x8 -> x10, blocking collectives: 82.3 us -> 72.4 us  [psum_all(): x = lax.psum(x, axis)]
    dot_general x8, matrix products: 10.4 us -> 19.5 us  [inner_cols(): lax.dot_general(left, right, (((1,), (1,)), ((), ())), preferred_element_...]
  transfers between devices with their start and end apart: 2 -> 4, of which waited for: 2 -> 4; matrix products, arithmetic and copies ran while one was open for 0% -> 2% of each run, Pallas kernels for 0% -> 0%
where the time goes in v3:
time: 712 us; the launch traced here: 705 us
  waiting for transfers between devices  373 us (52%)
  blocking collectives  206 us (29%)
  matrix products  62.1 us (9%)
  between operations  19.3 us (3%)
  local copies, waits for them, and re-layouts  18.6 us (3%)
  other arithmetic  14.8 us (2%)
  starting transfers between devices  11.6 us (2%)
    reduce_scatter x1, waiting for transfers between devices, local(): lax.psum_scatter(jnp.concatenate([grad_rows(target_x, error_tgt, hidden_t...  231 us
    all_to_all x1, waiting for transfers between devices, ag_rows(): lax.all_to_all(jnp.broadcast_to(piece[None], (n, rows, cols)), DP, 0, 0,...  99.8 us
    all_to_all x2, blocking collectives, ag_cols(): lax.all_to_all(jnp.broadcast_to(piece[None], (n, rows, cols)), FS, 0, 0,...  72.8 us
    psum x10, blocking collectives, psum_all(): x = lax.psum(x, axis)  72.4 us
    all_to_all x2, blocking collectives, rs_cols(): r = lax.all_to_all(r, FS, 0, 0, tiled=False)  61 us
    all_to_all x1, waiting for transfers between devices, rs_cols(): r = lax.all_to_all(r, FS, 0, 0, tiled=False)  39 us
    dot_general x10, matrix products, matmul(): return jnp.dot(left, right, preferred_element_type=jnp.float32)  24.7 us
    dot_general x8, matrix products, inner_cols(): lax.dot_general(left, right, (((1,), (1,)), ((), ())), preferred_element_...  19.5 us
  transfers between devices with their start and end apart: 4, of which 4 were waited for; matrix products, arithmetic and copies ran while one was open for 2% of the time, Pallas kernels for 0%

profile of v3, /device:TPU:0, one launch (start us, length us, event | category | flops | bytes accessed | tf_op | source)
XLA Modules:
  0.0 705.3 jit_solution(1604876894489453347)
XLA Ops:
  7.2 3.6 fusion.59
  10.8 2.9 fusion.58
  15.4 1.1 multiply_convert_fusion.3
  18.3 1.3 convolution_convert_fusion.6
  19.8 2.0 maximum_bitcast_fusion
  21.8 6.7 all-to-all-start
  28.5 39.0 %all-to-all-done = bf16[16,384,256]{2,1,0:T(8,128)(2,1)} async-done(((bf16[16,384,256]{2,1,0:T(8,128)(2,1)}), bf16[16,384,256]{2,1,0:T(8,128)(2,1)}, u32[]{:S(2)}, u32[]{:S(2)}) %all-to-all-start) | async-done | bytes 3145760 | tf_op jit(solution)/shard_map/all_to_all | solution.py:14
  67.6 2.5 convert_reduce_fusion
  71.8 42.0 %all_to_all.30 = bf16[16,384,256]{1,2,0:T(8,128)(2,1)S(1)} all-to-all(bf16[16,384,256]{1,2,0:T(8,128)(2,1)S(1)} %broadcast_in_dim.6), channel_id=1, replica_groups=mesh['z'=4,'ylo'=2,'core'=2,'x'=4,'yhi'=2] {'z','ylo','core'}, dimensions={0} | all-to-all | bytes 6291456 | tf_op jit(solution)/shard_map/all_to_all | solution.py:20
  114.1 2.4 copy-done.1
  117.7 1.1 multiply_convert_fusion.1
  118.8 2.9 fusion.3
  121.7 3.0 fusion.5
  124.7 3.0 fusion.1
  127.7 3.1 fusion.7
  130.9 2.9 fusion.9
  133.8 3.0 fusion
  136.8 231.4 %reduce-scatter.2.cloned.1.call-done = bf16[512,2688]{0,1:T(8,128)(2,1)} async-done(((bf16[4096,2688]{0,1:T(8,128)(2,1)}), bf16[512,2688]{0,1:T(8,128)(2,1)}) %reduce-scatter.2.cloned.1.call-update) | async-done | bytes 2752528 | tf_op jit(solution)/shard_map/reduce_scatter | solution.py:126
  368.2 2.5 convert_element_type.84
  370.8 2.4 copy-done.4
  373.2 1.4 multiply_reduce_fusion.1
  374.6 3.1 all-reduce.3
  377.7 5.6 all-reduce.4
  383.3 11.4 %all-reduce.1 = (f32[]{:T(128)}, f32[]{:T(128)}, f32[]{:T(128)}) all-reduce(f32[]{:T(128)} %get-tuple-element.17, f32[]{:T(128)} %get-tuple-element.18, f32[]{:T(128)} %get-tuple-element.19), channel_id=1, replica_groups=mesh['z'=4,'ylo'=2,'core'=2,'x'=4,'yhi'=2] {'z'}, use_global_device_ids=true, to_apply=%region_17.0 | all-reduce | flops 3 | bytes 24 | tf_op jit(solution)/shard_map/psum | solution.py:32
  394.7 9.3 %all-reduce = (f32[]{:T(128)}, f32[]{:T(128)}, f32[]{:T(128)}) all-reduce(f32[]{:T(128)} %get-tuple-element.8, f32[]{:T(128)} %get-tuple-element.9, f32[]{:T(128)} %get-tuple-element.10), channel_id=1, replica_groups=mesh['z'=4,'ylo'=2,'core'=2,'x'=4,'yhi'=2] {'x'}, use_global_device_ids=true, to_apply=%region_18.0 | all-reduce | flops 3 | bytes 24 | tf_op jit(solution)/shard_map/psum | solution.py:32
  404.0 7.3 %all-reduce.2 = (f32[]{:T(128)}, f32[]{:T(128)}, f32[]{:T(128)}) all-reduce(f32[]{:T(128)} %get-tuple-element.5, f32[]{:T(128)} %get-tuple-element.6, f32[]{:T(128)} %get-tuple-element.7), channel_id=1, replica_groups=mesh['z'=4,'ylo'=2,'core'=2,'x'=4,'yhi'=2] {'yhi'}, use_global_device_ids=true, to_apply=%region_19.0 | all-reduce | flops 3 | bytes 24 | tf_op jit(solution)/shard_map/psum | solution.py:32
  413.4 3.3 add_convert_fusion
  418.5 4.0 broadcast_in_dim.7
  422.4 4.8 all-to-all-start.2
  427.3 1.8 slice.47
  429.2 99.8 %all-to-all-done.2 = bf16[8,512,896]{2,1,0:T(8,128)(2,1)} async-done(((bf16[8,512,896]{2,1,0:T(8,128)(2,1)}), bf16[8,512,896]{2,1,0:T(8,128)(2,1)}, u32[]{:S(2)}, u32[]{:S(2)}) %all-to-all-start.2) | async-done | bytes 7340064 | tf_op jit(solution)/shard_map/all_to_all | solution.py:26
  529.0 4.4 fusion.18
  533.4 4.8 fusion.21
  538.2 3.6 fusion.34
  541.8 2.3 all-gather.2.cloned.1.call-done
  544.1 4.6 fusion.11
  548.9 30.6 %all_to_all.31 = bf16[16,256,256]{2,1,0:T(8,128)(2,1)S(1)} all-to-all(bf16[16,256,256]{2,1,0:T(8,128)(2,1)S(1)} %bitcast.98), channel_id=1, replica_groups=mesh['z'=4,'ylo'=2,'core'=2,'x'=4,'yhi'=2] {'z','ylo','core'}, dimensions={0} | all-to-all | bytes 4194304 | tf_op jit(solution)/shard_map/all_to_all | solution.py:14
  580.2 30.8 %all_to_all.32 = bf16[16,256,256]{1,2,0:T(8,128)(2,1)S(1)} all-to-all(bf16[16,256,256]{1,2,0:T(8,128)(2,1)S(1)} %broadcast_in_dim.8), channel_id=1, replica_groups=mesh['z'=4,'ylo'=2,'core'=2,'x'=4,'yhi'=2] {'z','ylo','core'}, dimensions={0} | all-to-all | bytes 4194304 | tf_op jit(solution)/shard_map/all_to_all | solution.py:20
  615.8 1.6 fusion.35
  617.8 1.6 convolution_add_fusion.2
  619.4 3.6 convolution_add_fusion.1
  623.0 4.8 fusion.10
  628.0 30.3 %all_to_all.33 = bf16[16,256,256]{2,1,0:T(8,128)(2,1)S(1)} all-to-all(bf16[16,256,256]{2,1,0:T(8,128)(2,1)S(1)} %bitcast.99), channel_id=1, replica_groups=mesh['z'=4,'ylo'=2,'core'=2,'x'=4,'yhi'=2] {'z','ylo','core'}, dimensions={0} | all-to-all | bytes 4194304 | tf_op jit(solution)/shard_map/all_to_all | solution.py:14
  659.3 3.1 psum.155
  662.4 5.5 psum.156
  667.9 9.2 %psum.157 = f32[]{:T(128)} all-reduce(f32[]{:T(128)} %psum.156), channel_id=1, replica_groups=mesh['z'=4,'ylo'=2,'core'=2,'x'=4,'yhi'=2] {'z'}, use_global_device_ids=true, to_apply=%region_25.0 | all-reduce | flops 1 | bytes 8 | tf_op jit(solution)/shard_map/psum | solution.py:32
  677.6 10.8 %psum.158 = f32[]{:T(128)} all-reduce(f32[]{:T(128)} %psum.157), channel_id=1, replica_groups=mesh['z'=4,'ylo'=2,'core'=2,'x'=4,'yhi'=2] {'x'}, use_global_device_ids=true, to_apply=%region_26.0 | all-reduce | flops 1 | bytes 8 | tf_op jit(solution)/shard_map/psum | solution.py:32
  688.4 7.0 psum.159
  (71 shorter events, 16.4 us)
Async XLA Ops:
  7.2 3.6 copy-start.7
  10.8 2.9 copy-start.5
  10.8 3.0 copy-start.9
  13.8 1.6 copy-start.12
  15.4 2.0 copy-start
  16.5 117.3 %copy-start.18 = (bf16[256,448]{0,1:T(8,128)(2,1)}, bf16[256,448]{0,1:T(8,128)(2,1)S(1)}, u32[]{:S(2)}) copy-start(bf16[256,448]{0,1:T(8,128)(2,1)S(1)} %get-tuple-element.20) | copy-start | bytes 688132
  21.8 48.3 %copy-start.22 = (f32[384]{0:T(512)S(1)}, f32[384]{0:T(512)}, u32[]{:S(2)}) copy-start(f32[384]{0:T(512)} %constant.43.clone.1) | copy-start | bytes 4612
  21.8 45.8 %all-to-all-start = ((bf16[16,384,256]{2,1,0:T(8,128)(2,1)}), bf16[16,384,256]{2,1,0:T(8,128)(2,1)}, u32[]{:S(2)}, u32[]{:S(2)}) async-start(bf16[16,384,256]{2,1,0:T(8,128)(2,1)} %maximum_bitcast_fusion), calls=%async_computation | async-start | bytes 6291456 | tf_op jit(solution)/shard_map/all_to_all | solution.py:14
  28.5 339.8 %reduce-scatter.2.cloned.1.call-start = ((), (), s32[]{:S(2)}) async-start(), calls=%async_computation.7 | async-start | bytes 24772608 | tf_op jit(solution)/shard_map/reduce_scatter | solution.py:126
  67.6 2.5 copy-start.13
  113.8 2.8 copy-start.1
  114.1 19.6 %copy-start.10 = (bf16[256,16,256]{0,2,1:T(8,128)(2,1)}, bf16[256,16,256]{0,2,1:T(8,128)(2,1)S(1)}, u32[]{:S(2)}) copy-start(bf16[256,16,256]{0,2,1:T(8,128)(2,1)S(1)} %slice.41) | copy-start | bytes 6291460
  118.8 12.1 %copy-start.20 = (bf16[256,448]{0,1:T(8,128)(2,1)}, bf16[256,448]{0,1:T(8,128)(2,1)S(1)}, u32[]{:S(2)}) copy-start(bf16[256,448]{0,1:T(8,128)(2,1)S(1)} %get-tuple-element.24) | copy-start | bytes 688132
  124.7 3.0 copy-start.14
  370.8 2.4 copy-start.4
  416.7 1.1 copy-start.16
  422.4 106.5 %all-to-all-start.2 = ((bf16[8,512,896]{2,1,0:T(8,128)(2,1)}), bf16[8,512,896]{2,1,0:T(8,128)(2,1)}, u32[]{:S(2)}, u32[]{:S(2)}) async-start(bf16[8,512,896]{2,1,0:T(8,128)(2,1)} %broadcast_in_dim.7), calls=%async_computation.3 | async-start | bytes 14680064 | tf_op jit(solution)/shard_map/all_to_all | solution.py:26
  427.3 116.8 %all-gather.2.cloned.1.call-start = ((), (), s32[]{:S(2)}) async-start(), calls=%async_computation.8 | async-start | bytes 4128768 | tf_op jit(solution)/shard_map/all_gather | solution.py:150
  529.0 4.4 copy-start.15
  533.4 4.8 copy-start.2
  538.2 5.9 copy-start.19
  580.0 31.1 %copy-start.3 = (bf16[448,4096]{1,0:T(8,128)(2,1)S(1)}, bf16[448,4096]{1,0:T(8,128)(2,1)}, u32[]{:S(2)}) copy-start(bf16[448,4096]{1,0:T(8,128)(2,1)} %param.13) | copy-start | bytes 11010052
  611.1 1.6 copy-start.11
  611.1 2.7 copy-start.17
  613.7 2.0 copy-start.8
  615.8 2.0 copy-start.6
  619.4 3.6 copy-start.21
Sparse Core Ops, SparseCore 0:
  136.9 231.2 reduce-scatter.1
  430.3 113.7 all-gather.1

commit v4 on v3

--- a/solution.py
+++ b/solution.py
@@ -123,20 +123,33 @@
     error_poi, back_poi, gback_poi, uback_poi = backward2(
         error_all[n_tgt:], upper_poi, silu_poi, slope_poi, w_down
     )
-    joint = lax.psum_scatter(
-        jnp.concatenate(
-            [
-                grad_rows(target_x, error_tgt, hidden_tgt, gback_tgt, uback_tgt),
-                grad_rows(poison_x, error_poi, hidden_poi, gback_poi, uback_poi),
-            ],
-            axis=1,
-        ).astype(jnp.bfloat16),
-        DP,
-        scatter_dimension=0,
-        tiled=True,
-    ).astype(jnp.float32)
-    grad_tgt = joint[:, : 3 * hidden_width]
-    grad_poi = joint[:, 3 * hidden_width :]
+    n_poi = poison_x.shape[0]
+    rows_d = model_width // dp_size
+    x_loc = jnp.concatenate([target_x, poison_x], 0)
+    x_rows = lax.all_to_all(
+        x_loc.reshape(-1, dp_size, rows_d).transpose(1, 0, 2), DP, 0, 0, tiled=False
+    )
+    e_rows = lax.all_to_all(
+        error_all.reshape(-1, dp_size, rows_d).transpose(1, 0, 2), DP, 0, 0, tiled=False
+    )
+    factors = jnp.concatenate(
+        [
+            jnp.concatenate([gback_tgt, uback_tgt, hidden_tgt], 1),
+            jnp.concatenate([gback_poi, uback_poi, hidden_poi], 1),
+        ],
+        0,
+    )
+    f_all = lax.all_gather(factors, DP, axis=0, tiled=False)
+    two = 2 * hidden_width
+
+    def block_grad(xr, er, fa):
+        dims = (((0, 1), (0, 1)), ((), ()))
+        gu = lax.dot_general(xr, fa[:, :, :two], dims, preferred_element_type=jnp.float32)
+        dn = lax.dot_general(er, fa[:, :, two:], dims, preferred_element_type=jnp.float32)
+        return jnp.concatenate([gu, dn], 1)
+
+    grad_tgt = block_grad(x_rows[:, :n_tgt], e_rows[:, :n_tgt], f_all[:, :n_tgt])
+    grad_poi = block_grad(x_rows[:, n_tgt:], e_rows[:, n_tgt:], f_all[:, n_tgt:])
     norm_tt, norm_pp, cross_tp = psum_all(
         (jnp.sum(grad_tgt * grad_tgt), jnp.sum(grad_poi * grad_poi), jnp.sum(grad_tgt * grad_poi))
     )

time: 712 us -> 676 us (0.949)
  waiting for transfers between devices: 373 us -> 319 us
  blocking collectives: 206 us -> 173 us
  starting transfers between devices: 11.6 us -> 35.8 us
  local copies, waits for them, and re-layouts: 18.6 us -> 41.6 us
    reduce_scatter x1 -> x0, waiting for transfers between devices: 231 us -> none  [local(): lax.psum_scatter(jnp.concatenate([grad_rows(target_x, error_tgt, hidden_t...]
    all_gather x0 -> x1, waiting for transfers between devices: none -> 108 us  [local(): f_all = lax.all_gather(factors, DP, axis=0, tiled=False)]
    all_to_all x0 -> x3, waiting for transfers between devices: none -> 68.8 us  [the longest x1 45.5 us: local(): lax.all_to_all(x_loc.reshape(-1, dp_size, rows_d).transpose(1, 0, 2), DP,...]
    all_to_all x2 -> x1, blocking collectives: 72.8 us -> 41.8 us  [ag_cols(): lax.all_to_all(jnp.broadcast_to(piece[None], (n, rows, cols)), FS, 0, 0,...]
    all_to_all x0 -> x3, starting transfers between devices: none -> 24.1 us  [the longest x1 12.8 us: local(): lax.all_to_all(error_all.reshape(-1, dp_size, rows_d).transpose(1, 0, 2),...]
    slice x0 -> x4, local copies, waits for them, and re-layouts: none -> 7.97 us  [the longest x2 4.08 us: block_grad(): fa[:, :, two:]]
    all_to_all x1, waiting for transfers between devices: 99.8 us -> 107 us  [ag_rows(): lax.all_to_all(jnp.broadcast_to(piece[None], (n, rows, cols)), DP, 0, 0,...]
    unnamed x46 -> x60, local copies, waits for them, and re-layouts: 10.2 us -> 16.3 us
  transfers between devices with their start and end apart: 4 -> 7, of which waited for: 4 -> 5; matrix products, arithmetic and copies ran while one was open for 2% -> 8% of each run, Pallas kernels for 0% -> 0%
where the time goes in v4:
time: 676 us; the launch traced here: 666 us
  waiting for transfers between devices  319 us (47%)
  blocking collectives  173 us (26%)
  matrix products  66.3 us (10%)
  local copies, waits for them, and re-layouts  41.6 us (6%)
  starting transfers between devices  35.8 us (5%)
  between operations  19.4 us (3%)
  other arithmetic  10.7 us (2%)
    all_gather x1, waiting for transfers between devices, local(): f_all = lax.all_gather(factors, DP, axis=0, tiled=False)  108 us
    all_to_all x1, waiting for transfers between devices, ag_rows(): lax.all_to_all(jnp.broadcast_to(piece[None], (n, rows, cols)), DP, 0, 0,...  107 us
    psum x10, blocking collectives, psum_all(): x = lax.psum(x, axis)  68.9 us
    all_to_all x2, blocking collectives, rs_cols(): r = lax.all_to_all(r, FS, 0, 0, tiled=False)  62.5 us
    all_to_all x1, waiting for transfers between devices, local(): lax.all_to_all(x_loc.reshape(-1, dp_size, rows_d).transpose(1, 0, 2), DP,...  45.5 us
    all_to_all x1, blocking collectives, ag_cols(): lax.all_to_all(jnp.broadcast_to(piece[None], (n, rows, cols)), FS, 0, 0,...  41.8 us
    all_to_all x1, waiting for transfers between devices, rs_cols(): r = lax.all_to_all(r, FS, 0, 0, tiled=False)  35 us
    dot_general x10, matrix products, matmul(): return jnp.dot(left, right, preferred_element_type=jnp.float32)  29.5 us
  transfers between devices with their start and end apart: 7, of which 5 were waited for; matrix products, arithmetic and copies ran while one was open for 8% of the time, Pallas kernels for 0%

profile of v4, /device:TPU:0, one launch (start us, length us, event | category | flops | bytes accessed | tf_op | source)
XLA Modules:
  0.0 666.1 jit_solution(12187804491762197555)
XLA Ops:
  7.2 3.6 fusion.67
  10.8 2.9 fusion.66
  15.7 1.9 multiply_convert_fusion.3
  20.1 1.9 maximum_bitcast_fusion
  22.0 6.5 all-to-all-start.1
  28.6 2.4 constant_dynamic-update-slice_fusion.1
  32.6 35.0 %all-to-all-done.1 = bf16[16,384,256]{2,1,0:T(8,128)(2,1)S(1)} async-done(((bf16[16,384,256]{2,1,0:T(8,128)(2,1)}), bf16[16,384,256]{2,1,0:T(8,128)(2,1)S(1)}, u32[]{:S(2)}, u32[]{:S(2)}) %all-to-all-start.1) | async-done | bytes 3145760 | tf_op jit(solution)/shard_map/all_to_all | solution.py:14
  71.1 41.8 %all_to_all.40 = bf16[16,384,256]{1,2,0:T(8,128)(2,1)S(1)} all-to-all(bf16[16,384,256]{1,2,0:T(8,128)(2,1)S(1)} %broadcast_in_dim.6), channel_id=1, replica_groups=mesh['z'=4,'ylo'=2,'core'=2,'x'=4,'yhi'=2] {'z','ylo','core'}, dimensions={0} | all-to-all | bytes 6291456 | tf_op jit(solution)/shard_map/all_to_all | solution.py:20
  113.3 2.4 copy-done.1
  120.7 4.7 copy.26
  125.4 6.6 all-to-all-start
  132.0 3.0 copy.31
  135.0 45.5 %all-to-all-done = bf16[8,384,512]{1,2,0:T(8,128)(2,1)} async-done(((bf16[8,384,512]{1,2,0:T(8,128)(2,1)}), bf16[8,384,512]{1,2,0:T(8,128)(2,1)}, u32[]{:S(2)}, u32[]{:S(2)}) %all-to-all-start) | async-done | bytes 3145760 | tf_op jit(solution)/shard_map/all_to_all | solution.py:129
  180.5 12.8 %all-to-all-start.3 = ((bf16[8,384,512]{2,1,0:T(8,128)(2,1)}), bf16[8,384,512]{2,1,0:T(8,128)(2,1)}, u32[]{:S(2)}, u32[]{:S(2)}) async-start(bf16[8,384,512]{2,1,0:T(8,128)(2,1)} %bitcast.88), calls=%async_computation.3 | async-start | bytes 6291456 | tf_op jit(solution)/shard_map/all_to_all | solution.py:132
  193.2 107.7 %all-gather.6.cloned.1.call-done = bf16[3072,1344]{0,1:T(8,128)(2,1)} async-done(((bf16[384,1344]{0,1:T(8,128)(2,1)}), bf16[3072,1344]{0,1:T(8,128)(2,1)}) %all-gather.6.cloned.1.call-update) | async-done | bytes 8257552 | tf_op jit(solution)/shard_map/all_gather | solution.py:142
  301.0 8.6 %copy.52 = bf16[168,8,8,384]{3,2,1,0:T(8,128)(2,1)} copy(bf16[168,8,8,384]{3,1,2,0:T(8,128)(2,1)} %bitcast.96) | data formatting | bytes 16515072
  312.4 2.8 slice.79
  315.2 2.3 slice.77
  317.5 2.5 fusion.16
  320.0 5.2 fusion.19
  325.2 3.4 fusion.24
  328.7 2.4 convolution_bitcast_fusion
  332.9 3.2 all-reduce.3
  336.0 5.7 all-reduce.4
  341.8 8.4 %all-reduce.1 = (f32[]{:T(128)}, f32[]{:T(128)}, f32[]{:T(128)}) all-reduce(f32[]{:T(128)} %get-tuple-element.17, f32[]{:T(128)} %get-tuple-element.18, f32[]{:T(128)} %get-tuple-element.19), channel_id=1, replica_groups=mesh['z'=4,'ylo'=2,'core'=2,'x'=4,'yhi'=2] {'z'}, use_global_device_ids=true, to_apply=%region_16.0 | all-reduce | flops 3 | bytes 24 | tf_op jit(solution)/shard_map/psum | solution.py:32
  350.2 10.8 %all-reduce = (f32[]{:T(128)}, f32[]{:T(128)}, f32[]{:T(128)}) all-reduce(f32[]{:T(128)} %get-tuple-element.8, f32[]{:T(128)} %get-tuple-element.9, f32[]{:T(128)} %get-tuple-element.10), channel_id=1, replica_groups=mesh['z'=4,'ylo'=2,'core'=2,'x'=4,'yhi'=2] {'x'}, use_global_device_ids=true, to_apply=%region_17.0 | all-reduce | flops 3 | bytes 24 | tf_op jit(solution)/shard_map/psum | solution.py:32
  361.0 7.1 %all-reduce.2 = (f32[]{:T(128)}, f32[]{:T(128)}, f32[]{:T(128)}) all-reduce(f32[]{:T(128)} %get-tuple-element.5, f32[]{:T(128)} %get-tuple-element.6, f32[]{:T(128)} %get-tuple-element.7), channel_id=1, replica_groups=mesh['z'=4,'ylo'=2,'core'=2,'x'=4,'yhi'=2] {'yhi'}, use_global_device_ids=true, to_apply=%region_18.0 | all-reduce | flops 3 | bytes 24 | tf_op jit(solution)/shard_map/psum | solution.py:32
  370.2 2.5 add_convert_fusion
  372.7 4.0 broadcast_in_dim.7
  376.7 4.8 all-to-all-start.4
  382.7 107.5 %all-to-all-done.4 = bf16[8,512,896]{2,1,0:T(8,128)(2,1)} async-done(((bf16[8,512,896]{2,1,0:T(8,128)(2,1)}), bf16[8,512,896]{2,1,0:T(8,128)(2,1)}, u32[]{:S(2)}, u32[]{:S(2)}) %all-to-all-start.4) | async-done | bytes 7340064 | tf_op jit(solution)/shard_map/all_to_all | solution.py:26
  490.1 4.3 fusion.29
  494.5 4.8 fusion.32
  499.3 3.6 fusion.48
  502.9 4.8 fusion
  507.9 31.9 %all_to_all.41 = bf16[16,256,256]{2,1,0:T(8,128)(2,1)S(1)} all-to-all(bf16[16,256,256]{2,1,0:T(8,128)(2,1)S(1)} %bitcast.92), channel_id=1, replica_groups=mesh['z'=4,'ylo'=2,'core'=2,'x'=4,'yhi'=2] {'z','ylo','core'}, dimensions={0} | all-to-all | bytes 4194304 | tf_op jit(solution)/shard_map/all_to_all | solution.py:14
  541.8 4.7 all-to-all-start.6
  546.5 4.5 fusion.68
  551.0 23.3 %all-to-all-done.6 = bf16[16,256,256]{1,2,0:T(8,128)(2,1)} async-done(((bf16[16,256,256]{1,2,0:T(8,128)(2,1)}), bf16[16,256,256]{1,2,0:T(8,128)(2,1)}, u32[]{:S(2)}, u32[]{:S(2)}) %all-to-all-start.6) | async-done | bytes 2097184 | tf_op jit(solution)/shard_map/all_to_all | solution.py:20
  574.3 4.0 convolution_add_fusion.4
  581.8 3.6 convolution_add_fusion.1
  585.5 4.8 fusion.1
  590.5 30.5 %all_to_all.42 = bf16[16,256,256]{2,1,0:T(8,128)(2,1)S(1)} all-to-all(bf16[16,256,256]{2,1,0:T(8,128)(2,1)S(1)} %bitcast.93), channel_id=1, replica_groups=mesh['z'=4,'ylo'=2,'core'=2,'x'=4,'yhi'=2] {'z','ylo','core'}, dimensions={0} | all-to-all | bytes 4194304 | tf_op jit(solution)/shard_map/all_to_all | solution.py:14
  622.0 3.1 psum.155
  625.0 5.5 psum.156
  630.6 9.2 %psum.157 = f32[]{:T(128)} all-reduce(f32[]{:T(128)} %psum.156), channel_id=1, replica_groups=mesh['z'=4,'ylo'=2,'core'=2,'x'=4,'yhi'=2] {'z'}, use_global_device_ids=true, to_apply=%region_24.0 | all-reduce | flops 1 | bytes 8 | tf_op jit(solution)/shard_map/psum | solution.py:32
  640.4 8.8 %psum.158 = f32[]{:T(128)} all-reduce(f32[]{:T(128)} %psum.157), channel_id=1, replica_groups=mesh['z'=4,'ylo'=2,'core'=2,'x'=4,'yhi'=2] {'x'}, use_global_device_ids=true, to_apply=%region_25.0 | all-reduce | flops 1 | bytes 8 | tf_op jit(solution)/shard_map/psum | solution.py:32
  649.2 7.0 %psum.159 = f32[]{:T(128)} all-reduce(f32[]{:T(128)} %psum.158), channel_id=1, replica_groups=mesh['z'=4,'ylo'=2,'core'=2,'x'=4,'yhi'=2] {'yhi'}, use_global_device_ids=true, to_apply=%region_26.0 | all-reduce | flops 1 | bytes 8 | tf_op jit(solution)/shard_map/psum | solution.py:32
  (94 shorter events, 28.0 us)
Async XLA Ops:
  7.2 3.6 copy-start.5
  10.8 2.9 copy-start.23
  10.8 2.9 copy-start.3
  10.8 3.0 copy-start.10
  13.9 3.7 copy-start.7
  13.9 1.8 copy-start.17
  15.7 2.0 copy-start
  22.0 45.6 %all-to-all-start.1 = ((bf16[16,384,256]{2,1,0:T(8,128)(2,1)}), bf16[16,384,256]{2,1,0:T(8,128)(2,1)S(1)}, u32[]{:S(2)}, u32[]{:S(2)}) async-start(bf16[16,384,256]{2,1,0:T(8,128)(2,1)} %maximum_bitcast_fusion), calls=%async_computation.1 | async-start | bytes 6291456 | tf_op jit(solution)/shard_map/all_to_all | solution.py:14
  28.6 272.4 %all-gather.6.cloned.1.call-start = ((), (), s32[]{:S(2)}) async-start(), calls=%async_computation.9 | async-start | bytes 9289728 | tf_op jit(solution)/shard_map/all_gather | solution.py:142
  28.6 2.4 copy-start.18
  31.1 37.0 %copy-start.28 = (f32[384]{0:T(512)S(1)}, f32[384]{0:T(512)}, u32[]{:S(2)}) copy-start(f32[384]{0:T(512)} %constant.43.clone.1) | copy-start | bytes 4612
  67.6 1.6 copy-start.21
  67.6 1.9 copy-start.22
  112.9 2.8 copy-start.1
  112.9 2.8 copy-start.24
  112.9 2.9 copy-start.27
  113.3 3.6 copy-start.20
  115.8 1.1 copy-start.8
  115.8 1.2 copy-start.12
  118.9 0.7 copy-start.25
  125.4 55.1 %all-to-all-start = ((bf16[8,384,512]{1,2,0:T(8,128)(2,1)}), bf16[8,384,512]{1,2,0:T(8,128)(2,1)}, u32[]{:S(2)}, u32[]{:S(2)}) async-start(bf16[8,384,512]{1,2,0:T(8,128)(2,1)} %bitcast.89), calls=%async_computation | async-start | bytes 6291456 | tf_op jit(solution)/shard_map/all_to_all | solution.py:129
  180.5 144.8 %all-to-all-start.3 = ((bf16[8,384,512]{2,1,0:T(8,128)(2,1)}), bf16[8,384,512]{2,1,0:T(8,128)(2,1)}, u32[]{:S(2)}, u32[]{:S(2)}) async-start(bf16[8,384,512]{2,1,0:T(8,128)(2,1)} %bitcast.88), calls=%async_computation.3 | async-start | bytes 6291456 | tf_op jit(solution)/shard_map/all_to_all | solution.py:132
  328.7 4.2 copy-start.15
  328.7 2.4 copy-start.14
  331.1 1.8 copy-start.16
  376.7 113.4 %all-to-all-start.4 = ((bf16[8,512,896]{2,1,0:T(8,128)(2,1)}), bf16[8,512,896]{2,1,0:T(8,128)(2,1)}, u32[]{:S(2)}, u32[]{:S(2)}) async-start(bf16[8,512,896]{2,1,0:T(8,128)(2,1)} %broadcast_in_dim.7), calls=%async_computation.4 | async-start | bytes 14680064 | tf_op jit(solution)/shard_map/all_to_all | solution.py:26
  381.5 121.4 %all-gather.4.cloned.1.call-start = ((), (), s32[]{:S(2)}) async-start(), calls=%async_computation.8 | async-start | bytes 4718592 | tf_op jit(solution)/shard_map/all_gather | solution.py:163
  490.1 4.3 copy-start.19
  494.5 4.8 copy-start.2
  494.5 4.8 copy-start.9
  494.5 4.8 copy-start.13
  541.8 32.5 %all-to-all-start.6 = ((bf16[16,256,256]{1,2,0:T(8,128)(2,1)}), bf16[16,256,256]{1,2,0:T(8,128)(2,1)}, u32[]{:S(2)}, u32[]{:S(2)}) async-start(bf16[16,256,256]{1,2,0:T(8,128)(2,1)} %broadcast_in_dim.8), calls=%async_computation.6 | async-start | bytes 4194304 | tf_op jit(solution)/shard_map/all_to_all | solution.py:20
  574.3 4.0 copy-start.6
  574.3 4.0 copy-start.11
  578.3 2.0 copy-start.4
  581.8 3.7 copy-start.26
Sparse Core Ops, SparseCore 0:
  120.8 180.1 all-gather.5
  384.7 113.6 all-gather.3

commit v5 on v4

--- a/solution.py
+++ b/solution.py
@@ -108,6 +108,11 @@
     out_cols = rs_cols(
         jnp.concatenate([part_tgt, part_poi], axis=0).astype(jnp.bfloat16), fs_size
     )
+    x_loc = jnp.concatenate([target_x, poison_x], 0)
+    x_rows = lax.all_to_all(
+        x_loc.reshape(-1, dp_size, model_width // dp_size).transpose(1, 0, 2), DP, 0, 0, tiled=False
+    )
+    x_rows, out_cols = lax.optimization_barrier((x_rows, out_cols))
     x_cols = lax.dynamic_slice_in_dim(jnp.concatenate([target_x, poison_x], 0), fidx * width, width, 1)
     y_cols = lax.dynamic_slice_in_dim(jnp.concatenate([target_y, poison_y], 0), fidx * width, width, 1)
     scale_rows = jnp.concatenate(
@@ -125,31 +130,29 @@
     )
     n_poi = poison_x.shape[0]
     rows_d = model_width // dp_size
-    x_loc = jnp.concatenate([target_x, poison_x], 0)
-    x_rows = lax.all_to_all(
-        x_loc.reshape(-1, dp_size, rows_d).transpose(1, 0, 2), DP, 0, 0, tiled=False
-    )
     e_rows = lax.all_to_all(
         error_all.reshape(-1, dp_size, rows_d).transpose(1, 0, 2), DP, 0, 0, tiled=False
     )
-    factors = jnp.concatenate(
+    h_all = lax.all_gather(jnp.concatenate([hidden_tgt, hidden_poi], 0), DP, axis=0, tiled=False)
+    gu_loc = jnp.concatenate(
         [
-            jnp.concatenate([gback_tgt, uback_tgt, hidden_tgt], 1),
-            jnp.concatenate([gback_poi, uback_poi, hidden_poi], 1),
+            jnp.concatenate([gback_tgt, uback_tgt], 1),
+            jnp.concatenate([gback_poi, uback_poi], 1),
         ],
         0,
     )
-    f_all = lax.all_gather(factors, DP, axis=0, tiled=False)
-    two = 2 * hidden_width
-
-    def block_grad(xr, er, fa):
+    gu_all = lax.all_to_all(
+        jnp.broadcast_to(gu_loc[None], (dp_size,) + gu_loc.shape), DP, 0, 0, tiled=False
+    )
+
+    def block_grad(xr, er, ga, ha):
         dims = (((0, 1), (0, 1)), ((), ()))
-        gu = lax.dot_general(xr, fa[:, :, :two], dims, preferred_element_type=jnp.float32)
-        dn = lax.dot_general(er, fa[:, :, two:], dims, preferred_element_type=jnp.float32)
+        gu = lax.dot_general(xr, ga, dims, preferred_element_type=jnp.float32)
+        dn = lax.dot_general(er, ha, dims, preferred_element_type=jnp.float32)
         return jnp.concatenate([gu, dn], 1)
 
-    grad_tgt = block_grad(x_rows[:, :n_tgt], e_rows[:, :n_tgt], f_all[:, :n_tgt])
-    grad_poi = block_grad(x_rows[:, n_tgt:], e_rows[:, n_tgt:], f_all[:, n_tgt:])
+    grad_tgt = block_grad(x_rows[:, :n_tgt], e_rows[:, :n_tgt], gu_all[:, :n_tgt], h_all[:, :n_tgt])
+    grad_poi = block_grad(x_rows[:, n_tgt:], e_rows[:, n_tgt:], gu_all[:, n_tgt:], h_all[:, n_tgt:])
     norm_tt, norm_pp, cross_tp = psum_all(
         (jnp.sum(grad_tgt * grad_tgt), jnp.sum(grad_poi * grad_poi), jnp.sum(grad_tgt * grad_poi))
     )

time: 676 us -> 676 us (level)
  waiting for transfers between devices: 319 us -> 328 us
  local copies, waits for them, and re-layouts: 41.6 us -> 33.1 us
    all_to_all x1, waiting for transfers between devices: 0.01 us -> 40.2 us  [local(): lax.all_to_all(error_all.reshape(-1, dp_size, rows_d).transpose(1, 0, 2),...]
    all_gather x1, waiting for transfers between devices: 108 us -> 84.3 us  [local(): lax.all_gather(jnp.concatenate([hidden_tgt, hidden_poi], 0), DP, axis=0,...]
    all_to_all x1, starting transfers between devices: 12.8 us -> 4.54 us  [local(): lax.all_to_all(error_all.reshape(-1, dp_size, rows_d).transpose(1, 0, 2),...]
    slice x4 -> x2, local copies, waits for them, and re-layouts: 7.97 us -> 0.18 us  [the longest x1 0.12 us: local(): h_all[:, n_tgt:]]
    unnamed x60 -> x58, local copies, waits for them, and re-layouts: 16.3 us -> 11.3 us
    all_to_all x1 -> x2, waiting for transfers between devices: 45.5 us -> 44.1 us  [the longest x1 44.1 us: local(): lax.all_to_all(x_loc.reshape(-1, dp_size, model_width // dp_size).transpo...]
  transfers between devices with their start and end apart: 7 -> 8, of which waited for: 5 -> 6; matrix products, arithmetic and copies ran while one was open for 8% -> 7% of each run, Pallas kernels for 0% -> 0%
where the time goes in v5:
time: 676 us; the launch traced here: 668 us
  waiting for transfers between devices  328 us (49%)
  blocking collectives  175 us (26%)
  matrix products  68.6 us (10%)
  local copies, waits for them, and re-layouts  33.1 us (5%)
  starting transfers between devices  32.5 us (5%)
  between operations  19.5 us (3%)
  other arithmetic  11.4 us (2%)
    all_to_all x1, waiting for transfers between devices, ag_rows(): lax.all_to_all(jnp.broadcast_to(piece[None], (n, rows, cols)), DP, 0, 0,...  105 us
    all_gather x1, waiting for transfers between devices, local(): lax.all_gather(jnp.concatenate([hidden_tgt, hidden_poi], 0), DP, axis=0,...  84.3 us
    psum x10, blocking collectives, psum_all(): x = lax.psum(x, axis)  72 us
    all_to_all x2, blocking collectives, rs_cols(): r = lax.all_to_all(r, FS, 0, 0, tiled=False)  61.1 us
    all_to_all x1, waiting for transfers between devices, local(): lax.all_to_all(x_loc.reshape(-1, dp_size, model_width // dp_size).transpo...  44.1 us
    all_to_all x1, blocking collectives, ag_cols(): lax.all_to_all(jnp.broadcast_to(piece[None], (n, rows, cols)), FS, 0, 0,...  41.6 us
    all_to_all x1, waiting for transfers between devices, local(): lax.all_to_all(error_all.reshape(-1, dp_size, rows_d).transpose(1, 0, 2),...  40.2 us
    all_to_all x1, waiting for transfers between devices, rs_cols(): r = lax.all_to_all(r, FS, 0, 0, tiled=False)  30.4 us
  transfers between devices with their start and end apart: 8, of which 6 were waited for; matrix products, arithmetic and copies ran while one was open for 7% of the time, Pallas kernels for 0%

profile of v5, /device:TPU:0, one launch (start us, length us, event | category | flops | bytes accessed | tf_op | source)
XLA Modules:
  0.0 667.8 jit_solution(11944103253270933700)
XLA Ops:
  7.2 3.6 fusion.67
  10.8 2.9 fusion.66
  22.0 6.5 all-to-all-start.1
  28.6 2.5 constant_dynamic-update-slice_fusion.1
  32.6 4.6 copy.24
  37.2 30.4 %all-to-all-done.1 = bf16[16,384,256]{2,1,0:T(8,128)(2,1)S(1)} async-done(((bf16[16,384,256]{2,1,0:T(8,128)(2,1)}), bf16[16,384,256]{2,1,0:T(8,128)(2,1)S(1)}, u32[]{:S(2)}, u32[]{:S(2)}) %all-to-all-start.1) | async-done | bytes 3145760 | tf_op jit(solution)/shard_map/all_to_all | solution.py:14
  67.6 6.6 all-to-all-start
  75.5 44.1 %all-to-all-done = bf16[8,384,512]{1,2,0:T(8,128)(2,1)} async-done(((bf16[8,384,512]{1,2,0:T(8,128)(2,1)}), bf16[8,384,512]{1,2,0:T(8,128)(2,1)}, u32[]{:S(2)}, u32[]{:S(2)}) %all-to-all-start) | async-done | bytes 3145760 | tf_op jit(solution)/shard_map/all_to_all | solution.py:112
  121.4 41.6 %all_to_all.45 = bf16[16,384,256]{1,2,0:T(8,128)(2,1)S(1)} all-to-all(bf16[16,384,256]{1,2,0:T(8,128)(2,1)S(1)} %broadcast_in_dim.8), channel_id=1, replica_groups=mesh['z'=4,'ylo'=2,'core'=2,'x'=4,'yhi'=2] {'z','ylo','core'}, dimensions={0} | all-to-all | bytes 6291456 | tf_op jit(solution)/shard_map/all_to_all | solution.py:20
  163.0 2.9 copy.29
  165.9 4.5 all-to-all-start.4
  171.6 3.3 multiply_convert_fusion.8
  175.2 2.6 copy-done.1
  180.2 40.2 %all-to-all-done.4 = bf16[8,384,512]{2,1,0:T(8,128)(2,1)} async-done(((bf16[8,384,512]{2,1,0:T(8,128)(2,1)}), bf16[8,384,512]{2,1,0:T(8,128)(2,1)}, u32[]{:S(2)}, u32[]{:S(2)}) %all-to-all-start.4) | async-done | bytes 3145760 | tf_op jit(solution)/shard_map/all_to_all | solution.py:133
  220.5 3.2 broadcast_in_dim.9
  223.6 4.7 all-to-all-start.3
  228.3 84.3 %all-gather.6.cloned.1.call-done = bf16[3072,448]{0,1:T(8,128)(2,1)} async-done(((bf16[384,448]{0,1:T(8,128)(2,1)}), bf16[3072,448]{0,1:T(8,128)(2,1)}) %all-gather.6.cloned.1.call-update) | async-done | bytes 2752528 | tf_op jit(solution)/shard_map/all_gather | solution.py:136
  312.6 2.4 copy.47
  315.2 3.0 convolution_bitcast_fusion
  318.2 3.9 fusion.24
  322.0 5.0 fusion.19
  327.1 3.2 fusion.16
  333.2 3.1 all-reduce.3
  336.4 5.6 all-reduce.4
  341.9 11.3 %all-reduce.1 = (f32[]{:T(128)}, f32[]{:T(128)}, f32[]{:T(128)}) all-reduce(f32[]{:T(128)} %get-tuple-element.21, f32[]{:T(128)} %get-tuple-element.22, f32[]{:T(128)} %get-tuple-element.23), channel_id=1, replica_groups=mesh['z'=4,'ylo'=2,'core'=2,'x'=4,'yhi'=2] {'z'}, use_global_device_ids=true, to_apply=%region_16.0 | all-reduce | flops 3 | bytes 24 | tf_op jit(solution)/shard_map/psum | solution.py:32
  353.2 11.2 %all-reduce = (f32[]{:T(128)}, f32[]{:T(128)}, f32[]{:T(128)}) all-reduce(f32[]{:T(128)} %get-tuple-element.12, f32[]{:T(128)} %get-tuple-element.13, f32[]{:T(128)} %get-tuple-element.14), channel_id=1, replica_groups=mesh['z'=4,'ylo'=2,'core'=2,'x'=4,'yhi'=2] {'x'}, use_global_device_ids=true, to_apply=%region_17.0 | all-reduce | flops 3 | bytes 24 | tf_op jit(solution)/shard_map/psum | solution.py:32
  364.3 7.1 %all-reduce.2 = (f32[]{:T(128)}, f32[]{:T(128)}, f32[]{:T(128)}) all-reduce(f32[]{:T(128)} %get-tuple-element.9, f32[]{:T(128)} %get-tuple-element.10, f32[]{:T(128)} %get-tuple-element.11), channel_id=1, replica_groups=mesh['z'=4,'ylo'=2,'core'=2,'x'=4,'yhi'=2] {'yhi'}, use_global_device_ids=true, to_apply=%region_18.0 | all-reduce | flops 3 | bytes 24 | tf_op jit(solution)/shard_map/psum | solution.py:32
  373.5 2.5 add_convert_fusion
  377.2 4.0 broadcast_in_dim.10
  381.2 5.0 all-to-all-start.5
  388.3 105.5 %all-to-all-done.5 = bf16[8,512,896]{2,1,0:T(8,128)(2,1)} async-done(((bf16[8,512,896]{2,1,0:T(8,128)(2,1)}), bf16[8,512,896]{2,1,0:T(8,128)(2,1)}, u32[]{:S(2)}, u32[]{:S(2)}) %all-to-all-start.5) | async-done | bytes 7340064 | tf_op jit(solution)/shard_map/all_to_all | solution.py:26
  493.8 3.7 fusion.29
  497.5 4.8 fusion.32
  502.4 3.6 fusion.48
  505.9 4.8 fusion
  510.9 30.6 %all_to_all.46 = bf16[16,256,256]{2,1,0:T(8,128)(2,1)S(1)} all-to-all(bf16[16,256,256]{2,1,0:T(8,128)(2,1)S(1)} %bitcast.90), channel_id=1, replica_groups=mesh['z'=4,'ylo'=2,'core'=2,'x'=4,'yhi'=2] {'z','ylo','core'}, dimensions={0} | all-to-all | bytes 4194304 | tf_op jit(solution)/shard_map/all_to_all | solution.py:14
  543.4 4.7 all-to-all-start.7
  548.1 4.5 fusion.68
  552.6 23.3 %all-to-all-done.7 = bf16[16,256,256]{1,2,0:T(8,128)(2,1)} async-done(((bf16[16,256,256]{1,2,0:T(8,128)(2,1)}), bf16[16,256,256]{1,2,0:T(8,128)(2,1)}, u32[]{:S(2)}, u32[]{:S(2)}) %all-to-all-start.7) | async-done | bytes 2097184 | tf_op jit(solution)/shard_map/all_to_all | solution.py:20
  576.0 4.0 convolution_add_fusion.4
  583.5 3.6 convolution_add_fusion.1
  587.1 4.8 fusion.1
  592.1 30.5 %all_to_all.47 = bf16[16,256,256]{2,1,0:T(8,128)(2,1)S(1)} all-to-all(bf16[16,256,256]{2,1,0:T(8,128)(2,1)S(1)} %bitcast.91), channel_id=1, replica_groups=mesh['z'=4,'ylo'=2,'core'=2,'x'=4,'yhi'=2] {'z','ylo','core'}, dimensions={0} | all-to-all | bytes 4194304 | tf_op jit(solution)/shard_map/all_to_all | solution.py:14
  623.6 3.1 psum.155
  626.7 5.5 psum.156
  632.2 9.2 %psum.157 = f32[]{:T(128)} all-reduce(f32[]{:T(128)} %psum.156), channel_id=1, replica_groups=mesh['z'=4,'ylo'=2,'core'=2,'x'=4,'yhi'=2] {'z'}, use_global_device_ids=true, to_apply=%region_24.0 | all-reduce | flops 1 | bytes 8 | tf_op jit(solution)/shard_map/psum | solution.py:32
  642.0 8.8 %psum.158 = f32[]{:T(128)} all-reduce(f32[]{:T(128)} %psum.157), channel_id=1, replica_groups=mesh['z'=4,'ylo'=2,'core'=2,'x'=4,'yhi'=2] {'x'}, use_global_device_ids=true, to_apply=%region_25.0 | all-reduce | flops 1 | bytes 8 | tf_op jit(solution)/shard_map/psum | solution.py:32
  650.9 7.0 %psum.159 = f32[]{:T(128)} all-reduce(f32[]{:T(128)} %psum.158), channel_id=1, replica_groups=mesh['z'=4,'ylo'=2,'core'=2,'x'=4,'yhi'=2] {'yhi'}, use_global_device_ids=true, to_apply=%region_26.0 | all-reduce | flops 1 | bytes 8 | tf_op jit(solution)/shard_map/psum | solution.py:32
  (95 shorter events, 30.5 us)
Async XLA Ops:
  7.2 3.6 copy-start.5
  10.8 2.9 copy-start.24
  10.8 2.9 copy-start.3
  10.8 3.0 copy-start.10
  13.9 3.8 copy-start.7
  13.9 1.8 copy-start.17
  15.7 2.0 copy-start
  17.6 153.0 %copy-start.22 = (bf16[256,448]{0,1:T(8,128)(2,1)}, bf16[256,448]{0,1:T(8,128)(2,1)S(1)}, u32[]{:S(2)}) copy-start(bf16[256,448]{0,1:T(8,128)(2,1)S(1)} %get-tuple-element.28) | copy-start | bytes 688132
  22.0 45.6 %all-to-all-start.1 = ((bf16[16,384,256]{2,1,0:T(8,128)(2,1)}), bf16[16,384,256]{2,1,0:T(8,128)(2,1)S(1)}, u32[]{:S(2)}, u32[]{:S(2)}) async-start(bf16[16,384,256]{2,1,0:T(8,128)(2,1)} %maximum_bitcast_fusion), calls=%async_computation.1 | async-start | bytes 6291456 | tf_op jit(solution)/shard_map/all_to_all | solution.py:14
  28.6 2.5 copy-start.18
  67.6 51.9 %all-to-all-start = ((bf16[8,384,512]{1,2,0:T(8,128)(2,1)}), bf16[8,384,512]{1,2,0:T(8,128)(2,1)}, u32[]{:S(2)}, u32[]{:S(2)}) async-start(bf16[8,384,512]{1,2,0:T(8,128)(2,1)} %bitcast.84), calls=%async_computation | async-start | bytes 6291456 | tf_op jit(solution)/shard_map/all_to_all | solution.py:112
  74.3 45.3 %copy-start.27 = (f32[384]{0:T(512)S(1)}, f32[384]{0:T(512)}, u32[]{:S(2)}) copy-start(f32[384]{0:T(512)} %constant.43.clone.1) | copy-start | bytes 4612
  165.9 54.6 %all-to-all-start.4 = ((bf16[8,384,512]{2,1,0:T(8,128)(2,1)}), bf16[8,384,512]{2,1,0:T(8,128)(2,1)}, u32[]{:S(2)}, u32[]{:S(2)}) async-start(bf16[8,384,512]{2,1,0:T(8,128)(2,1)} %bitcast.85), calls=%async_computation.4 | async-start | bytes 6291456 | tf_op jit(solution)/shard_map/all_to_all | solution.py:133
  170.4 142.2 %all-gather.6.cloned.1.call-start = ((), (), s32[]{:S(2)}) async-start(), calls=%async_computation.10 | async-start | bytes 3096576 | tf_op jit(solution)/shard_map/all_gather | solution.py:136
  171.6 3.6 copy-start.11
  175.0 2.8 copy-start.1
  175.0 2.9 copy-start.8
  175.2 3.9 copy-start.21
  179.1 0.7 copy-start.25
  223.6 98.4 %all-to-all-start.3 = ((bf16[8,384,896]{2,1,0:T(8,128)(2,1)}), bf16[8,384,896]{2,1,0:T(8,128)(2,1)}, u32[]{:S(2)}, u32[]{:S(2)}) async-start(bf16[8,384,896]{2,1,0:T(8,128)(2,1)} %broadcast_in_dim.9), calls=%async_computation.3 | async-start | bytes 11010048 | tf_op jit(solution)/shard_map/all_to_all | solution.py:144
  327.0 4.5 copy-start.15
  327.1 4.5 copy-start.16
  330.3 1.3 copy-start.13
  376.0 1.1 copy-start.14
  381.2 112.6 %copy-start.19 = (bf16[256,4096]{1,0:T(8,128)(2,1)S(1)}, bf16[256,4096]{1,0:T(8,128)(2,1)}, u32[]{:S(2)}) copy-start(bf16[256,4096]{1,0:T(8,128)(2,1)} %param.9) | copy-start | bytes 6291460
  381.2 112.6 %all-to-all-start.5 = ((bf16[8,512,896]{2,1,0:T(8,128)(2,1)}), bf16[8,512,896]{2,1,0:T(8,128)(2,1)}, u32[]{:S(2)}, u32[]{:S(2)}) async-start(bf16[8,512,896]{2,1,0:T(8,128)(2,1)} %broadcast_in_dim.10), calls=%async_computation.5 | async-start | bytes 14680064 | tf_op jit(solution)/shard_map/all_to_all | solution.py:26
  386.2 119.8 %all-gather.4.cloned.1.call-start = ((), (), s32[]{:S(2)}) async-start(), calls=%async_computation.9 | async-start | bytes 4718592 | tf_op jit(solution)/shard_map/all_gather | solution.py:166
  493.8 3.7 copy-start.20
  497.5 4.9 copy-start.2
  497.5 4.9 copy-start.9
  497.5 4.9 copy-start.12
  502.3 3.6 copy-start.23
  543.4 32.5 %all-to-all-start.7 = ((bf16[16,256,256]{1,2,0:T(8,128)(2,1)}), bf16[16,256,256]{1,2,0:T(8,128)(2,1)}, u32[]{:S(2)}, u32[]{:S(2)}) async-start(bf16[16,256,256]{1,2,0:T(8,128)(2,1)} %broadcast_in_dim.11), calls=%async_computation.7 | async-start | bytes 4194304 | tf_op jit(solution)/shard_map/all_to_all | solution.py:20
  576.0 4.0 copy-start.6
  579.9 2.0 copy-start.4
  583.5 3.6 copy-start.26
Sparse Core Ops, SparseCore 0:
  173.4 139.1 all-gather.5
  389.3 113.0 all-gather.3

commit v6 on v5

--- a/solution.py
+++ b/solution.py
@@ -25,6 +25,17 @@
     rows, cols = piece.shape
     g = lax.all_to_all(jnp.broadcast_to(piece[None], (n, rows, cols)), DP, 0, 0, tiled=False)
     return g.reshape(n * rows, cols)
+
+
+def exchange_rows(local_x, n):
+    pieces = local_x.reshape(local_x.shape[0], n, -1).transpose(1, 0, 2)
+    d = lax.axis_index(DP)
+    got = [lax.dynamic_index_in_dim(pieces, d, 0, keepdims=False)]
+    for s in range(1, n):
+        send = lax.dynamic_index_in_dim(pieces, (d + s) % n, 0, keepdims=False)
+        got.append(lax.ppermute(send, DP, [(i, (i + s) % n) for i in range(n)]))
+    got = jnp.stack(got)
+    return jnp.take(got, (d - jnp.arange(n)) % n, axis=0)
 
 
 def psum_all(x):
@@ -108,10 +119,7 @@
     out_cols = rs_cols(
         jnp.concatenate([part_tgt, part_poi], axis=0).astype(jnp.bfloat16), fs_size
     )
-    x_loc = jnp.concatenate([target_x, poison_x], 0)
-    x_rows = lax.all_to_all(
-        x_loc.reshape(-1, dp_size, model_width // dp_size).transpose(1, 0, 2), DP, 0, 0, tiled=False
-    )
+    x_rows = exchange_rows(jnp.concatenate([target_x, poison_x], 0), dp_size)
     x_rows, out_cols = lax.optimization_barrier((x_rows, out_cols))
     x_cols = lax.dynamic_slice_in_dim(jnp.concatenate([target_x, poison_x], 0), fidx * width, width, 1)
     y_cols = lax.dynamic_slice_in_dim(jnp.concatenate([target_y, poison_y], 0), fidx * width, width, 1)

time: 676 us -> 689 us (1.019)
  waiting for transfers between devices: 328 us -> 276 us
  local copies, waits for them, and re-layouts: 33.1 us -> 74.8 us
  starting transfers between devices: 32.5 us -> 48.9 us
    all_to_all x1 -> x0, waiting for transfers between devices: 44.1 us -> none  [local(): lax.all_to_all(x_loc.reshape(-1, dp_size, model_width // dp_size).transpo...]
    all_to_all x1, waiting for transfers between devices: 30.4 us -> 0.01 us  [rs_cols(): r = lax.all_to_all(r, FS, 0, 0, tiled=False)]
    ppermute x0 -> x7, waiting for transfers between devices: none -> 22.1 us  [exchange_rows(): got.append(lax.ppermute(send, DP, [(i, (i + s) % n) for i in range(n)]))]
    ppermute x0 -> x7, starting transfers between devices: none -> 20.1 us  [exchange_rows(): got.append(lax.ppermute(send, DP, [(i, (i + s) % n) for i in range(n)]))]
    another operation x0 -> x10, local copies, waits for them, and re-layouts: none -> 19.8 us
    unnamed x58 -> x71, local copies, waits for them, and re-layouts: 11.3 us -> 24.2 us
    gather x0 -> x2, local copies, waits for them, and re-layouts: none -> 9.02 us  [exchange_rows(): return jnp.take(got, (d - jnp.arange(n)) % n, axis=0)]
  transfers between devices with their start and end apart: 8 -> 14, of which waited for: 6 -> 6; matrix products, arithmetic and copies ran while one was open for 7% -> 13% of each run, Pallas kernels for 0% -> 0%
where the time goes in v6:
time: 689 us; the launch traced here: 679 us
  waiting for transfers between devices  276 us (40%)
  blocking collectives  177 us (26%)
  local copies, waits for them, and re-layouts  74.8 us (11%)
  matrix products  68.5 us (10%)
  starting transfers between devices  48.9 us (7%)
  between operations  19.7 us (3%)
  other arithmetic  14.4 us (2%)
    all_to_all x1, waiting for transfers between devices, ag_rows(): lax.all_to_all(jnp.broadcast_to(piece[None], (n, rows, cols)), DP, 0, 0,...  106 us
    all_gather x1, waiting for transfers between devices, local(): lax.all_gather(jnp.concatenate([hidden_tgt, hidden_poi], 0), DP, axis=0,...  84.1 us
    psum x10, blocking collectives, psum_all(): x = lax.psum(x, axis)  71.7 us
    all_to_all x2, blocking collectives, rs_cols(): r = lax.all_to_all(r, FS, 0, 0, tiled=False)  61.5 us
    all_to_all x1, blocking collectives, ag_cols(): lax.all_to_all(jnp.broadcast_to(piece[None], (n, rows, cols)), FS, 0, 0,...  43.3 us
    all_to_all x1, waiting for transfers between devices, local(): lax.all_to_all(error_all.reshape(-1, dp_size, rows_d).transpose(1, 0, 2),...  40.4 us
    dot_general x10, matrix products, matmul(): return jnp.dot(left, right, preferred_element_type=jnp.float32)  28.8 us
    dot_general x8, matrix products, inner_cols(): lax.dot_general(left, right, (((1,), (1,)), ((), ())), preferred_element_...  24.8 us
  transfers between devices with their start and end apart: 14, of which 6 were waited for; matrix products, arithmetic and copies ran while one was open for 13% of the time, Pallas kernels for 0%

profile of v6, /device:TPU:0, one launch (start us, length us, event | category | flops | bytes accessed | tf_op | source)
XLA Modules:
  0.0 678.6 jit_solution(14259358001804180765)
XLA Ops:
  7.2 3.6 fusion.70
  22.0 6.5 all-to-all-start
  32.5 4.7 copy.43
  37.1 3.5 constant_dynamic-slice_fusion
  58.9 4.5 collective-permute-start.4
  71.0 19.0 %collective-permute-done = bf16[384,512]{1,0:T(8,128)(2,1)} collective-permute-done((bf16[384,512]{1,0:T(8,128)(2,1)}, bf16[384,512]{1,0:T(8,128)(2,1)}, u32[]{:S(2)}, u32[]{:S(2)}) %collective-permute-start) | collective-permute-done | bytes 393248 | tf_op jit(solution)/shard_map/ppermute | solution.py:36
  94.4 4.4 collective-permute-start.6
  106.7 3.1 collective-permute-done.6
  110.6 4.4 gather_fusion
  115.0 4.7 copy.52
  119.6 3.9 broadcast_select_fusion
  127.1 43.3 %all_to_all.40 = bf16[16,384,256]{1,2,0:T(8,128)(2,1)S(1)} all-to-all(bf16[16,384,256]{1,2,0:T(8,128)(2,1)S(1)} %broadcast_in_dim.20), channel_id=1, replica_groups=mesh['z'=4,'ylo'=2,'core'=2,'x'=4,'yhi'=2] {'z','ylo','core'}, dimensions={0} | all-to-all | bytes 6291456 | tf_op jit(solution)/shard_map/all_to_all | solution.py:20
  170.4 2.9 copy.58
  173.3 7.9 %all-to-all-start.3 = ((bf16[8,384,512]{2,1,0:T(8,128)(2,1)}), bf16[8,384,512]{2,1,0:T(8,128)(2,1)}, u32[]{:S(2)}, u32[]{:S(2)}) async-start(bf16[8,384,512]{2,1,0:T(8,128)(2,1)} %bitcast.107), calls=%async_computation.3 | async-start | bytes 6291456 | tf_op jit(solution)/shard_map/all_to_all | solution.py:141
  182.3 3.3 multiply_convert_fusion.8
  190.8 40.4 %all-to-all-done.3 = bf16[8,384,512]{2,1,0:T(8,128)(2,1)} async-done(((bf16[8,384,512]{2,1,0:T(8,128)(2,1)}), bf16[8,384,512]{2,1,0:T(8,128)(2,1)}, u32[]{:S(2)}, u32[]{:S(2)}) %all-to-all-start.3) | async-done | bytes 3145760 | tf_op jit(solution)/shard_map/all_to_all | solution.py:141
  231.2 3.2 broadcast_in_dim.21
  234.3 4.7 all-to-all-start.2
  239.0 84.1 %all-gather.6.cloned.1.call-done = bf16[3072,448]{0,1:T(8,128)(2,1)} async-done(((bf16[384,448]{0,1:T(8,128)(2,1)}), bf16[3072,448]{0,1:T(8,128)(2,1)}) %all-gather.6.cloned.1.call-update) | async-done | bytes 2752528 | tf_op jit(solution)/shard_map/all_gather | solution.py:144
  325.8 3.0 convolution_bitcast_fusion
  328.7 3.9 fusion.24
  332.6 5.1 fusion.19
  337.8 2.9 fusion.16
  343.7 3.2 all-reduce.3
  346.9 5.8 all-reduce.4
  352.7 11.0 %all-reduce.1 = (f32[]{:T(128)}, f32[]{:T(128)}, f32[]{:T(128)}) all-reduce(f32[]{:T(128)} %get-tuple-element.21, f32[]{:T(128)} %get-tuple-element.22, f32[]{:T(128)} %get-tuple-element.23), channel_id=1, replica_groups=mesh['z'=4,'ylo'=2,'core'=2,'x'=4,'yhi'=2] {'z'}, use_global_device_ids=true, to_apply=%region_16.17 | all-reduce | flops 3 | bytes 24 | tf_op jit(solution)/shard_map/psum | solution.py:43
  363.7 11.0 %all-reduce = (f32[]{:T(128)}, f32[]{:T(128)}, f32[]{:T(128)}) all-reduce(f32[]{:T(128)} %get-tuple-element.12, f32[]{:T(128)} %get-tuple-element.13, f32[]{:T(128)} %get-tuple-element.14), channel_id=1, replica_groups=mesh['z'=4,'ylo'=2,'core'=2,'x'=4,'yhi'=2] {'x'}, use_global_device_ids=true, to_apply=%region_17.18 | all-reduce | flops 3 | bytes 24 | tf_op jit(solution)/shard_map/psum | solution.py:43
  374.7 7.1 %all-reduce.2 = (f32[]{:T(128)}, f32[]{:T(128)}, f32[]{:T(128)}) all-reduce(f32[]{:T(128)} %get-tuple-element.9, f32[]{:T(128)} %get-tuple-element.10, f32[]{:T(128)} %get-tuple-element.11), channel_id=1, replica_groups=mesh['z'=4,'ylo'=2,'core'=2,'x'=4,'yhi'=2] {'yhi'}, use_global_device_ids=true, to_apply=%region_18.19 | all-reduce | flops 3 | bytes 24 | tf_op jit(solution)/shard_map/psum | solution.py:43
  387.6 4.0 broadcast_in_dim.38
  391.5 5.0 all-to-all-start.4
  398.5 105.7 %all-to-all-done.4 = bf16[8,512,896]{2,1,0:T(8,128)(2,1)} async-done(((bf16[8,512,896]{2,1,0:T(8,128)(2,1)}), bf16[8,512,896]{2,1,0:T(8,128)(2,1)}, u32[]{:S(2)}, u32[]{:S(2)}) %all-to-all-start.4) | async-done | bytes 7340064 | tf_op jit(solution)/shard_map/all_to_all | solution.py:26
  504.1 3.7 fusion.29
  507.9 4.8 fusion.32
  512.7 3.6 fusion.48
  516.3 4.8 fusion
  521.3 31.0 %all_to_all.41 = bf16[16,256,256]{2,1,0:T(8,128)(2,1)S(1)} all-to-all(bf16[16,256,256]{2,1,0:T(8,128)(2,1)S(1)} %bitcast.113), channel_id=1, replica_groups=mesh['z'=4,'ylo'=2,'core'=2,'x'=4,'yhi'=2] {'z','ylo','core'}, dimensions={0} | all-to-all | bytes 4194304 | tf_op jit(solution)/shard_map/all_to_all | solution.py:14
  554.2 4.7 all-to-all-start.6
  558.9 4.5 fusion.71
  563.4 23.3 %all-to-all-done.6 = bf16[16,256,256]{1,2,0:T(8,128)(2,1)} async-done(((bf16[16,256,256]{1,2,0:T(8,128)(2,1)}), bf16[16,256,256]{1,2,0:T(8,128)(2,1)}, u32[]{:S(2)}, u32[]{:S(2)}) %all-to-all-start.6) | async-done | bytes 2097184 | tf_op jit(solution)/shard_map/all_to_all | solution.py:20
  586.7 4.0 convolution_add_fusion.4
  594.3 3.6 convolution_add_fusion.1
  597.9 4.8 fusion.1
  602.9 30.5 %all_to_all.42 = bf16[16,256,256]{2,1,0:T(8,128)(2,1)S(1)} all-to-all(bf16[16,256,256]{2,1,0:T(8,128)(2,1)S(1)} %bitcast.114), channel_id=1, replica_groups=mesh['z'=4,'ylo'=2,'core'=2,'x'=4,'yhi'=2] {'z','ylo','core'}, dimensions={0} | all-to-all | bytes 4194304 | tf_op jit(solution)/shard_map/all_to_all | solution.py:14
  634.4 3.1 psum.155
  637.4 5.5 psum.156
  643.0 9.2 %psum.157 = f32[]{:T(128)} all-reduce(f32[]{:T(128)} %psum.156), channel_id=1, replica_groups=mesh['z'=4,'ylo'=2,'core'=2,'x'=4,'yhi'=2] {'z'}, use_global_device_ids=true, to_apply=%region_24.25 | all-reduce | flops 1 | bytes 8 | tf_op jit(solution)/shard_map/psum | solution.py:43
  652.9 8.8 %psum.158 = f32[]{:T(128)} all-reduce(f32[]{:T(128)} %psum.157), channel_id=1, replica_groups=mesh['z'=4,'ylo'=2,'core'=2,'x'=4,'yhi'=2] {'x'}, use_global_device_ids=true, to_apply=%region_25.26 | all-reduce | flops 1 | bytes 8 | tf_op jit(solution)/shard_map/psum | solution.py:43
  661.7 7.0 %psum.159 = f32[]{:T(128)} all-reduce(f32[]{:T(128)} %psum.158), channel_id=1, replica_groups=mesh['z'=4,'ylo'=2,'core'=2,'x'=4,'yhi'=2] {'yhi'}, use_global_device_ids=true, to_apply=%region_26.27 | all-reduce | flops 1 | bytes 8 | tf_op jit(solution)/shard_map/psum | solution.py:43
  (136 shorter events, 82.4 us)
Async XLA Ops:
  7.2 3.6 copy-start.5
  10.8 2.9 copy-start.27
  10.8 2.9 copy-start.3
  10.8 3.0 copy-start.10
  13.9 3.7 copy-start.7
  13.9 1.8 copy-start.18
  15.7 2.0 copy-start
  17.6 163.6 %copy-start.24 = (bf16[256,448]{0,1:T(8,128)(2,1)}, bf16[256,448]{0,1:T(8,128)(2,1)S(1)}, u32[]{:S(2)}) copy-start(bf16[256,448]{0,1:T(8,128)(2,1)S(1)} %get-tuple-element.36) | copy-start | bytes 688132
  22.0 101.6 %all-to-all-start = ((bf16[16,384,256]{2,1,0:T(8,128)(2,1)}), bf16[16,384,256]{2,1,0:T(8,128)(2,1)S(1)}, u32[]{:S(2)}, u32[]{:S(2)}) async-start(bf16[16,384,256]{2,1,0:T(8,128)(2,1)} %maximum_bitcast_fusion), calls=%async_computation | async-start | bytes 6291456 | tf_op jit(solution)/shard_map/all_to_all | solution.py:14
  28.6 2.4 copy-start.19
  42.6 47.4 %collective-permute-start = (bf16[384,512]{1,0:T(8,128)(2,1)}, bf16[384,512]{1,0:T(8,128)(2,1)}, u32[]{:S(2)}, u32[]{:S(2)}) collective-permute-start(bf16[384,512]{1,0:T(8,128)(2,1)} %bitcast.127), channel_id=1, source_target_pairs={{0,1},{1,2},{2,3},{3,4},{4,5},{5,6},{6,7},{7,0},{8,9},{9,10},{10,1... | collective-permute-start | bytes 1179656 | tf_op jit(solution)/shard_map/ppermute | solution.py:36
  47.4 47.0 %collective-permute-start.1 = (bf16[384,512]{1,0:T(8,128)(2,1)}, bf16[384,512]{1,0:T(8,128)(2,1)}, u32[]{:S(2)}, u32[]{:S(2)}) collective-permute-start(bf16[384,512]{1,0:T(8,128)(2,1)} %bitcast.126), channel_id=1, source_target_pairs={{0,2},{1,3},{2,4},{3,5},{4,6},{5,7},{6,0},{7,1},{8,10},{9,11},{10,... | collective-permute-start | bytes 1179656 | tf_op jit(solution)/shard_map/ppermute | solution.py:36
  50.9 49.7 %collective-permute-start.2 = (bf16[384,512]{1,0:T(8,128)(2,1)}, bf16[384,512]{1,0:T(8,128)(2,1)}, u32[]{:S(2)}, u32[]{:S(2)}) collective-permute-start(bf16[384,512]{1,0:T(8,128)(2,1)} %bitcast.125), channel_id=1, source_target_pairs={{0,3},{1,4},{2,5},{3,6},{4,7},{5,0},{6,1},{7,2},{8,11},{9,12},{10,... | collective-permute-start | bytes 1179656 | tf_op jit(solution)/shard_map/ppermute | solution.py:36
  55.0 47.4 %collective-permute-start.3 = (bf16[384,512]{1,0:T(8,128)(2,1)}, bf16[384,512]{1,0:T(8,128)(2,1)}, u32[]{:S(2)}, u32[]{:S(2)}) collective-permute-start(bf16[384,512]{1,0:T(8,128)(2,1)} %bitcast.124), channel_id=1, source_target_pairs={{0,4},{1,5},{2,6},{3,7},{4,0},{5,1},{6,2},{7,3},{8,12},{9,13},{10,... | collective-permute-start | bytes 1179656 | tf_op jit(solution)/shard_map/ppermute | solution.py:36
  58.9 45.2 %collective-permute-start.4 = (bf16[384,512]{1,0:T(8,128)(2,1)}, bf16[384,512]{1,0:T(8,128)(2,1)}, u32[]{:S(2)}, u32[]{:S(2)}) collective-permute-start(bf16[384,512]{1,0:T(8,128)(2,1)} %bitcast.123), channel_id=1, source_target_pairs={{0,5},{1,6},{2,7},{3,0},{4,1},{5,2},{6,3},{7,4},{8,13},{9,14},{10,... | collective-permute-start | bytes 1179656 | tf_op jit(solution)/shard_map/ppermute | solution.py:36
  90.0 15.9 %collective-permute-start.5 = (bf16[384,512]{1,0:T(8,128)(2,1)}, bf16[384,512]{1,0:T(8,128)(2,1)S(1)}, u32[]{:S(2)}, u32[]{:S(2)}) collective-permute-start(bf16[384,512]{1,0:T(8,128)(2,1)} %bitcast.129), channel_id=1, source_target_pairs={{0,6},{1,7},{2,0},{3,1},{4,2},{5,3},{6,4},{7,5},{8,14},{9,15},{10,... | collective-permute-start | bytes 1179656 | tf_op jit(solution)/shard_map/ppermute | solution.py:36
  94.4 15.4 %collective-permute-start.6 = (bf16[384,512]{1,0:T(8,128)(2,1)}, bf16[384,512]{1,0:T(8,128)(2,1)S(1)}, u32[]{:S(2)}, u32[]{:S(2)}) collective-permute-start(bf16[384,512]{1,0:T(8,128)(2,1)} %bitcast.128), channel_id=1, source_target_pairs={{0,7},{1,0},{2,1},{3,2},{4,3},{5,4},{6,5},{7,6},{8,15},{9,8},{10,9... | collective-permute-start | bytes 1179656 | tf_op jit(solution)/shard_map/ppermute | solution.py:36
  123.6 0.7 copy-start.30
  123.6 1.6 copy-start.23
  123.6 1.9 copy-start.26
  173.3 57.9 %all-to-all-start.3 = ((bf16[8,384,512]{2,1,0:T(8,128)(2,1)}), bf16[8,384,512]{2,1,0:T(8,128)(2,1)}, u32[]{:S(2)}, u32[]{:S(2)}) async-start(bf16[8,384,512]{2,1,0:T(8,128)(2,1)} %bitcast.107), calls=%async_computation.3 | async-start | bytes 6291456 | tf_op jit(solution)/shard_map/all_to_all | solution.py:141
  181.2 142.0 %all-gather.6.cloned.1.call-start = ((), (), s32[]{:S(2)}) async-start(), calls=%async_computation.9 | async-start | bytes 3096576 | tf_op jit(solution)/shard_map/all_gather | solution.py:144
  182.2 3.6 copy-start.11
  185.6 2.8 copy-start.1
  185.6 2.9 copy-start.8
  185.8 3.9 copy-start.22
  189.7 0.7 copy-start.28
  234.3 98.3 %all-to-all-start.2 = ((bf16[8,384,896]{2,1,0:T(8,128)(2,1)}), bf16[8,384,896]{2,1,0:T(8,128)(2,1)}, u32[]{:S(2)}, u32[]{:S(2)}) async-start(bf16[8,384,896]{2,1,0:T(8,128)(2,1)} %broadcast_in_dim.21), calls=%async_computation.2 | async-start | bytes 11010048 | tf_op jit(solution)/shard_map/all_to_all | solution.py:152
  332.6 5.2 copy-start.17
  337.8 4.2 copy-start.15
  337.8 4.2 copy-start.16
  340.7 1.3 copy-start.13
  386.4 1.1 copy-start.14
  391.5 112.6 %copy-start.20 = (bf16[256,4096]{1,0:T(8,128)(2,1)S(1)}, bf16[256,4096]{1,0:T(8,128)(2,1)}, u32[]{:S(2)}) copy-start(bf16[256,4096]{1,0:T(8,128)(2,1)} %param.9) | copy-start | bytes 6291460
  391.5 112.6 %all-to-all-start.4 = ((bf16[8,512,896]{2,1,0:T(8,128)(2,1)}), bf16[8,512,896]{2,1,0:T(8,128)(2,1)}, u32[]{:S(2)}, u32[]{:S(2)}) async-start(bf16[8,512,896]{2,1,0:T(8,128)(2,1)} %broadcast_in_dim.38), calls=%async_computation.4 | async-start | bytes 14680064 | tf_op jit(solution)/shard_map/all_to_all | solution.py:26
  396.5 119.7 %all-gather.4.cloned.1.call-start = ((), (), s32[]{:S(2)}) async-start(), calls=%async_computation.8 | async-start | bytes 4718592 | tf_op jit(solution)/shard_map/all_gather | solution.py:174
  504.1 3.7 copy-start.21
  507.8 4.9 copy-start.2
  507.8 4.8 copy-start.9
  507.8 4.8 copy-start.12
  512.7 3.6 copy-start.25
  554.2 32.5 %all-to-all-start.6 = ((bf16[16,256,256]{1,2,0:T(8,128)(2,1)}), bf16[16,256,256]{1,2,0:T(8,128)(2,1)}, u32[]{:S(2)}, u32[]{:S(2)}) async-start(bf16[16,256,256]{1,2,0:T(8,128)(2,1)} %broadcast_in_dim.39), calls=%async_computation.6 | async-start | bytes 4194304 | tf_op jit(solution)/shard_map/all_to_all | solution.py:20
  586.7 4.0 copy-start.6
  590.7 2.0 copy-start.4
  594.2 3.6 copy-start.29
Sparse Core Ops, SparseCore 0:
  184.2 138.9 all-gather.5
  399.7 113.0 all-gather.3

commit v7 on v5

--- a/solution.py
+++ b/solution.py
@@ -105,14 +105,14 @@
     n_tgt = target_x.shape[0]
     fidx = lax.axis_index(FS)
     width = model_width // fs_size
-    out_cols = rs_cols(
-        jnp.concatenate([part_tgt, part_poi], axis=0).astype(jnp.bfloat16), fs_size
-    )
     x_loc = jnp.concatenate([target_x, poison_x], 0)
     x_rows = lax.all_to_all(
         x_loc.reshape(-1, dp_size, model_width // dp_size).transpose(1, 0, 2), DP, 0, 0, tiled=False
     )
-    x_rows, out_cols = lax.optimization_barrier((x_rows, out_cols))
+    x_rows, part_tgt, part_poi = lax.optimization_barrier((x_rows, part_tgt, part_poi))
+    out_cols = rs_cols(
+        jnp.concatenate([part_tgt, part_poi], axis=0).astype(jnp.bfloat16), fs_size
+    )
     x_cols = lax.dynamic_slice_in_dim(jnp.concatenate([target_x, poison_x], 0), fidx * width, width, 1)
     y_cols = lax.dynamic_slice_in_dim(jnp.concatenate([target_y, poison_y], 0), fidx * width, width, 1)
     scale_rows = jnp.concatenate(

time: 676 us -> 670 us (level)
    all_to_all x1, waiting for transfers between devices: 44.1 us -> 33.6 us  [local(): lax.all_to_all(x_loc.reshape(-1, dp_size, model_width // dp_size).transpo...]
    all_to_all x1, waiting for transfers between devices: 30.4 us -> 39 us  [rs_cols(): r = lax.all_to_all(r, FS, 0, 0, tiled=False)]
where the time goes in v7:
time: 670 us; the launch traced here: 662 us
  waiting for transfers between devices  326 us (49%)
  blocking collectives  175 us (26%)
  matrix products  66.6 us (10%)
  local copies, waits for them, and re-layouts  32.6 us (5%)
  starting transfers between devices  32.2 us (5%)
  between operations  19.4 us (3%)
  other arithmetic  10.6 us (2%)
    all_to_all x1, waiting for transfers between devices, ag_rows(): lax.all_to_all(jnp.broadcast_to(piece[None], (n, rows, cols)), DP, 0, 0,...  105 us
    all_gather x1, waiting for transfers between devices, local(): lax.all_gather(jnp.concatenate([hidden_tgt, hidden_poi], 0), DP, axis=0,...  84.2 us
    psum x10, blocking collectives, psum_all(): x = lax.psum(x, axis)  71.9 us
    all_to_all x2, blocking collectives, rs_cols(): r = lax.all_to_all(r, FS, 0, 0, tiled=False)  61.1 us
    all_to_all x1, blocking collectives, ag_cols(): lax.all_to_all(jnp.broadcast_to(piece[None], (n, rows, cols)), FS, 0, 0,...  41.8 us
    all_to_all x1, waiting for transfers between devices, local(): lax.all_to_all(error_all.reshape(-1, dp_size, rows_d).transpose(1, 0, 2),...  40.2 us
    all_to_all x1, waiting for transfers between devices, rs_cols(): r = lax.all_to_all(r, FS, 0, 0, tiled=False)  39 us
    all_to_all x1, waiting for transfers between devices, local(): lax.all_to_all(x_loc.reshape(-1, dp_size, model_width // dp_size).transpo...  33.6 us
  transfers between devices with their start and end apart: 8, of which 6 were waited for; matrix products, arithmetic and copies ran while one was open for 7% of the time, Pallas kernels for 0%

profile of v7, /device:TPU:0, one launch (start us, length us, event | category | flops | bytes accessed | tf_op | source)
XLA Modules:
  0.0 662.1 jit_solution(991830739365773832)
XLA Ops:
  9.2 3.3 copy.24
  12.5 7.2 %all-to-all-start = ((bf16[8,384,512]{1,2,0:T(8,128)(2,1)}), bf16[8,384,512]{1,2,0:T(8,128)(2,1)}, u32[]{:S(2)}, u32[]{:S(2)}) async-start(bf16[8,384,512]{1,2,0:T(8,128)(2,1)} %bitcast.1), calls=%async_computation | async-start | bytes 6291456 | tf_op jit(solution)/shard_map/all_to_all | solution.py:109
  19.7 3.3 fusion.67
  28.3 2.0 multiply_convert_fusion.3
  31.6 33.6 %all-to-all-done = bf16[8,384,512]{1,2,0:T(8,128)(2,1)} async-done(((bf16[8,384,512]{1,2,0:T(8,128)(2,1)}), bf16[8,384,512]{1,2,0:T(8,128)(2,1)}, u32[]{:S(2)}, u32[]{:S(2)}) %all-to-all-start) | async-done | bytes 3145760 | tf_op jit(solution)/shard_map/all_to_all | solution.py:109
  65.5 2.0 maximum_bitcast_fusion
  67.5 5.5 all-to-all-start.1
  73.1 39.0 %all-to-all-done.1 = bf16[16,384,256]{2,1,0:T(8,128)(2,1)S(1)} async-done(((bf16[16,384,256]{2,1,0:T(8,128)(2,1)}), bf16[16,384,256]{2,1,0:T(8,128)(2,1)S(1)}, u32[]{:S(2)}, u32[]{:S(2)}) %all-to-all-start.1) | async-done | bytes 3145760 | tf_op jit(solution)/shard_map/all_to_all | solution.py:14
  115.6 41.8 %all_to_all.45 = bf16[16,384,256]{1,2,0:T(8,128)(2,1)S(1)} all-to-all(bf16[16,384,256]{1,2,0:T(8,128)(2,1)S(1)} %broadcast_in_dim.8), channel_id=1, replica_groups=mesh['z'=4,'ylo'=2,'core'=2,'x'=4,'yhi'=2] {'z','ylo','core'}, dimensions={0} | all-to-all | bytes 6291456 | tf_op jit(solution)/shard_map/all_to_all | solution.py:20
  157.4 2.9 copy.29
  160.3 4.7 all-to-all-start.4
  166.2 3.3 multiply_convert_fusion.8
  169.7 2.6 copy-done.1
  174.7 40.2 %all-to-all-done.4 = bf16[8,384,512]{2,1,0:T(8,128)(2,1)} async-done(((bf16[8,384,512]{2,1,0:T(8,128)(2,1)}), bf16[8,384,512]{2,1,0:T(8,128)(2,1)}, u32[]{:S(2)}, u32[]{:S(2)}) %all-to-all-start.4) | async-done | bytes 3145760 | tf_op jit(solution)/shard_map/all_to_all | solution.py:133
  214.9 3.2 broadcast_in_dim.9
  218.1 4.7 all-to-all-start.3
  222.8 84.2 %all-gather.6.cloned.1.call-done = bf16[3072,448]{0,1:T(8,128)(2,1)} async-done(((bf16[384,448]{0,1:T(8,128)(2,1)}), bf16[3072,448]{0,1:T(8,128)(2,1)}) %all-gather.6.cloned.1.call-update) | async-done | bytes 2752528 | tf_op jit(solution)/shard_map/all_gather | solution.py:136
  307.1 2.4 copy.47
  309.7 3.0 convolution_bitcast_fusion
  312.6 3.9 fusion.24
  316.5 5.0 fusion.19
  321.5 3.2 fusion.16
  327.7 3.1 all-reduce.3
  330.9 5.6 all-reduce.4
  336.5 11.2 %all-reduce.1 = (f32[]{:T(128)}, f32[]{:T(128)}, f32[]{:T(128)}) all-reduce(f32[]{:T(128)} %get-tuple-element.23, f32[]{:T(128)} %get-tuple-element.24, f32[]{:T(128)} %get-tuple-element.25), channel_id=1, replica_groups=mesh['z'=4,'ylo'=2,'core'=2,'x'=4,'yhi'=2] {'z'}, use_global_device_ids=true, to_apply=%region_16.0 | all-reduce | flops 3 | bytes 24 | tf_op jit(solution)/shard_map/psum | solution.py:32
  347.7 11.2 %all-reduce = (f32[]{:T(128)}, f32[]{:T(128)}, f32[]{:T(128)}) all-reduce(f32[]{:T(128)} %get-tuple-element.14, f32[]{:T(128)} %get-tuple-element.15, f32[]{:T(128)} %get-tuple-element.16), channel_id=1, replica_groups=mesh['z'=4,'ylo'=2,'core'=2,'x'=4,'yhi'=2] {'x'}, use_global_device_ids=true, to_apply=%region_17.0 | all-reduce | flops 3 | bytes 24 | tf_op jit(solution)/shard_map/psum | solution.py:32
  358.8 7.1 %all-reduce.2 = (f32[]{:T(128)}, f32[]{:T(128)}, f32[]{:T(128)}) all-reduce(f32[]{:T(128)} %get-tuple-element.11, f32[]{:T(128)} %get-tuple-element.12, f32[]{:T(128)} %get-tuple-element.13), channel_id=1, replica_groups=mesh['z'=4,'ylo'=2,'core'=2,'x'=4,'yhi'=2] {'yhi'}, use_global_device_ids=true, to_apply=%region_18.0 | all-reduce | flops 3 | bytes 24 | tf_op jit(solution)/shard_map/psum | solution.py:32
  367.9 2.5 add_convert_fusion
  371.6 3.9 broadcast_in_dim.10
  375.6 5.0 all-to-all-start.5
  382.7 105.4 %all-to-all-done.5 = bf16[8,512,896]{2,1,0:T(8,128)(2,1)} async-done(((bf16[8,512,896]{2,1,0:T(8,128)(2,1)}), bf16[8,512,896]{2,1,0:T(8,128)(2,1)}, u32[]{:S(2)}, u32[]{:S(2)}) %all-to-all-start.5) | async-done | bytes 7340064 | tf_op jit(solution)/shard_map/all_to_all | solution.py:26
  488.2 3.7 fusion.29
  491.9 4.8 fusion.32
  496.8 3.6 fusion.48
  500.3 4.8 fusion
  505.3 30.6 %all_to_all.46 = bf16[16,256,256]{2,1,0:T(8,128)(2,1)S(1)} all-to-all(bf16[16,256,256]{2,1,0:T(8,128)(2,1)S(1)} %bitcast.89), channel_id=1, replica_groups=mesh['z'=4,'ylo'=2,'core'=2,'x'=4,'yhi'=2] {'z','ylo','core'}, dimensions={0} | all-to-all | bytes 4194304 | tf_op jit(solution)/shard_map/all_to_all | solution.py:14
  537.8 4.7 all-to-all-start.7
  542.5 4.5 fusion.70
  547.0 23.3 %all-to-all-done.7 = bf16[16,256,256]{1,2,0:T(8,128)(2,1)} async-done(((bf16[16,256,256]{1,2,0:T(8,128)(2,1)}), bf16[16,256,256]{1,2,0:T(8,128)(2,1)}, u32[]{:S(2)}, u32[]{:S(2)}) %all-to-all-start.7) | async-done | bytes 2097184 | tf_op jit(solution)/shard_map/all_to_all | solution.py:20
  570.4 4.0 convolution_add_fusion.4
  577.9 3.6 convolution_add_fusion.1
  581.5 4.8 fusion.1
  586.5 30.5 %all_to_all.47 = bf16[16,256,256]{2,1,0:T(8,128)(2,1)S(1)} all-to-all(bf16[16,256,256]{2,1,0:T(8,128)(2,1)S(1)} %bitcast.90), channel_id=1, replica_groups=mesh['z'=4,'ylo'=2,'core'=2,'x'=4,'yhi'=2] {'z','ylo','core'}, dimensions={0} | all-to-all | bytes 4194304 | tf_op jit(solution)/shard_map/all_to_all | solution.py:14
  618.0 3.1 psum.155
  621.1 5.5 psum.156
  626.6 9.2 %psum.157 = f32[]{:T(128)} all-reduce(f32[]{:T(128)} %psum.156), channel_id=1, replica_groups=mesh['z'=4,'ylo'=2,'core'=2,'x'=4,'yhi'=2] {'z'}, use_global_device_ids=true, to_apply=%region_24.0 | all-reduce | flops 1 | bytes 8 | tf_op jit(solution)/shard_map/psum | solution.py:32
  636.4 8.9 %psum.158 = f32[]{:T(128)} all-reduce(f32[]{:T(128)} %psum.157), channel_id=1, replica_groups=mesh['z'=4,'ylo'=2,'core'=2,'x'=4,'yhi'=2] {'x'}, use_global_device_ids=true, to_apply=%region_25.0 | all-reduce | flops 1 | bytes 8 | tf_op jit(solution)/shard_map/psum | solution.py:32
  645.2 7.0 %psum.159 = f32[]{:T(128)} all-reduce(f32[]{:T(128)} %psum.158), channel_id=1, replica_groups=mesh['z'=4,'ylo'=2,'core'=2,'x'=4,'yhi'=2] {'yhi'}, use_global_device_ids=true, to_apply=%region_26.0 | all-reduce | flops 1 | bytes 8 | tf_op jit(solution)/shard_map/psum | solution.py:32
  (101 shorter events, 30.2 us)
Async XLA Ops:
  7.2 1.9 copy-start.18
  9.2 3.3 copy-start.14
  12.5 7.2 %copy-start.10 = (bf16[128,4096]{1,0:T(8,128)(2,1)S(1)}, bf16[128,4096]{1,0:T(8,128)(2,1)}, u32[]{:S(2)}) copy-start(bf16[128,4096]{1,0:T(8,128)(2,1)} %param.7) | copy-start | bytes 3145732
  12.5 52.7 %all-to-all-start = ((bf16[8,384,512]{1,2,0:T(8,128)(2,1)}), bf16[8,384,512]{1,2,0:T(8,128)(2,1)}, u32[]{:S(2)}, u32[]{:S(2)}) async-start(bf16[8,384,512]{1,2,0:T(8,128)(2,1)} %bitcast.1), calls=%async_computation | async-start | bytes 6291456 | tf_op jit(solution)/shard_map/all_to_all | solution.py:109
  19.7 3.3 copy-start.3
  23.0 2.9 copy-start.27
  23.0 2.2 copy-start
  23.0 2.9 copy-start.19
  24.8 2.3 copy-start.5
  28.3 2.0 copy-start.7
  30.3 134.9 %copy-start.24 = (bf16[256,448]{0,1:T(8,128)(2,1)}, bf16[256,448]{0,1:T(8,128)(2,1)S(1)}, u32[]{:S(2)}) copy-start(bf16[256,448]{0,1:T(8,128)(2,1)S(1)} %get-tuple-element.32) | copy-start | bytes 688132
  67.5 44.6 %all-to-all-start.1 = ((bf16[16,384,256]{2,1,0:T(8,128)(2,1)}), bf16[16,384,256]{2,1,0:T(8,128)(2,1)S(1)}, u32[]{:S(2)}, u32[]{:S(2)}) async-start(bf16[16,384,256]{2,1,0:T(8,128)(2,1)} %maximum_bitcast_fusion), calls=%async_computation.1 | async-start | bytes 6291456 | tf_op jit(solution)/shard_map/all_to_all | solution.py:14
  73.1 39.5 %copy-start.30 = (f32[384]{0:T(512)S(1)}, f32[384]{0:T(512)}, u32[]{:S(2)}) copy-start(f32[384]{0:T(512)} %constant.43.clone.1) | copy-start | bytes 4612
  112.1 1.6 copy-start.23
  112.1 1.9 copy-start.26
  160.3 54.7 %all-to-all-start.4 = ((bf16[8,384,512]{2,1,0:T(8,128)(2,1)}), bf16[8,384,512]{2,1,0:T(8,128)(2,1)}, u32[]{:S(2)}, u32[]{:S(2)}) async-start(bf16[8,384,512]{2,1,0:T(8,128)(2,1)} %bitcast.84), calls=%async_computation.4 | async-start | bytes 6291456 | tf_op jit(solution)/shard_map/all_to_all | solution.py:133
  165.0 142.1 %all-gather.6.cloned.1.call-start = ((), (), s32[]{:S(2)}) async-start(), calls=%async_computation.10 | async-start | bytes 3096576 | tf_op jit(solution)/shard_map/all_gather | solution.py:136
  166.2 3.6 copy-start.11
  169.5 2.8 copy-start.1
  169.5 2.9 copy-start.8
  169.7 3.9 copy-start.22
  173.6 0.7 copy-start.28
  218.1 98.4 %all-to-all-start.3 = ((bf16[8,384,896]{2,1,0:T(8,128)(2,1)}), bf16[8,384,896]{2,1,0:T(8,128)(2,1)}, u32[]{:S(2)}, u32[]{:S(2)}) async-start(bf16[8,384,896]{2,1,0:T(8,128)(2,1)} %broadcast_in_dim.9), calls=%async_computation.3 | async-start | bytes 11010048 | tf_op jit(solution)/shard_map/all_to_all | solution.py:144
  321.5 4.5 copy-start.16
  321.5 4.5 copy-start.17
  324.7 1.2 copy-start.13
  370.4 1.1 copy-start.15
  375.6 112.6 %copy-start.20 = (bf16[256,4096]{1,0:T(8,128)(2,1)S(1)}, bf16[256,4096]{1,0:T(8,128)(2,1)}, u32[]{:S(2)}) copy-start(bf16[256,4096]{1,0:T(8,128)(2,1)} %param.9) | copy-start | bytes 6291460
  375.6 112.6 %all-to-all-start.5 = ((bf16[8,512,896]{2,1,0:T(8,128)(2,1)}), bf16[8,512,896]{2,1,0:T(8,128)(2,1)}, u32[]{:S(2)}, u32[]{:S(2)}) async-start(bf16[8,512,896]{2,1,0:T(8,128)(2,1)} %broadcast_in_dim.10), calls=%async_computation.5 | async-start | bytes 14680064 | tf_op jit(solution)/shard_map/all_to_all | solution.py:26
  380.6 119.8 %all-gather.4.cloned.1.call-start = ((), (), s32[]{:S(2)}) async-start(), calls=%async_computation.9 | async-start | bytes 4718592 | tf_op jit(solution)/shard_map/all_gather | solution.py:166
  488.2 3.7 copy-start.21
  491.9 4.9 copy-start.2
  491.9 4.8 copy-start.9
  491.9 4.8 copy-start.12
  496.7 3.6 copy-start.25
  537.8 32.5 %all-to-all-start.7 = ((bf16[16,256,256]{1,2,0:T(8,128)(2,1)}), bf16[16,256,256]{1,2,0:T(8,128)(2,1)}, u32[]{:S(2)}, u32[]{:S(2)}) async-start(bf16[16,256,256]{1,2,0:T(8,128)(2,1)} %broadcast_in_dim.11), calls=%async_computation.7 | async-start | bytes 4194304 | tf_op jit(solution)/shard_map/all_to_all | solution.py:20
  570.4 4.0 copy-start.6
  574.4 2.0 copy-start.4
  577.9 3.6 copy-start.29
Sparse Core Ops, SparseCore 0:
  168.0 139.0 all-gather.5
  383.7 113.0 all-gather.3

commit v8 on v7

--- a/solution.py
+++ b/solution.py
@@ -130,10 +130,14 @@
     )
     n_poi = poison_x.shape[0]
     rows_d = model_width // dp_size
-    e_rows = lax.all_to_all(
-        error_all.reshape(-1, dp_size, rows_d).transpose(1, 0, 2), DP, 0, 0, tiled=False
-    )
-    h_all = lax.all_gather(jnp.concatenate([hidden_tgt, hidden_poi], 0), DP, axis=0, tiled=False)
+    joint_dn = lax.psum_scatter(
+        jnp.concatenate(
+            [inner_rows(error_tgt, hidden_tgt), inner_rows(error_poi, hidden_poi)], axis=1
+        ).astype(jnp.bfloat16),
+        DP,
+        scatter_dimension=0,
+        tiled=True,
+    ).astype(jnp.float32)
     gu_loc = jnp.concatenate(
         [
             jnp.concatenate([gback_tgt, uback_tgt], 1),
@@ -144,15 +148,15 @@
     gu_all = lax.all_to_all(
         jnp.broadcast_to(gu_loc[None], (dp_size,) + gu_loc.shape), DP, 0, 0, tiled=False
     )
-
-    def block_grad(xr, er, ga, ha):
-        dims = (((0, 1), (0, 1)), ((), ()))
-        gu = lax.dot_general(xr, ga, dims, preferred_element_type=jnp.float32)
-        dn = lax.dot_general(er, ha, dims, preferred_element_type=jnp.float32)
-        return jnp.concatenate([gu, dn], 1)
-
-    grad_tgt = block_grad(x_rows[:, :n_tgt], e_rows[:, :n_tgt], gu_all[:, :n_tgt], h_all[:, :n_tgt])
-    grad_poi = block_grad(x_rows[:, n_tgt:], e_rows[:, n_tgt:], gu_all[:, n_tgt:], h_all[:, n_tgt:])
+    dims = (((0, 1), (0, 1)), ((), ()))
+    gu_tgt_blk = lax.dot_general(
+        x_rows[:, :n_tgt], gu_all[:, :n_tgt], dims, preferred_element_type=jnp.float32
+    )
+    gu_poi_blk = lax.dot_general(
+        x_rows[:, n_tgt:], gu_all[:, n_tgt:], dims, preferred_element_type=jnp.float32
+    )
+    grad_tgt = jnp.concatenate([gu_tgt_blk, joint_dn[:, :hidden_width]], 1)
+    grad_poi = jnp.concatenate([gu_poi_blk, joint_dn[:, hidden_width:]], 1)
     norm_tt, norm_pp, cross_tp = psum_all(
         (jnp.sum(grad_tgt * grad_tgt), jnp.sum(grad_poi * grad_poi), jnp.sum(grad_tgt * grad_poi))
     )

time: 670 us -> 684 us (1.021)
  blocking collectives: 175 us -> 265 us
  waiting for transfers between devices: 326 us -> 249 us
  other arithmetic: 10.6 us -> 20.8 us
  starting transfers between devices: 32.2 us -> 22.7 us
    all_to_all x0 -> x1, blocking collectives: none -> 91.2 us  [local(): lax.all_to_all(jnp.broadcast_to(gu_loc[None], (dp_size,) + gu_loc.shape),...]
    all_gather x1 -> x0, waiting for transfers between devices: 84.2 us -> none  [local(): lax.all_gather(jnp.concatenate([hidden_tgt, hidden_poi], 0), DP, axis=0,...]
    reduce_scatter x0 -> x1, waiting for transfers between devices: none -> 48.4 us  [local(): lax.psum_scatter(jnp.concatenate([inner_rows(error_tgt, hidden_tgt), inne...]
    all_to_all x2 -> x0, waiting for transfers between devices: 40.2 us -> none  [the longest x1 40.2 us: local(): lax.all_to_all(error_all.reshape(-1, dp_size, rows_d).transpose(1, 0, 2),...]
    all_to_all x2 -> x0, starting transfers between devices: 9.37 us -> none  [the longest x1 4.69 us: local(): lax.all_to_all(jnp.broadcast_to(gu_loc[None], (dp_size,) + gu_loc.shape),...]
  transfers between devices with their start and end apart: 8 -> 6, of which waited for: 6 -> 5; matrix products, arithmetic and copies ran while one was open for 7% -> 7% of each run, Pallas kernels for 0% -> 0%
where the time goes in v8:
time: 684 us; the launch traced here: 676 us
  blocking collectives  265 us (39%)
  waiting for transfers between devices  249 us (36%)
  matrix products  67.2 us (10%)
  local copies, waits for them, and re-layouts  31.8 us (5%)
  starting transfers between devices  22.7 us (3%)
  other arithmetic  20.8 us (3%)
  between operations  19.5 us (3%)
    all_to_all x1, waiting for transfers between devices, ag_rows(): lax.all_to_all(jnp.broadcast_to(piece[None], (n, rows, cols)), DP, 0, 0,...  105 us
    all_to_all x1, blocking collectives, local(): lax.all_to_all(jnp.broadcast_to(gu_loc[None], (dp_size,) + gu_loc.shape),...  91.2 us
    psum x10, blocking collectives, psum_all(): x = lax.psum(x, axis)  71.1 us
    all_to_all x2, blocking collectives, rs_cols(): r = lax.all_to_all(r, FS, 0, 0, tiled=False)  61.1 us
    reduce_scatter x1, waiting for transfers between devices, local(): lax.psum_scatter(jnp.concatenate([inner_rows(error_tgt, hidden_tgt), inne...  48.4 us
    all_to_all x1, blocking collectives, ag_cols(): lax.all_to_all(jnp.broadcast_to(piece[None], (n, rows, cols)), FS, 0, 0,...  42 us
    all_to_all x1, waiting for transfers between devices, rs_cols(): r = lax.all_to_all(r, FS, 0, 0, tiled=False)  39 us
    all_to_all x1, waiting for transfers between devices, local(): lax.all_to_all(x_loc.reshape(-1, dp_size, model_width // dp_size).transpo...  33.1 us
  transfers between devices with their start and end apart: 6, of which 5 were waited for; matrix products, arithmetic and copies ran while one was open for 7% of the time, Pallas kernels for 0%

profile of v8, /device:TPU:0, one launch (start us, length us, event | category | flops | bytes accessed | tf_op | source)
XLA Modules:
  0.0 675.9 jit_solution(11750267838036126511)
XLA Ops:
  11.9 2.8 copy.29
  14.7 7.2 %all-to-all-start = ((bf16[8,384,512]{1,2,0:T(8,128)(2,1)}), bf16[8,384,512]{1,2,0:T(8,128)(2,1)}, u32[]{:S(2)}, u32[]{:S(2)}) async-start(bf16[8,384,512]{1,2,0:T(8,128)(2,1)} %bitcast.1), calls=%async_computation | async-start | bytes 6291456 | tf_op jit(solution)/shard_map/all_to_all | solution.py:109
  21.9 3.3 fusion.58
  25.2 1.8 multiply_convert_fusion.9
  31.7 2.6 fusion.60
  34.3 33.1 %all-to-all-done = bf16[8,384,512]{1,2,0:T(8,128)(2,1)} async-done(((bf16[8,384,512]{1,2,0:T(8,128)(2,1)}), bf16[8,384,512]{1,2,0:T(8,128)(2,1)}, u32[]{:S(2)}, u32[]{:S(2)}) %all-to-all-start) | async-done | bytes 3145760 | tf_op jit(solution)/shard_map/all_to_all | solution.py:109
  69.3 2.0 maximum_bitcast_fusion
  71.3 5.7 all-to-all-start.1
  77.1 39.0 %all-to-all-done.1 = bf16[16,384,256]{2,1,0:T(8,128)(2,1)} async-done(((bf16[16,384,256]{2,1,0:T(8,128)(2,1)}), bf16[16,384,256]{2,1,0:T(8,128)(2,1)}, u32[]{:S(2)}, u32[]{:S(2)}) %all-to-all-start.1) | async-done | bytes 3145760 | tf_op jit(solution)/shard_map/all_to_all | solution.py:14
  116.1 2.4 convert_reduce_fusion
  120.2 42.0 %all_to_all.40 = bf16[16,384,256]{1,2,0:T(8,128)(2,1)S(1)} all-to-all(bf16[16,384,256]{1,2,0:T(8,128)(2,1)S(1)} %broadcast_in_dim.8), channel_id=1, replica_groups=mesh['z'=4,'ylo'=2,'core'=2,'x'=4,'yhi'=2] {'z','ylo','core'}, dimensions={0} | all-to-all | bytes 6291456 | tf_op jit(solution)/shard_map/all_to_all | solution.py:20
  164.1 3.1 convolution_convert_fusion
  167.1 5.9 pad_maximum_fusion
  174.4 3.8 multiply_convert_fusion.8
  182.4 91.2 %all_to_all.41 = bf16[8,384,896]{2,1,0:T(8,128)(2,1)S(1)} all-to-all(bf16[8,384,896]{2,1,0:T(8,128)(2,1)S(1)} %broadcast_in_dim.9), channel_id=1, replica_groups=mesh['z'=4,'ylo'=2,'core'=2,'x'=4,'yhi'=2] {'x','yhi'}, dimensions={0} | all-to-all | bytes 11010048 | tf_op jit(solution)/shard_map/all_to_all | solution.py:148
  273.6 3.7 fusion.13
  277.4 5.3 fusion.16
  282.6 48.4 %reduce-scatter.2.cloned.1.call-done = bf16[512,896]{0,1:T(8,128)(2,1)} async-done(((bf16[4096,896]{0,1:T(8,128)(2,1)}), bf16[512,896]{0,1:T(8,128)(2,1)}) %reduce-scatter.2.cloned.1.call-update) | async-done | bytes 917520 | tf_op jit(solution)/shard_map/reduce_scatter | solution.py:133
  331.0 2.6 fusion.56
  335.2 2.5 copy.35
  337.7 3.7 multiply_reduce_fusion.1
  341.4 3.2 all-reduce.3
  344.6 5.5 all-reduce.4
  350.1 11.3 %all-reduce.1 = (f32[]{:T(128)}, f32[]{:T(128)}, f32[]{:T(128)}) all-reduce(f32[]{:T(128)} %get-tuple-element.23, f32[]{:T(128)} %get-tuple-element.24, f32[]{:T(128)} %get-tuple-element.25), channel_id=1, replica_groups=mesh['z'=4,'ylo'=2,'core'=2,'x'=4,'yhi'=2] {'z'}, use_global_device_ids=true, to_apply=%region_17.0 | all-reduce | flops 3 | bytes 24 | tf_op jit(solution)/shard_map/psum | solution.py:32
  361.5 10.1 %all-reduce = (f32[]{:T(128)}, f32[]{:T(128)}, f32[]{:T(128)}) all-reduce(f32[]{:T(128)} %get-tuple-element.14, f32[]{:T(128)} %get-tuple-element.15, f32[]{:T(128)} %get-tuple-element.16), channel_id=1, replica_groups=mesh['z'=4,'ylo'=2,'core'=2,'x'=4,'yhi'=2] {'x'}, use_global_device_ids=true, to_apply=%region_18.0 | all-reduce | flops 3 | bytes 24 | tf_op jit(solution)/shard_map/psum | solution.py:32
  371.6 7.1 %all-reduce.2 = (f32[]{:T(128)}, f32[]{:T(128)}, f32[]{:T(128)}) all-reduce(f32[]{:T(128)} %get-tuple-element.11, f32[]{:T(128)} %get-tuple-element.12, f32[]{:T(128)} %get-tuple-element.13), channel_id=1, replica_groups=mesh['z'=4,'ylo'=2,'core'=2,'x'=4,'yhi'=2] {'yhi'}, use_global_device_ids=true, to_apply=%region_19.0 | all-reduce | flops 3 | bytes 24 | tf_op jit(solution)/shard_map/psum | solution.py:32
  380.9 2.7 add_convert_fusion
  384.8 4.0 broadcast_in_dim.10
  388.8 4.8 all-to-all-start.4
  393.9 1.9 slice.65
  395.8 105.5 %all-to-all-done.4 = bf16[8,512,896]{2,1,0:T(8,128)(2,1)} async-done(((bf16[8,512,896]{2,1,0:T(8,128)(2,1)}), bf16[8,512,896]{2,1,0:T(8,128)(2,1)}, u32[]{:S(2)}, u32[]{:S(2)}) %all-to-all-start.4) | async-done | bytes 7340064 | tf_op jit(solution)/shard_map/all_to_all | solution.py:26
  501.3 4.3 fusion.21
  505.6 4.8 fusion.24
  510.4 3.6 fusion.38
  514.0 4.8 fusion
  519.0 30.5 %all_to_all.42 = bf16[16,256,256]{2,1,0:T(8,128)(2,1)S(1)} all-to-all(bf16[16,256,256]{2,1,0:T(8,128)(2,1)S(1)} %bitcast.81), channel_id=1, replica_groups=mesh['z'=4,'ylo'=2,'core'=2,'x'=4,'yhi'=2] {'z','ylo','core'}, dimensions={0} | all-to-all | bytes 4194304 | tf_op jit(solution)/shard_map/all_to_all | solution.py:14
  551.5 4.7 all-to-all-start.6
  556.2 5.3 fusion.61
  561.5 22.6 %all-to-all-done.6 = bf16[16,256,256]{1,2,0:T(8,128)(2,1)} async-done(((bf16[16,256,256]{1,2,0:T(8,128)(2,1)}), bf16[16,256,256]{1,2,0:T(8,128)(2,1)}, u32[]{:S(2)}, u32[]{:S(2)}) %all-to-all-start.6) | async-done | bytes 2097184 | tf_op jit(solution)/shard_map/all_to_all | solution.py:20
  584.0 4.0 convolution_add_fusion.4
  591.5 3.6 convolution_add_fusion.1
  595.2 4.8 fusion.1
  600.2 30.5 %all_to_all.43 = bf16[16,256,256]{2,1,0:T(8,128)(2,1)S(1)} all-to-all(bf16[16,256,256]{2,1,0:T(8,128)(2,1)S(1)} %bitcast.82), channel_id=1, replica_groups=mesh['z'=4,'ylo'=2,'core'=2,'x'=4,'yhi'=2] {'z','ylo','core'}, dimensions={0} | all-to-all | bytes 4194304 | tf_op jit(solution)/shard_map/all_to_all | solution.py:14
  631.7 3.1 psum.155
  634.7 5.5 psum.156
  640.3 9.2 %psum.157 = f32[]{:T(128)} all-reduce(f32[]{:T(128)} %psum.156), channel_id=1, replica_groups=mesh['z'=4,'ylo'=2,'core'=2,'x'=4,'yhi'=2] {'z'}, use_global_device_ids=true, to_apply=%region_25.0 | all-reduce | flops 1 | bytes 8 | tf_op jit(solution)/shard_map/psum | solution.py:32
  650.1 8.9 %psum.158 = f32[]{:T(128)} all-reduce(f32[]{:T(128)} %psum.157), channel_id=1, replica_groups=mesh['z'=4,'ylo'=2,'core'=2,'x'=4,'yhi'=2] {'x'}, use_global_device_ids=true, to_apply=%region_26.0 | all-reduce | flops 1 | bytes 8 | tf_op jit(solution)/shard_map/psum | solution.py:32
  659.1 7.0 %psum.159 = f32[]{:T(128)} all-reduce(f32[]{:T(128)} %psum.158), channel_id=1, replica_groups=mesh['z'=4,'ylo'=2,'core'=2,'x'=4,'yhi'=2] {'yhi'}, use_global_device_ids=true, to_apply=%region_27.0 | all-reduce | flops 1 | bytes 8 | tf_op jit(solution)/shard_map/psum | solution.py:32
  (77 shorter events, 30.8 us)
Async XLA Ops:
  10.2 1.7 copy-start.12
  14.7 7.2 %copy-start.9 = (bf16[128,4096]{1,0:T(8,128)(2,1)S(1)}, bf16[128,4096]{1,0:T(8,128)(2,1)}, u32[]{:S(2)}) copy-start(bf16[128,4096]{1,0:T(8,128)(2,1)} %param.7) | copy-start | bytes 3145732
  14.7 52.7 %all-to-all-start = ((bf16[8,384,512]{1,2,0:T(8,128)(2,1)}), bf16[8,384,512]{1,2,0:T(8,128)(2,1)}, u32[]{:S(2)}, u32[]{:S(2)}) async-start(bf16[8,384,512]{1,2,0:T(8,128)(2,1)} %bitcast.1), calls=%async_computation | async-start | bytes 6291456 | tf_op jit(solution)/shard_map/all_to_all | solution.py:109
  21.9 3.3 copy-start.3
  25.2 2.9 copy-start.17
  25.2 2.2 copy-start
  25.2 2.9 copy-start.14
  27.1 2.3 copy-start.5
  71.3 47.2 %copy-start.16 = (bf16[128,4096]{1,0:T(8,128)(2,1)S(1)}, bf16[128,4096]{1,0:T(8,128)(2,1)}, u32[]{:S(2)}) copy-start(bf16[128,4096]{1,0:T(8,128)(2,1)} %param.8) | copy-start | bytes 3145732
  71.3 47.2 %copy-start.20 = (f32[384]{0:T(512)S(1)}, f32[384]{0:T(512)}, u32[]{:S(2)}) copy-start(f32[384]{0:T(512)} %constant.43.clone.1) | copy-start | bytes 4612
  71.3 44.8 %all-to-all-start.1 = ((bf16[16,384,256]{2,1,0:T(8,128)(2,1)}), bf16[16,384,256]{2,1,0:T(8,128)(2,1)}, u32[]{:S(2)}, u32[]{:S(2)}) async-start(bf16[16,384,256]{2,1,0:T(8,128)(2,1)} %maximum_bitcast_fusion), calls=%async_computation.1 | async-start | bytes 6291456 | tf_op jit(solution)/shard_map/all_to_all | solution.py:14
  77.0 254.0 %reduce-scatter.2.cloned.1.call-start = ((), (), s32[]{:S(2)}) async-start(), calls=%async_computation.9 | async-start | bytes 8257536 | tf_op jit(solution)/shard_map/reduce_scatter | solution.py:133
  162.4 1.3 copy-start.10
  162.6 1.5 copy-start.7
  173.0 1.2 copy-start.11
  173.0 1.3 copy-start.18
  173.0 1.3 copy-start.19
  173.1 5.1 copy-start.1
  173.1 5.1 copy-start.8
  383.6 1.1 copy-start.13
  388.8 112.5 %all-to-all-start.4 = ((bf16[8,512,896]{2,1,0:T(8,128)(2,1)}), bf16[8,512,896]{2,1,0:T(8,128)(2,1)}, u32[]{:S(2)}, u32[]{:S(2)}) async-start(bf16[8,512,896]{2,1,0:T(8,128)(2,1)} %broadcast_in_dim.10), calls=%async_computation.5 | async-start | bytes 14680064 | tf_op jit(solution)/shard_map/all_to_all | solution.py:26
  393.6 120.4 %all-gather.2.cloned.1.call-start = ((), (), s32[]{:S(2)}) async-start(), calls=%async_computation.10 | async-start | bytes 4718592 | tf_op jit(solution)/shard_map/all_gather | solution.py:170
  501.3 4.3 copy-start.15
  505.6 4.8 copy-start.2
  551.5 32.5 %all-to-all-start.6 = ((bf16[16,256,256]{1,2,0:T(8,128)(2,1)}), bf16[16,256,256]{1,2,0:T(8,128)(2,1)}, u32[]{:S(2)}, u32[]{:S(2)}) async-start(bf16[16,256,256]{1,2,0:T(8,128)(2,1)} %broadcast_in_dim.11), calls=%async_computation.7 | async-start | bytes 4194304 | tf_op jit(solution)/shard_map/all_to_all | solution.py:20
  584.0 4.0 copy-start.6
  588.0 2.0 copy-start.4
Sparse Core Ops, SparseCore 0:
  173.2 157.7 reduce-scatter.1
  396.8 113.0 all-gather.1

commit v9 on v7

--- a/solution.py
+++ b/solution.py
@@ -163,10 +163,12 @@
     coef_tgt = -1.0 / denom
     coef_poi = cross_tp / (denom * length_poi * length_poi)
     local_sens = (coef_tgt * grad_tgt + coef_poi * grad_poi).astype(jnp.bfloat16)
-    v_down = lax.all_gather(local_sens[:, 2 * hidden_width :], DP, axis=0, tiled=True)
-    full_gu = ag_rows(local_sens[:, : 2 * hidden_width], dp_size)
-    v_gate = full_gu[:, :hidden_width]
-    v_upper = full_gu[:, hidden_width:]
+    cut = hidden_width + hidden_width // 2
+    tail = lax.all_gather(local_sens[:, cut:], DP, axis=0, tiled=True)
+    head = ag_rows(local_sens[:, :cut], dp_size)
+    v_gate = head[:, :hidden_width]
+    v_upper = jnp.concatenate([head[:, hidden_width:], tail[:, : cut - hidden_width]], 1)
+    v_down = tail[:, cut - hidden_width :]
     tan_gate = matmul(poison_x, v_gate)
     tan_upper = matmul(poison_x, v_upper)
     hidden_tan = (slope_poi * tan_gate * upper_poi + silu_poi * tan_upper).astype(jnp.bfloat16)

time: 670 us -> 672 us (level)
  blocking collectives: 175 us -> 282 us
  waiting for transfers between devices: 326 us -> 230 us
  matrix products: 66.6 us -> 54.4 us
  local copies, waits for them, and re-layouts: 32.6 us -> 44.1 us
  starting transfers between devices: 32.2 us -> 22.3 us
    all_to_all x2 -> x0, waiting for transfers between devices: 129 us -> none  [the longest x1 105 us: ag_rows(): lax.all_to_all(jnp.broadcast_to(piece[None], (n, rows, cols)), DP, 0, 0,...]
    all_to_all x0 -> x1, blocking collectives: none -> 75.1 us  [ag_rows(): lax.all_to_all(jnp.broadcast_to(piece[None], (n, rows, cols)), DP, 0, 0,...]
    all_gather x1, waiting for transfers between devices: 0.01 us -> 32.5 us  [local(): tail = lax.all_gather(local_sens[:, cut:], DP, axis=0, tiled=True)]
    all_to_all x1 -> x2, blocking collectives: 41.8 us -> 72.6 us  [ag_cols(): lax.all_to_all(jnp.broadcast_to(piece[None], (n, rows, cols)), FS, 0, 0,...]
    all_to_all x2 -> x0, starting transfers between devices: 9.68 us -> none  [the longest x1 4.99 us: ag_rows(): lax.all_to_all(jnp.broadcast_to(piece[None], (n, rows, cols)), DP, 0, 0,...]
    dot_general x8, matrix products: 24.7 us -> 15.7 us  [inner_cols(): lax.dot_general(left, right, (((1,), (1,)), ((), ())), preferred_element_...]
    all_to_all x0 -> x1, local copies, waits for them, and re-layouts: none -> 8.23 us  [ag_rows(): lax.all_to_all(jnp.broadcast_to(piece[None], (n, rows, cols)), DP, 0, 0,...]
    unnamed x64 -> x78, local copies, waits for them, and re-layouts: 13.5 us -> 15.6 us
  transfers between devices with their start and end apart: 8 -> 6, of which waited for: 6 -> 5; matrix products, arithmetic and copies ran while one was open for 7% -> 7% of each run, Pallas kernels for 0% -> 0%
where the time goes in v9:
time: 672 us; the launch traced here: 664 us
  blocking collectives  282 us (42%)
  waiting for transfers between devices  230 us (34%)
  matrix products  54.4 us (8%)
  local copies, waits for them, and re-layouts  44.1 us (7%)
  starting transfers between devices  22.3 us (3%)
  between operations  19.7 us (3%)
  other arithmetic  10.5 us (2%)
    all_gather x1, waiting for transfers between devices, local(): lax.all_gather(jnp.concatenate([hidden_tgt, hidden_poi], 0), DP, axis=0,...  84.2 us
    all_to_all x1, blocking collectives, ag_rows(): lax.all_to_all(jnp.broadcast_to(piece[None], (n, rows, cols)), DP, 0, 0,...  75.1 us
    all_to_all x2, blocking collectives, ag_cols(): lax.all_to_all(jnp.broadcast_to(piece[None], (n, rows, cols)), FS, 0, 0,...  72.6 us
    psum x10, blocking collectives, psum_all(): x = lax.psum(x, axis)  72.3 us
    all_to_all x2, blocking collectives, rs_cols(): r = lax.all_to_all(r, FS, 0, 0, tiled=False)  62.4 us
    all_to_all x1, waiting for transfers between devices, local(): lax.all_to_all(error_all.reshape(-1, dp_size, rows_d).transpose(1, 0, 2),...  40.9 us
    all_to_all x1, waiting for transfers between devices, rs_cols(): r = lax.all_to_all(r, FS, 0, 0, tiled=False)  39 us
    all_to_all x1, waiting for transfers between devices, local(): lax.all_to_all(x_loc.reshape(-1, dp_size, model_width // dp_size).transpo...  33.7 us
  transfers between devices with their start and end apart: 6, of which 5 were waited for; matrix products, arithmetic and copies ran while one was open for 7% of the time, Pallas kernels for 0%

profile of v9, /device:TPU:0, one launch (start us, length us, event | category | flops | bytes accessed | tf_op | source)
XLA Modules:
  0.0 663.6 jit_solution(9856970507435948420)
XLA Ops:
  9.2 3.2 copy.24
  12.5 7.2 %all-to-all-start = ((bf16[8,384,512]{1,2,0:T(8,128)(2,1)}), bf16[8,384,512]{1,2,0:T(8,128)(2,1)}, u32[]{:S(2)}, u32[]{:S(2)}) async-start(bf16[8,384,512]{1,2,0:T(8,128)(2,1)} %bitcast.1), calls=%async_computation | async-start | bytes 6291456 | tf_op jit(solution)/shard_map/all_to_all | solution.py:109
  19.7 3.3 fusion.72
  23.0 1.8 multiply_convert_fusion.9
  28.3 1.9 multiply_convert_fusion.3
  31.5 33.7 %all-to-all-done = bf16[8,384,512]{1,2,0:T(8,128)(2,1)} async-done(((bf16[8,384,512]{1,2,0:T(8,128)(2,1)}), bf16[8,384,512]{1,2,0:T(8,128)(2,1)}, u32[]{:S(2)}, u32[]{:S(2)}) %all-to-all-start) | async-done | bytes 3145760 | tf_op jit(solution)/shard_map/all_to_all | solution.py:109
  65.5 2.0 maximum_bitcast_fusion
  67.5 5.5 all-to-all-start.1
  73.1 39.0 %all-to-all-done.1 = bf16[16,384,256]{2,1,0:T(8,128)(2,1)S(1)} async-done(((bf16[16,384,256]{2,1,0:T(8,128)(2,1)}), bf16[16,384,256]{2,1,0:T(8,128)(2,1)S(1)}, u32[]{:S(2)}, u32[]{:S(2)}) %all-to-all-start.1) | async-done | bytes 3145760 | tf_op jit(solution)/shard_map/all_to_all | solution.py:14
  115.6 41.8 %all_to_all.45 = bf16[16,384,256]{1,2,0:T(8,128)(2,1)S(1)} all-to-all(bf16[16,384,256]{1,2,0:T(8,128)(2,1)S(1)} %broadcast_in_dim.8), channel_id=1, replica_groups=mesh['z'=4,'ylo'=2,'core'=2,'x'=4,'yhi'=2] {'z','ylo','core'}, dimensions={0} | all-to-all | bytes 6291456 | tf_op jit(solution)/shard_map/all_to_all | solution.py:20
  157.4 2.9 copy.29
  160.3 4.7 all-to-all-start.4
  166.2 3.3 multiply_convert_fusion.8
  169.8 2.6 copy-done.1
  174.1 40.9 %all-to-all-done.4 = bf16[8,384,512]{2,1,0:T(8,128)(2,1)} async-done(((bf16[8,384,512]{2,1,0:T(8,128)(2,1)}), bf16[8,384,512]{2,1,0:T(8,128)(2,1)}, u32[]{:S(2)}, u32[]{:S(2)}) %all-to-all-start.4) | async-done | bytes 3145760 | tf_op jit(solution)/shard_map/all_to_all | solution.py:133
  215.0 3.1 broadcast_in_dim.9
  218.1 4.7 all-to-all-start.3
  222.8 84.2 %all-gather.6.cloned.1.call-done = bf16[3072,448]{0,1:T(8,128)(2,1)} async-done(((bf16[384,448]{0,1:T(8,128)(2,1)}), bf16[3072,448]{0,1:T(8,128)(2,1)}) %all-gather.6.cloned.1.call-update) | async-done | bytes 2752528 | tf_op jit(solution)/shard_map/all_gather | solution.py:136
  307.0 2.4 copy.49
  309.6 3.0 convolution_bitcast_fusion
  312.6 3.9 fusion.25
  316.5 5.0 fusion.20
  321.6 3.2 fusion.17
  326.0 1.7 multiply_reduce_fusion.1
  327.7 3.1 all-reduce.3
  330.9 5.6 all-reduce.4
  336.5 11.2 %all-reduce.1 = (f32[]{:T(128)}, f32[]{:T(128)}, f32[]{:T(128)}) all-reduce(f32[]{:T(128)} %get-tuple-element.23, f32[]{:T(128)} %get-tuple-element.24, f32[]{:T(128)} %get-tuple-element.25), channel_id=1, replica_groups=mesh['z'=4,'ylo'=2,'core'=2,'x'=4,'yhi'=2] {'z'}, use_global_device_ids=true, to_apply=%region_16.0 | all-reduce | flops 3 | bytes 24 | tf_op jit(solution)/shard_map/psum | solution.py:32
  347.7 11.2 %all-reduce = (f32[]{:T(128)}, f32[]{:T(128)}, f32[]{:T(128)}) all-reduce(f32[]{:T(128)} %get-tuple-element.14, f32[]{:T(128)} %get-tuple-element.15, f32[]{:T(128)} %get-tuple-element.16), channel_id=1, replica_groups=mesh['z'=4,'ylo'=2,'core'=2,'x'=4,'yhi'=2] {'x'}, use_global_device_ids=true, to_apply=%region_17.0 | all-reduce | flops 3 | bytes 24 | tf_op jit(solution)/shard_map/psum | solution.py:32
  358.9 7.1 %all-reduce.2 = (f32[]{:T(128)}, f32[]{:T(128)}, f32[]{:T(128)}) all-reduce(f32[]{:T(128)} %get-tuple-element.11, f32[]{:T(128)} %get-tuple-element.12, f32[]{:T(128)} %get-tuple-element.13), channel_id=1, replica_groups=mesh['z'=4,'ylo'=2,'core'=2,'x'=4,'yhi'=2] {'yhi'}, use_global_device_ids=true, to_apply=%region_18.0 | all-reduce | flops 3 | bytes 24 | tf_op jit(solution)/shard_map/psum | solution.py:32
  368.1 2.5 add_convert_fusion
  372.7 75.1 %all_to_all.46 = bf16[8,512,672]{1,2,0:T(8,128)(2,1)} all-to-all(bf16[8,512,672]{1,2,0:T(8,128)(2,1)S(1)} %broadcast_in_dim.10), channel_id=1, replica_groups=mesh['z'=4,'ylo'=2,'core'=2,'x'=4,'yhi'=2] {'x','yhi'}, dimensions={0} | all-to-all | bytes 11010048 | tf_op jit(solution)/shard_map/all_to_all | solution.py:26
  447.8 8.2 %copy.35 = bf16[8,512,672]{2,1,0:T(8,128)(2,1)} copy(bf16[8,512,672]{1,2,0:T(8,128)(2,1)} %all_to_all.46) | data formatting | bytes 11010048 | tf_op jit(solution)/shard_map/all_to_all | solution.py:26
  456.0 4.4 slice.82
  460.5 3.6 fusion.31
  464.0 32.5 %all-gather.4.cloned.1.call-done = bf16[4096,672]{1,0:T(8,128)(2,1)} async-done(((bf16[512,672]{1,0:T(8,128)(2,1)}), bf16[4096,672]{1,0:T(8,128)(2,1)}) %all-gather.4.cloned.1.call-update) | async-done | bytes 5505040 | tf_op jit(solution)/shard_map/all_gather | solution.py:167
  496.5 1.9 slice.84
  499.7 2.2 fusion.30
  504.1 2.6 fusion
  506.9 32.0 %all_to_all.47 = bf16[16,256,256]{2,1,0:T(8,128)(2,1)S(1)} all-to-all(bf16[16,256,256]{2,1,0:T(8,128)(2,1)S(1)} %bitcast.92), channel_id=1, replica_groups=mesh['z'=4,'ylo'=2,'core'=2,'x'=4,'yhi'=2] {'z','ylo','core'}, dimensions={0} | all-to-all | bytes 4194304 | tf_op jit(solution)/shard_map/all_to_all | solution.py:14
  539.6 30.8 %all_to_all.48 = bf16[16,256,256]{1,2,0:T(8,128)(2,1)S(1)} all-to-all(bf16[16,256,256]{1,2,0:T(8,128)(2,1)S(1)} %broadcast_in_dim.11), channel_id=1, replica_groups=mesh['z'=4,'ylo'=2,'core'=2,'x'=4,'yhi'=2] {'z','ylo','core'}, dimensions={0} | all-to-all | bytes 4194304 | tf_op jit(solution)/shard_map/all_to_all | solution.py:20
  572.0 6.2 fusion.34
  584.6 3.0 fusion.1
  587.8 30.3 %all_to_all.49 = bf16[16,256,256]{2,1,0:T(8,128)(2,1)S(1)} all-to-all(bf16[16,256,256]{2,1,0:T(8,128)(2,1)S(1)} %bitcast.93), channel_id=1, replica_groups=mesh['z'=4,'ylo'=2,'core'=2,'x'=4,'yhi'=2] {'z','ylo','core'}, dimensions={0} | all-to-all | bytes 4194304 | tf_op jit(solution)/shard_map/all_to_all | solution.py:14
  619.0 3.1 psum.155
  622.1 5.5 psum.156
  627.7 9.2 %psum.157 = f32[]{:T(128)} all-reduce(f32[]{:T(128)} %psum.156), channel_id=1, replica_groups=mesh['z'=4,'ylo'=2,'core'=2,'x'=4,'yhi'=2] {'z'}, use_global_device_ids=true, to_apply=%region_24.0 | all-reduce | flops 1 | bytes 8 | tf_op jit(solution)/shard_map/psum | solution.py:32
  637.5 9.2 %psum.158 = f32[]{:T(128)} all-reduce(f32[]{:T(128)} %psum.157), channel_id=1, replica_groups=mesh['z'=4,'ylo'=2,'core'=2,'x'=4,'yhi'=2] {'x'}, use_global_device_ids=true, to_apply=%region_25.0 | all-reduce | flops 1 | bytes 8 | tf_op jit(solution)/shard_map/psum | solution.py:32
  646.7 7.0 %psum.159 = f32[]{:T(128)} all-reduce(f32[]{:T(128)} %psum.158), channel_id=1, replica_groups=mesh['z'=4,'ylo'=2,'core'=2,'x'=4,'yhi'=2] {'yhi'}, use_global_device_ids=true, to_apply=%region_26.0 | all-reduce | flops 1 | bytes 8 | tf_op jit(solution)/shard_map/psum | solution.py:32
  (118 shorter events, 31.3 us)
Async XLA Ops:
  7.2 1.9 copy-start.18
  9.2 3.3 copy-start.15
  12.5 7.2 %copy-start.11 = (bf16[128,4096]{1,0:T(8,128)(2,1)S(1)}, bf16[128,4096]{1,0:T(8,128)(2,1)}, u32[]{:S(2)}) copy-start(bf16[128,4096]{1,0:T(8,128)(2,1)} %param.7) | copy-start | bytes 3145732
  12.5 52.7 %all-to-all-start = ((bf16[8,384,512]{1,2,0:T(8,128)(2,1)}), bf16[8,384,512]{1,2,0:T(8,128)(2,1)}, u32[]{:S(2)}, u32[]{:S(2)}) async-start(bf16[8,384,512]{1,2,0:T(8,128)(2,1)} %bitcast.1), calls=%async_computation | async-start | bytes 6291456 | tf_op jit(solution)/shard_map/all_to_all | solution.py:109
  19.7 3.3 copy-start.4
  23.0 2.9 copy-start.30
  23.0 2.2 copy-start
  23.0 2.9 copy-start.19
  24.8 2.3 copy-start.6
  28.3 1.9 copy-start.8
  67.5 44.6 %all-to-all-start.1 = ((bf16[16,384,256]{2,1,0:T(8,128)(2,1)}), bf16[16,384,256]{2,1,0:T(8,128)(2,1)S(1)}, u32[]{:S(2)}, u32[]{:S(2)}) async-start(bf16[16,384,256]{2,1,0:T(8,128)(2,1)} %maximum_bitcast_fusion), calls=%async_computation.1 | async-start | bytes 6291456 | tf_op jit(solution)/shard_map/all_to_all | solution.py:14
  73.0 39.5 %copy-start.33 = (f32[384]{0:T(512)S(1)}, f32[384]{0:T(512)}, u32[]{:S(2)}) copy-start(f32[384]{0:T(512)} %constant.43.clone.1) | copy-start | bytes 4612
  112.1 1.6 copy-start.28
  112.1 1.9 copy-start.29
  160.3 54.7 %all-to-all-start.4 = ((bf16[8,384,512]{2,1,0:T(8,128)(2,1)}), bf16[8,384,512]{2,1,0:T(8,128)(2,1)}, u32[]{:S(2)}, u32[]{:S(2)}) async-start(bf16[8,384,512]{2,1,0:T(8,128)(2,1)} %bitcast.87), calls=%async_computation.4 | async-start | bytes 6291456 | tf_op jit(solution)/shard_map/all_to_all | solution.py:133
  165.0 142.1 %all-gather.6.cloned.1.call-start = ((), (), s32[]{:S(2)}) async-start(), calls=%async_computation.10 | async-start | bytes 3096576 | tf_op jit(solution)/shard_map/all_gather | solution.py:136
  166.2 3.6 copy-start.12
  169.6 2.8 copy-start.1
  169.6 2.9 copy-start.9
  169.7 3.9 copy-start.22
  173.6 44.5 %copy-start.31 = (bf16[256,448]{0,1:T(8,128)(2,1)}, bf16[256,448]{0,1:T(8,128)(2,1)S(1)}, u32[]{:S(2)}) copy-start(bf16[256,448]{0,1:T(8,128)(2,1)S(1)} %get-tuple-element.29) | copy-start | bytes 688132
  218.1 98.4 %all-to-all-start.3 = ((bf16[8,384,896]{2,1,0:T(8,128)(2,1)}), bf16[8,384,896]{2,1,0:T(8,128)(2,1)}, u32[]{:S(2)}, u32[]{:S(2)}) async-start(bf16[8,384,896]{2,1,0:T(8,128)(2,1)} %broadcast_in_dim.9), calls=%async_computation.3 | async-start | bytes 11010048 | tf_op jit(solution)/shard_map/all_to_all | solution.py:144
  222.8 273.7 %all-gather.4.cloned.1.call-start = ((), (), s32[]{:S(2)}) async-start(), calls=%async_computation.9 | async-start | bytes 7077888 | tf_op jit(solution)/shard_map/all_gather | solution.py:167
  321.5 4.5 copy-start.16
  321.5 4.5 copy-start.17
  324.8 1.3 copy-start.14
  456.0 4.5 copy-start.20
  496.5 3.2 copy-start.21
  496.5 3.2 copy-start.24
  498.4 1.3 copy-start.26
  499.7 2.2 copy-start.2
  499.7 2.2 copy-start.10
  499.7 2.3 copy-start.13
  499.7 3.7 slice-start.2
  502.0 2.1 slice-start.3
  539.4 31.1 %copy-start.3 = (bf16[448,4096]{1,0:T(8,128)(2,1)S(1)}, bf16[448,4096]{1,0:T(8,128)(2,1)}, u32[]{:S(2)}) copy-start(bf16[448,4096]{1,0:T(8,128)(2,1)} %param.13) | copy-start | bytes 11010052
  570.4 1.6 copy-start.23
  572.0 6.2 copy-start.7
  578.2 2.0 copy-start.5
  578.2 3.5 slice-start
  580.3 2.1 slice-start.1
  582.4 1.6 copy-start.25
  582.4 2.2 copy-start.27
  582.4 2.2 copy-start.32
Sparse Core Ops, SparseCore 0:
  168.0 139.0 all-gather.5
  372.1 124.3 all-gather.3

commit v10 on v7

--- a/solution.py
+++ b/solution.py
@@ -121,7 +121,13 @@
     err_cols = (
         (x_cols.astype(jnp.float32) + out_cols - y_cols.astype(jnp.float32)) / scale_rows
     ).astype(jnp.bfloat16)
-    error_all = ag_cols(err_cols, fs_size)
+    error_all = jnp.concatenate(
+        [
+            lax.all_gather(err_cols[:n_tgt], FS, axis=1, tiled=True),
+            ag_cols(err_cols[n_tgt:], fs_size),
+        ],
+        0,
+    )
     error_tgt, back_tgt, gback_tgt, uback_tgt = backward2(
         error_all[:n_tgt], upper_tgt, silu_tgt, slope_tgt, w_down
     )

time: 670 us -> 688 us (1.027)
  waiting for transfers between devices: 326 us -> 371 us
  blocking collectives: 175 us -> 133 us
    all_to_all x1 -> x0, blocking collectives: 41.8 us -> none  [ag_cols(): lax.all_to_all(jnp.broadcast_to(piece[None], (n, rows, cols)), FS, 0, 0,...]
    all_gather x0 -> x1, waiting for transfers between devices: none -> 40.3 us  [local(): lax.all_gather(err_cols[:n_tgt], FS, axis=1, tiled=True)]
    all_to_all x1 -> x2, waiting for transfers between devices: 23.3 us -> 23.3 us  [ag_cols(): lax.all_to_all(jnp.broadcast_to(piece[None], (n, rows, cols)), FS, 0, 0,...]
  transfers between devices with their start and end apart: 8 -> 10, of which waited for: 6 -> 7; matrix products, arithmetic and copies ran while one was open for 7% -> 8% of each run, Pallas kernels for 0% -> 0%
where the time goes in v10:
time: 688 us; the launch traced here: 680 us
  waiting for transfers between devices  371 us (54%)
  blocking collectives  133 us (19%)
  matrix products  69.3 us (10%)
  starting transfers between devices  37.8 us (5%)
  local copies, waits for them, and re-layouts  31.2 us (5%)
  between operations  20.9 us (3%)
  other arithmetic  16.6 us (2%)
    all_to_all x1, waiting for transfers between devices, ag_rows(): lax.all_to_all(jnp.broadcast_to(piece[None], (n, rows, cols)), DP, 0, 0,...  106 us
    all_gather x1, waiting for transfers between devices, local(): lax.all_gather(jnp.concatenate([hidden_tgt, hidden_poi], 0), DP, axis=0,...  84.6 us
    psum x10, blocking collectives, psum_all(): x = lax.psum(x, axis)  71.7 us
    all_to_all x2, blocking collectives, rs_cols(): r = lax.all_to_all(r, FS, 0, 0, tiled=False)  61.2 us
    all_to_all x1, waiting for transfers between devices, local(): lax.all_to_all(error_all.reshape(-1, dp_size, rows_d).transpose(1, 0, 2),...  43.8 us
    all_gather x1, waiting for transfers between devices, local(): lax.all_gather(err_cols[:n_tgt], FS, axis=1, tiled=True)  40.3 us
    all_to_all x1, waiting for transfers between devices, rs_cols(): r = lax.all_to_all(r, FS, 0, 0, tiled=False)  39 us
    all_to_all x1, waiting for transfers between devices, local(): lax.all_to_all(x_loc.reshape(-1, dp_size, model_width // dp_size).transpo...  33.2 us
  transfers between devices with their start and end apart: 10, of which 7 were waited for; matrix products, arithmetic and copies ran while one was open for 8% of the time, Pallas kernels for 0%

profile of v10, /device:TPU:0, one launch (start us, length us, event | category | flops | bytes accessed | tf_op | source)
XLA Modules:
  0.0 679.5 jit_solution(12569585736385522032)
XLA Ops:
  10.1 3.2 copy.27
  13.3 7.2 %all-to-all-start = ((bf16[8,384,512]{1,2,0:T(8,128)(2,1)}), bf16[8,384,512]{1,2,0:T(8,128)(2,1)}, u32[]{:S(2)}, u32[]{:S(2)}) async-start(bf16[8,384,512]{1,2,0:T(8,128)(2,1)} %bitcast.1), calls=%async_computation | async-start | bytes 6291456 | tf_op jit(solution)/shard_map/all_to_all | solution.py:109
  20.5 3.3 fusion.67
  30.2 2.6 fusion.69
  32.9 33.2 %all-to-all-done = bf16[8,384,512]{1,2,0:T(8,128)(2,1)} async-done(((bf16[8,384,512]{1,2,0:T(8,128)(2,1)}), bf16[8,384,512]{1,2,0:T(8,128)(2,1)}, u32[]{:S(2)}, u32[]{:S(2)}) %all-to-all-start) | async-done | bytes 3145760 | tf_op jit(solution)/shard_map/all_to_all | solution.py:109
  69.8 5.6 all-to-all-start.1
  75.5 39.0 %all-to-all-done.1 = bf16[16,384,256]{2,1,0:T(8,128)(2,1)} async-done(((bf16[16,384,256]{2,1,0:T(8,128)(2,1)}), bf16[16,384,256]{2,1,0:T(8,128)(2,1)}, u32[]{:S(2)}, u32[]{:S(2)}) %all-to-all-start.1) | async-done | bytes 3145760 | tf_op jit(solution)/shard_map/all_to_all | solution.py:14
  120.3 4.4 all-to-all-start.2
  124.8 40.3 %all-gather.5.cloned.1.call-done = bf16[128,4096]{1,0:T(8,128)(2,1)} async-done(((bf16[128,256]{1,0:T(8,128)(2,1)}), bf16[128,4096]{1,0:T(8,128)(2,1)}) %all-gather.5.cloned.1.call-update) | async-done | bytes 1048592 | tf_op jit(solution)/shard_map/all_gather | solution.py:126
  168.0 4.0 copy.35
  172.1 3.5 maximum_bitcast_fusion.1
  175.6 5.8 all-to-all-start.4
  182.5 3.3 multiply_convert_fusion.8
  185.8 2.8 multiply_convert_fusion.2
  189.1 43.8 %all-to-all-done.4 = bf16[8,384,512]{2,1,0:T(8,128)(2,1)} async-done(((bf16[8,384,512]{2,1,0:T(8,128)(2,1)}), bf16[8,384,512]{2,1,0:T(8,128)(2,1)}, u32[]{:S(2)}, u32[]{:S(2)}) %all-to-all-start.4) | async-done | bytes 3145760 | tf_op jit(solution)/shard_map/all_to_all | solution.py:139
  232.9 3.2 broadcast_in_dim.9
  236.1 4.7 all-to-all-start.3
  240.8 84.6 %all-gather.9.cloned.1.call-done = bf16[3072,448]{0,1:T(8,128)(2,1)} async-done(((bf16[384,448]{0,1:T(8,128)(2,1)}), bf16[3072,448]{0,1:T(8,128)(2,1)}) %all-gather.9.cloned.1.call-update) | async-done | bytes 2752528 | tf_op jit(solution)/shard_map/all_gather | solution.py:142
  325.4 2.4 copy.54
  330.0 4.2 fusion.24
  334.3 5.0 fusion.19
  339.3 3.7 fusion.16
  344.8 3.1 all-reduce.3
  347.9 5.6 all-reduce.4
  353.5 10.9 %all-reduce.1 = (f32[]{:T(128)}, f32[]{:T(128)}, f32[]{:T(128)}) all-reduce(f32[]{:T(128)} %get-tuple-element.23, f32[]{:T(128)} %get-tuple-element.24, f32[]{:T(128)} %get-tuple-element.25), channel_id=1, replica_groups=mesh['z'=4,'ylo'=2,'core'=2,'x'=4,'yhi'=2] {'z'}, use_global_device_ids=true, to_apply=%region_16.0 | all-reduce | flops 3 | bytes 24 | tf_op jit(solution)/shard_map/psum | solution.py:32
  364.4 11.2 %all-reduce = (f32[]{:T(128)}, f32[]{:T(128)}, f32[]{:T(128)}) all-reduce(f32[]{:T(128)} %get-tuple-element.14, f32[]{:T(128)} %get-tuple-element.15, f32[]{:T(128)} %get-tuple-element.16), channel_id=1, replica_groups=mesh['z'=4,'ylo'=2,'core'=2,'x'=4,'yhi'=2] {'x'}, use_global_device_ids=true, to_apply=%region_17.0 | all-reduce | flops 3 | bytes 24 | tf_op jit(solution)/shard_map/psum | solution.py:32
  375.6 7.1 %all-reduce.2 = (f32[]{:T(128)}, f32[]{:T(128)}, f32[]{:T(128)}) all-reduce(f32[]{:T(128)} %get-tuple-element.11, f32[]{:T(128)} %get-tuple-element.12, f32[]{:T(128)} %get-tuple-element.13), channel_id=1, replica_groups=mesh['z'=4,'ylo'=2,'core'=2,'x'=4,'yhi'=2] {'yhi'}, use_global_device_ids=true, to_apply=%region_18.0 | all-reduce | flops 3 | bytes 24 | tf_op jit(solution)/shard_map/psum | solution.py:32
  384.7 3.1 add_convert_fusion
  387.8 4.0 broadcast_in_dim.10
  391.8 4.9 all-to-all-start.5
  397.8 106.5 %all-to-all-done.5 = bf16[8,512,896]{2,1,0:T(8,128)(2,1)} async-done(((bf16[8,512,896]{2,1,0:T(8,128)(2,1)}), bf16[8,512,896]{2,1,0:T(8,128)(2,1)}, u32[]{:S(2)}, u32[]{:S(2)}) %all-to-all-start.5) | async-done | bytes 7340064 | tf_op jit(solution)/shard_map/all_to_all | solution.py:26
  504.2 4.3 fusion.29
  508.6 4.8 fusion.32
  513.4 3.6 fusion.48
  517.0 4.8 fusion
  522.0 30.7 %all_to_all.45 = bf16[16,256,256]{2,1,0:T(8,128)(2,1)S(1)} all-to-all(bf16[16,256,256]{2,1,0:T(8,128)(2,1)S(1)} %bitcast.87), channel_id=1, replica_groups=mesh['z'=4,'ylo'=2,'core'=2,'x'=4,'yhi'=2] {'z','ylo','core'}, dimensions={0} | all-to-all | bytes 4194304 | tf_op jit(solution)/shard_map/all_to_all | solution.py:14
  554.6 4.7 all-to-all-start.7
  559.3 4.5 fusion.70
  563.8 23.3 %all-to-all-done.7 = bf16[16,256,256]{1,2,0:T(8,128)(2,1)} async-done(((bf16[16,256,256]{1,2,0:T(8,128)(2,1)}), bf16[16,256,256]{1,2,0:T(8,128)(2,1)}, u32[]{:S(2)}, u32[]{:S(2)}) %all-to-all-start.7) | async-done | bytes 2097184 | tf_op jit(solution)/shard_map/all_to_all | solution.py:20
  587.1 4.0 convolution_add_fusion.4
  594.6 3.6 convolution_add_fusion.1
  598.3 4.8 fusion.1
  603.2 30.5 %all_to_all.46 = bf16[16,256,256]{2,1,0:T(8,128)(2,1)S(1)} all-to-all(bf16[16,256,256]{2,1,0:T(8,128)(2,1)S(1)} %bitcast.88), channel_id=1, replica_groups=mesh['z'=4,'ylo'=2,'core'=2,'x'=4,'yhi'=2] {'z','ylo','core'}, dimensions={0} | all-to-all | bytes 4194304 | tf_op jit(solution)/shard_map/all_to_all | solution.py:14
  634.7 3.1 psum.155
  637.8 5.5 psum.156
  643.4 9.2 %psum.157 = f32[]{:T(128)} all-reduce(f32[]{:T(128)} %psum.156), channel_id=1, replica_groups=mesh['z'=4,'ylo'=2,'core'=2,'x'=4,'yhi'=2] {'z'}, use_global_device_ids=true, to_apply=%region_24.0 | all-reduce | flops 1 | bytes 8 | tf_op jit(solution)/shard_map/psum | solution.py:32
  653.2 8.9 %psum.158 = f32[]{:T(128)} all-reduce(f32[]{:T(128)} %psum.157), channel_id=1, replica_groups=mesh['z'=4,'ylo'=2,'core'=2,'x'=4,'yhi'=2] {'x'}, use_global_device_ids=true, to_apply=%region_25.0 | all-reduce | flops 1 | bytes 8 | tf_op jit(solution)/shard_map/psum | solution.py:32
  662.0 7.0 %psum.159 = f32[]{:T(128)} all-reduce(f32[]{:T(128)} %psum.158), channel_id=1, replica_groups=mesh['z'=4,'ylo'=2,'core'=2,'x'=4,'yhi'=2] {'yhi'}, use_global_device_ids=true, to_apply=%region_26.0 | all-reduce | flops 1 | bytes 8 | tf_op jit(solution)/shard_map/psum | solution.py:32
  (94 shorter events, 35.0 us)
Async XLA Ops:
  8.0 1.9 copy-start.15
  10.0 3.3 copy-start.11
  13.3 7.2 %copy-start.7 = (bf16[128,4096]{1,0:T(8,128)(2,1)S(1)}, bf16[128,4096]{1,0:T(8,128)(2,1)}, u32[]{:S(2)}) copy-start(bf16[128,4096]{1,0:T(8,128)(2,1)} %param.7) | copy-start | bytes 3145732
  13.3 52.7 %all-to-all-start = ((bf16[8,384,512]{1,2,0:T(8,128)(2,1)}), bf16[8,384,512]{1,2,0:T(8,128)(2,1)}, u32[]{:S(2)}, u32[]{:S(2)}) async-start(bf16[8,384,512]{1,2,0:T(8,128)(2,1)} %bitcast.1), calls=%async_computation | async-start | bytes 6291456 | tf_op jit(solution)/shard_map/all_to_all | solution.py:109
  20.5 3.3 copy-start.3
  23.8 2.0 copy-start
  23.8 2.8 copy-start.16
  25.7 2.2 copy-start.5
  66.0 1.6 copy-start.8
  69.8 44.7 %all-to-all-start.1 = ((bf16[16,384,256]{2,1,0:T(8,128)(2,1)}), bf16[16,384,256]{2,1,0:T(8,128)(2,1)}, u32[]{:S(2)}, u32[]{:S(2)}) async-start(bf16[16,384,256]{2,1,0:T(8,128)(2,1)} %maximum_bitcast_fusion), calls=%async_computation.1 | async-start | bytes 6291456 | tf_op jit(solution)/shard_map/all_to_all | solution.py:14
  75.4 41.5 %copy-start.19 = (bf16[128,4096]{1,0:T(8,128)(2,1)S(1)}, bf16[128,4096]{1,0:T(8,128)(2,1)}, u32[]{:S(2)}) copy-start(bf16[128,4096]{1,0:T(8,128)(2,1)} %param.8) | copy-start | bytes 3145732
  75.4 41.5 %copy-start.23 = (f32[384]{0:T(512)S(1)}, f32[384]{0:T(512)}, u32[]{:S(2)}) copy-start(f32[384]{0:T(512)} %constant.43.clone.1) | copy-start | bytes 4612
  75.4 89.7 %all-gather.5.cloned.1.call-start = ((), (), s32[]{:S(2)}) async-start(), calls=%async_computation.9 | async-start | bytes 1114112 | tf_op jit(solution)/shard_map/all_gather | solution.py:126
  120.3 47.7 %all-to-all-start.2 = ((bf16[16,256,256]{1,2,0:T(8,128)(2,1)}), bf16[16,256,256]{1,2,0:T(8,128)(2,1)}, u32[]{:S(2)}, u32[]{:S(2)}) async-start(bf16[16,256,256]{1,2,0:T(8,128)(2,1)} %broadcast_in_dim.8), calls=%async_computation.2 | async-start | bytes 4194304 | tf_op jit(solution)/shard_map/all_to_all | solution.py:20
  168.0 4.0 copy-start.12
  175.6 6.9 %copy-start.18 = (bf16[128,4096]{1,0:T(8,128)(2,1)S(1)}, bf16[128,4096]{1,0:T(8,128)(2,1)}, u32[]{:S(2)}) copy-start(bf16[128,4096]{1,0:T(8,128)(2,1)} %all-gather.5.cloned.1.call-done) | copy-start | bytes 3145732
  175.6 6.9 %copy-start.22 = (f32[128,448]{0,1:T(8,128)S(1)}, f32[128,448]{0,1:T(8,128)}, u32[]{:S(2)}) copy-start(f32[128,448]{0,1:T(8,128)} %get-tuple-element.31) | copy-start | bytes 688132
  175.6 57.3 %all-to-all-start.4 = ((bf16[8,384,512]{2,1,0:T(8,128)(2,1)}), bf16[8,384,512]{2,1,0:T(8,128)(2,1)}, u32[]{:S(2)}, u32[]{:S(2)}) async-start(bf16[8,384,512]{2,1,0:T(8,128)(2,1)} %maximum_bitcast_fusion.1), calls=%async_computation.4 | async-start | bytes 6291456 | tf_op jit(solution)/shard_map/all_to_all | solution.py:139
  181.4 144.0 %all-gather.9.cloned.1.call-start = ((), (), s32[]{:S(2)}) async-start(), calls=%async_computation.11 | async-start | bytes 3096576 | tf_op jit(solution)/shard_map/all_gather | solution.py:142
  182.5 3.4 copy-start.1
  188.6 47.4 %copy-start.20 = (bf16[256,448]{0,1:T(8,128)(2,1)}, bf16[256,448]{0,1:T(8,128)(2,1)S(1)}, u32[]{:S(2)}) copy-start(bf16[256,448]{0,1:T(8,128)(2,1)S(1)} %get-tuple-element.27) | copy-start | bytes 688132
  236.1 98.2 %all-to-all-start.3 = ((bf16[8,384,896]{2,1,0:T(8,128)(2,1)}), bf16[8,384,896]{2,1,0:T(8,128)(2,1)}, u32[]{:S(2)}, u32[]{:S(2)}) async-start(bf16[8,384,896]{2,1,0:T(8,128)(2,1)} %broadcast_in_dim.9), calls=%async_computation.3 | async-start | bytes 11010048 | tf_op jit(solution)/shard_map/all_to_all | solution.py:150
  330.0 13.0 %copy-start.13 = (f32[512,448]{1,0:T(8,128)}, f32[512,448]{1,0:T(8,128)S(1)}, u32[]{:S(2)}) copy-start(f32[512,448]{1,0:T(8,128)S(1)} %convolution_bitcast_fusion) | copy-start | bytes 2752516
  339.3 3.8 copy-start.9
  339.3 3.8 copy-start.14
  343.1 1.7 copy-start.10
  391.8 112.5 %all-to-all-start.5 = ((bf16[8,512,896]{2,1,0:T(8,128)(2,1)}), bf16[8,512,896]{2,1,0:T(8,128)(2,1)}, u32[]{:S(2)}, u32[]{:S(2)}) async-start(bf16[8,512,896]{2,1,0:T(8,128)(2,1)} %broadcast_in_dim.10), calls=%async_computation.5 | async-start | bytes 14680064 | tf_op jit(solution)/shard_map/all_to_all | solution.py:26
  396.6 120.4 %all-gather.7.cloned.1.call-start = ((), (), s32[]{:S(2)}) async-start(), calls=%async_computation.10 | async-start | bytes 4718592 | tf_op jit(solution)/shard_map/all_gather | solution.py:172
  504.2 4.3 copy-start.17
  508.6 4.8 copy-start.2
  554.6 32.5 %all-to-all-start.7 = ((bf16[16,256,256]{1,2,0:T(8,128)(2,1)}), bf16[16,256,256]{1,2,0:T(8,128)(2,1)}, u32[]{:S(2)}, u32[]{:S(2)}) async-start(bf16[16,256,256]{1,2,0:T(8,128)(2,1)} %broadcast_in_dim.11), calls=%async_computation.7 | async-start | bytes 4194304 | tf_op jit(solution)/shard_map/all_to_all | solution.py:20
  587.1 4.0 copy-start.6
  591.1 2.0 copy-start.4
  594.6 3.6 copy-start.21
Sparse Core Ops, SparseCore 0:
  118.8 46.2 all-gather.4
Sparse Core Ops, SparseCore 1:
  184.1 141.3 all-gather.8
  399.5 113.3 all-gather.6

commit v11 on v7

--- a/solution.py
+++ b/solution.py
@@ -28,7 +28,7 @@
 
 
 def psum_all(x):
-    for axis in ("core", "ylo", "z", "x", "yhi"):
+    for axis in (("core", "ylo"), "z", "x", "yhi"):
         x = lax.psum(x, axis)
     return x
 

time: 670 us -> 670 us (level)
    psum x10 -> x8, blocking collectives: 71.9 us -> 68.8 us  [psum_all(): x = lax.psum(x, axis)]
where the time goes in v11:
time: 670 us; the launch traced here: 661 us
  waiting for transfers between devices  328 us (49%)
  blocking collectives  171 us (26%)
  matrix products  66.6 us (10%)
  local copies, waits for them, and re-layouts  32.6 us (5%)
  starting transfers between devices  32.2 us (5%)
  between operations  19.4 us (3%)
  other arithmetic  10.5 us (2%)
    all_to_all x1, waiting for transfers between devices, ag_rows(): lax.all_to_all(jnp.broadcast_to(piece[None], (n, rows, cols)), DP, 0, 0,...  108 us
    all_gather x1, waiting for transfers between devices, local(): lax.all_gather(jnp.concatenate([hidden_tgt, hidden_poi], 0), DP, axis=0,...  84.2 us
    psum x8, blocking collectives, psum_all(): x = lax.psum(x, axis)  68.8 us
    all_to_all x2, blocking collectives, rs_cols(): r = lax.all_to_all(r, FS, 0, 0, tiled=False)  60.9 us
    all_to_all x1, blocking collectives, ag_cols(): lax.all_to_all(jnp.broadcast_to(piece[None], (n, rows, cols)), FS, 0, 0,...  41.8 us
    all_to_all x1, waiting for transfers between devices, local(): lax.all_to_all(error_all.reshape(-1, dp_size, rows_d).transpose(1, 0, 2),...  40.2 us
    all_to_all x1, waiting for transfers between devices, rs_cols(): r = lax.all_to_all(r, FS, 0, 0, tiled=False)  39 us
    all_to_all x1, waiting for transfers between devices, local(): lax.all_to_all(x_loc.reshape(-1, dp_size, model_width // dp_size).transpo...  33.7 us
  transfers between devices with their start and end apart: 8, of which 6 were waited for; matrix products, arithmetic and copies ran while one was open for 7% of the time, Pallas kernels for 0%

profile of v11, /device:TPU:0, one launch (start us, length us, event | category | flops | bytes accessed | tf_op | source)
XLA Modules:
  0.0 661.0 jit_solution(3315063899763865685)
XLA Ops:
  9.2 3.2 copy.24
  12.5 7.2 %all-to-all-start = ((bf16[8,384,512]{1,2,0:T(8,128)(2,1)}), bf16[8,384,512]{1,2,0:T(8,128)(2,1)}, u32[]{:S(2)}, u32[]{:S(2)}) async-start(bf16[8,384,512]{1,2,0:T(8,128)(2,1)} %bitcast.1), calls=%async_computation | async-start | bytes 6291456 | tf_op jit(solution)/shard_map/all_to_all | solution.py:109
  19.6 3.3 fusion.67
  23.0 1.8 multiply_convert_fusion.9
  28.3 1.9 multiply_convert_fusion.3
  31.5 33.7 %all-to-all-done = bf16[8,384,512]{1,2,0:T(8,128)(2,1)} async-done(((bf16[8,384,512]{1,2,0:T(8,128)(2,1)}), bf16[8,384,512]{1,2,0:T(8,128)(2,1)}, u32[]{:S(2)}, u32[]{:S(2)}) %all-to-all-start) | async-done | bytes 3145760 | tf_op jit(solution)/shard_map/all_to_all | solution.py:109
  65.5 1.9 maximum_bitcast_fusion
  67.5 5.5 all-to-all-start.1
  73.0 39.0 %all-to-all-done.1 = bf16[16,384,256]{2,1,0:T(8,128)(2,1)S(1)} async-done(((bf16[16,384,256]{2,1,0:T(8,128)(2,1)}), bf16[16,384,256]{2,1,0:T(8,128)(2,1)S(1)}, u32[]{:S(2)}, u32[]{:S(2)}) %all-to-all-start.1) | async-done | bytes 3145760 | tf_op jit(solution)/shard_map/all_to_all | solution.py:14
  115.5 41.8 %all_to_all.45 = bf16[16,384,256]{1,2,0:T(8,128)(2,1)S(1)} all-to-all(bf16[16,384,256]{1,2,0:T(8,128)(2,1)S(1)} %broadcast_in_dim.8), channel_id=1, replica_groups=mesh['z'=4,'ylo'=2,'core'=2,'x'=4,'yhi'=2] {'z','ylo','core'}, dimensions={0} | all-to-all | bytes 6291456 | tf_op jit(solution)/shard_map/all_to_all | solution.py:20
  157.3 2.9 copy.29
  160.2 4.7 all-to-all-start.4
  166.2 3.3 multiply_convert_fusion.8
  169.7 2.6 copy-done.1
  174.7 40.2 %all-to-all-done.4 = bf16[8,384,512]{2,1,0:T(8,128)(2,1)} async-done(((bf16[8,384,512]{2,1,0:T(8,128)(2,1)}), bf16[8,384,512]{2,1,0:T(8,128)(2,1)}, u32[]{:S(2)}, u32[]{:S(2)}) %all-to-all-start.4) | async-done | bytes 3145760 | tf_op jit(solution)/shard_map/all_to_all | solution.py:133
  214.9 3.2 broadcast_in_dim.9
  218.1 4.7 all-to-all-start.3
  222.8 84.2 %all-gather.6.cloned.1.call-done = bf16[3072,448]{0,1:T(8,128)(2,1)} async-done(((bf16[384,448]{0,1:T(8,128)(2,1)}), bf16[3072,448]{0,1:T(8,128)(2,1)}) %all-gather.6.cloned.1.call-update) | async-done | bytes 2752528 | tf_op jit(solution)/shard_map/all_gather | solution.py:136
  307.0 2.4 copy.47
  309.6 3.0 convolution_bitcast_fusion
  312.6 3.9 fusion.24
  316.5 5.0 fusion.19
  321.5 3.2 fusion.16
  327.7 8.4 %all-reduce.1 = (f32[]{:T(128)}, f32[]{:T(128)}, f32[]{:T(128)}) all-reduce(f32[]{:T(128)} %get-tuple-element.9, f32[]{:T(128)} %get-tuple-element.10, f32[]{:T(128)} %get-tuple-element.8), channel_id=1, replica_groups=mesh['z'=4,'ylo'=2,'core'=2,'x'=4,'yhi'=2] {'core','ylo'}, use_global_device_ids=true, to_apply=%region_12.0 | all-reduce | flops 3 | bytes 24 | tf_op jit(solution)/shard_map/psum | solution.py:32
  336.1 10.2 %all-reduce.2 = (f32[]{:T(128)}, f32[]{:T(128)}, f32[]{:T(128)}) all-reduce(f32[]{:T(128)} %get-tuple-element.14, f32[]{:T(128)} %get-tuple-element.15, f32[]{:T(128)} %get-tuple-element.16), channel_id=1, replica_groups=mesh['z'=4,'ylo'=2,'core'=2,'x'=4,'yhi'=2] {'z'}, use_global_device_ids=true, to_apply=%region_13.0 | all-reduce | flops 3 | bytes 24 | tf_op jit(solution)/shard_map/psum | solution.py:32
  346.3 11.2 %all-reduce = (f32[]{:T(128)}, f32[]{:T(128)}, f32[]{:T(128)}) all-reduce(f32[]{:T(128)} %get-tuple-element.17, f32[]{:T(128)} %get-tuple-element.18, f32[]{:T(128)} %get-tuple-element.19), channel_id=1, replica_groups=mesh['z'=4,'ylo'=2,'core'=2,'x'=4,'yhi'=2] {'x'}, use_global_device_ids=true, to_apply=%region_14.0 | all-reduce | flops 3 | bytes 24 | tf_op jit(solution)/shard_map/psum | solution.py:32
  357.5 7.1 %all-reduce.3 = (f32[]{:T(128)}, f32[]{:T(128)}, f32[]{:T(128)}) all-reduce(f32[]{:T(128)} %get-tuple-element.11, f32[]{:T(128)} %get-tuple-element.12, f32[]{:T(128)} %get-tuple-element.13), channel_id=1, replica_groups=mesh['z'=4,'ylo'=2,'core'=2,'x'=4,'yhi'=2] {'yhi'}, use_global_device_ids=true, to_apply=%region_15.0 | all-reduce | flops 3 | bytes 24 | tf_op jit(solution)/shard_map/psum | solution.py:32
  366.6 2.5 add_convert_fusion
  370.3 3.9 broadcast_in_dim.10
  374.2 5.0 all-to-all-start.5
  379.5 1.9 slice.75
  381.4 107.8 %all-to-all-done.5 = bf16[8,512,896]{2,1,0:T(8,128)(2,1)} async-done(((bf16[8,512,896]{2,1,0:T(8,128)(2,1)}), bf16[8,512,896]{2,1,0:T(8,128)(2,1)}, u32[]{:S(2)}, u32[]{:S(2)}) %all-to-all-start.5) | async-done | bytes 7340064 | tf_op jit(solution)/shard_map/all_to_all | solution.py:26
  489.1 3.7 fusion.29
  492.9 4.8 fusion.32
  497.7 3.5 fusion.48
  501.3 4.8 fusion
  506.3 30.3 %all_to_all.46 = bf16[16,256,256]{2,1,0:T(8,128)(2,1)S(1)} all-to-all(bf16[16,256,256]{2,1,0:T(8,128)(2,1)S(1)} %bitcast.89), channel_id=1, replica_groups=mesh['z'=4,'ylo'=2,'core'=2,'x'=4,'yhi'=2] {'z','ylo','core'}, dimensions={0} | all-to-all | bytes 4194304 | tf_op jit(solution)/shard_map/all_to_all | solution.py:14
  538.5 4.7 all-to-all-start.7
  543.2 4.5 fusion.70
  547.7 23.3 %all-to-all-done.7 = bf16[16,256,256]{1,2,0:T(8,128)(2,1)} async-done(((bf16[16,256,256]{1,2,0:T(8,128)(2,1)}), bf16[16,256,256]{1,2,0:T(8,128)(2,1)}, u32[]{:S(2)}, u32[]{:S(2)}) %all-to-all-start.7) | async-done | bytes 2097184 | tf_op jit(solution)/shard_map/all_to_all | solution.py:20
  571.0 4.0 convolution_add_fusion.4
  578.5 3.6 convolution_add_fusion.1
  582.2 4.8 fusion.1
  587.2 30.5 %all_to_all.47 = bf16[16,256,256]{2,1,0:T(8,128)(2,1)S(1)} all-to-all(bf16[16,256,256]{2,1,0:T(8,128)(2,1)S(1)} %bitcast.90), channel_id=1, replica_groups=mesh['z'=4,'ylo'=2,'core'=2,'x'=4,'yhi'=2] {'z','ylo','core'}, dimensions={0} | all-to-all | bytes 4194304 | tf_op jit(solution)/shard_map/all_to_all | solution.py:14
  618.6 7.4 %psum.124 = f32[]{:T(128)} all-reduce(f32[]{:T(128)} %multiply_reduce_fusion.3), channel_id=1, replica_groups=mesh['z'=4,'ylo'=2,'core'=2,'x'=4,'yhi'=2] {'core','ylo'}, use_global_device_ids=true, to_apply=%region_19.0 | all-reduce | flops 1 | bytes 8 | tf_op jit(solution)/shard_map/psum | solution.py:32
  626.0 8.7 %psum.125 = f32[]{:T(128)} all-reduce(f32[]{:T(128)} %psum.124), channel_id=1, replica_groups=mesh['z'=4,'ylo'=2,'core'=2,'x'=4,'yhi'=2] {'z'}, use_global_device_ids=true, to_apply=%region_20.0 | all-reduce | flops 1 | bytes 8 | tf_op jit(solution)/shard_map/psum | solution.py:32
  635.3 8.7 %psum.126 = f32[]{:T(128)} all-reduce(f32[]{:T(128)} %psum.125), channel_id=1, replica_groups=mesh['z'=4,'ylo'=2,'core'=2,'x'=4,'yhi'=2] {'x'}, use_global_device_ids=true, to_apply=%region_21.0 | all-reduce | flops 1 | bytes 8 | tf_op jit(solution)/shard_map/psum | solution.py:32
  644.1 7.0 %psum.127 = f32[]{:T(128)} all-reduce(f32[]{:T(128)} %psum.126), channel_id=1, replica_groups=mesh['z'=4,'ylo'=2,'core'=2,'x'=4,'yhi'=2] {'yhi'}, use_global_device_ids=true, to_apply=%region_22.0 | all-reduce | flops 1 | bytes 8 | tf_op jit(solution)/shard_map/psum | solution.py:32
  (99 shorter events, 26.5 us)
Async XLA Ops:
  7.2 1.9 copy-start.18
  9.2 3.2 copy-start.14
  12.4 7.2 %copy-start.10 = (bf16[128,4096]{1,0:T(8,128)(2,1)S(1)}, bf16[128,4096]{1,0:T(8,128)(2,1)}, u32[]{:S(2)}) copy-start(bf16[128,4096]{1,0:T(8,128)(2,1)} %param.7) | copy-start | bytes 3145732
  12.5 52.7 %all-to-all-start = ((bf16[8,384,512]{1,2,0:T(8,128)(2,1)}), bf16[8,384,512]{1,2,0:T(8,128)(2,1)}, u32[]{:S(2)}, u32[]{:S(2)}) async-start(bf16[8,384,512]{1,2,0:T(8,128)(2,1)} %bitcast.1), calls=%async_computation | async-start | bytes 6291456 | tf_op jit(solution)/shard_map/all_to_all | solution.py:109
  19.6 3.3 copy-start.3
  23.0 2.9 copy-start.27
  23.0 2.2 copy-start
  23.0 2.9 copy-start.19
  24.8 2.3 copy-start.5
  28.3 2.0 copy-start.7
  30.2 134.9 %copy-start.24 = (bf16[256,448]{0,1:T(8,128)(2,1)}, bf16[256,448]{0,1:T(8,128)(2,1)S(1)}, u32[]{:S(2)}) copy-start(bf16[256,448]{0,1:T(8,128)(2,1)S(1)} %get-tuple-element.29) | copy-start | bytes 688132
  67.5 44.6 %all-to-all-start.1 = ((bf16[16,384,256]{2,1,0:T(8,128)(2,1)}), bf16[16,384,256]{2,1,0:T(8,128)(2,1)S(1)}, u32[]{:S(2)}, u32[]{:S(2)}) async-start(bf16[16,384,256]{2,1,0:T(8,128)(2,1)} %maximum_bitcast_fusion), calls=%async_computation.1 | async-start | bytes 6291456 | tf_op jit(solution)/shard_map/all_to_all | solution.py:14
  73.0 39.5 %copy-start.30 = (f32[384]{0:T(512)S(1)}, f32[384]{0:T(512)}, u32[]{:S(2)}) copy-start(f32[384]{0:T(512)} %constant.43.clone.1) | copy-start | bytes 4612
  112.0 1.6 copy-start.23
  112.0 1.9 copy-start.26
  160.2 54.7 %all-to-all-start.4 = ((bf16[8,384,512]{2,1,0:T(8,128)(2,1)}), bf16[8,384,512]{2,1,0:T(8,128)(2,1)}, u32[]{:S(2)}, u32[]{:S(2)}) async-start(bf16[8,384,512]{2,1,0:T(8,128)(2,1)} %bitcast.84), calls=%async_computation.4 | async-start | bytes 6291456 | tf_op jit(solution)/shard_map/all_to_all | solution.py:133
  164.9 142.1 %all-gather.6.cloned.1.call-start = ((), (), s32[]{:S(2)}) async-start(), calls=%async_computation.10 | async-start | bytes 3096576 | tf_op jit(solution)/shard_map/all_gather | solution.py:136
  166.2 3.6 copy-start.11
  169.5 2.8 copy-start.1
  169.5 2.9 copy-start.8
  169.7 3.9 copy-start.22
  173.6 0.7 copy-start.28
  218.1 98.4 %all-to-all-start.3 = ((bf16[8,384,896]{2,1,0:T(8,128)(2,1)}), bf16[8,384,896]{2,1,0:T(8,128)(2,1)}, u32[]{:S(2)}, u32[]{:S(2)}) async-start(bf16[8,384,896]{2,1,0:T(8,128)(2,1)} %broadcast_in_dim.9), calls=%async_computation.3 | async-start | bytes 11010048 | tf_op jit(solution)/shard_map/all_to_all | solution.py:144
  321.5 4.5 copy-start.16
  321.5 4.5 copy-start.17
  324.7 1.3 copy-start.13
  369.1 1.1 copy-start.15
  374.2 114.9 %copy-start.20 = (bf16[256,4096]{1,0:T(8,128)(2,1)S(1)}, bf16[256,4096]{1,0:T(8,128)(2,1)}, u32[]{:S(2)}) copy-start(bf16[256,4096]{1,0:T(8,128)(2,1)} %param.9) | copy-start | bytes 6291460
  374.2 114.9 %all-to-all-start.5 = ((bf16[8,512,896]{2,1,0:T(8,128)(2,1)}), bf16[8,512,896]{2,1,0:T(8,128)(2,1)}, u32[]{:S(2)}, u32[]{:S(2)}) async-start(bf16[8,512,896]{2,1,0:T(8,128)(2,1)} %broadcast_in_dim.10), calls=%async_computation.5 | async-start | bytes 14680064 | tf_op jit(solution)/shard_map/all_to_all | solution.py:26
  379.2 122.1 %all-gather.4.cloned.1.call-start = ((), (), s32[]{:S(2)}) async-start(), calls=%async_computation.9 | async-start | bytes 4718592 | tf_op jit(solution)/shard_map/all_gather | solution.py:166
  489.1 3.7 copy-start.21
  492.8 4.8 copy-start.2
  492.8 4.8 copy-start.9
  492.8 4.8 copy-start.12
  497.7 3.6 copy-start.25
  538.5 32.5 %all-to-all-start.7 = ((bf16[16,256,256]{1,2,0:T(8,128)(2,1)}), bf16[16,256,256]{1,2,0:T(8,128)(2,1)}, u32[]{:S(2)}, u32[]{:S(2)}) async-start(bf16[16,256,256]{1,2,0:T(8,128)(2,1)} %broadcast_in_dim.11), calls=%async_computation.7 | async-start | bytes 4194304 | tf_op jit(solution)/shard_map/all_to_all | solution.py:20
  571.0 4.0 copy-start.6
  575.0 2.0 copy-start.4
  578.5 3.6 copy-start.29
Sparse Core Ops, SparseCore 0:
  167.9 139.0 all-gather.5
  382.3 114.4 all-gather.3
